TPU v7x, 256 devices: a whole 4x4x8 slice. The times are simulated.
256 devices in a mesh: line: 8 (over x, core), grp: 32 (over y, z).
Axes of the slice: x: 4, y: 4, z: 8, core: 2. Of those that a mesh axis runs over, the one named last changes fastest.
Arguments:
- shot_traces: float32 [512, 192, 4096], P(('line', 'grp')), may hold values from -6 to 6
- aperture: int32 [256, 3, 32, 16], replicated, may hold values from -1 to 95, as said below
- taper_index: int32 [256, 3, 32, 16], P(('line', 'grp')), may hold values from 0 to 7
- taper_table: float32 [8, 2], replicated, may hold values from 0.2 to 1
Outputs:
- multiples: float32 [512, 192, 2, 128], P(('line', 'grp'))
Inputs may be any that keep to these rules, and one draw needn't show every extreme that they name: `aperture`: each entry is -1 for an empty slot, or r = q * 32 + h with q - s between -1 and 1, s being the entry's second index.
All inputs are finite; a program needn't handle non-finite values.
Results may differ from a plain program's by a relative error of at most 0.0003.
Values sent between devices are 32-bit elements; how exact they have to be, the bound alone decides.
No kernel may reach another device: no remote copies, remote signals or barrier semaphores. Data moves between devices by JAX's collectives and lax.ppermute only.
A program may use at most 128 MiB of HBM per device.

v0:
```python
import math

import jax
import jax.numpy as jnp
import numpy as np
from jax import lax
from jax.sharding import Mesh, NamedSharding
from jax.sharding import PartitionSpec as P

NF = 128
BP = 2
CAP = 16
RADIX = 64

HIGH = lax.Precision.HIGH


def dft_matrix(samples):
    inner = samples // RADIX
    major = jnp.arange(RADIX, dtype=jnp.int32)
    minor = jnp.arange(inner, dtype=jnp.int32)
    bins = jnp.arange(NF, dtype=jnp.int32)
    step = 2.0 * math.pi / samples
    angle_a = ((major[:, None] * inner * bins[None, :]) % samples).astype(jnp.float32) * step
    angle_n = ((minor[:, None] * bins[None, :]) % samples).astype(jnp.float32) * step
    a_re, a_im = jnp.cos(angle_a), -jnp.sin(angle_a)
    n_re, n_im = jnp.cos(angle_n), -jnp.sin(angle_n)
    scale = 1.0 / math.sqrt(samples)
    c_re = (a_re[:, None, :] * n_re[None, :, :] - a_im[:, None, :] * n_im[None, :, :]) * scale
    c_im = (a_re[:, None, :] * n_im[None, :, :] + a_im[:, None, :] * n_re[None, :, :]) * scale
    return jnp.concatenate([c_re, c_im], axis=-1).reshape(samples, 2 * NF)


def spectrum(traces, table):
    shots, recv, samples = traces.shape
    out = jnp.dot(traces.reshape(shots * recv, samples), table, precision=HIGH)
    return out.reshape(shots, recv // BP, BP, 2, NF)


def combine(cols, weight, block):
    scaled = block[None] * weight[:, :, :, None, None, :, None]
    col_re = cols[:, :, :, :, None, 0, None, :]
    col_im = cols[:, :, :, :, None, 1, None, :]
    row_re = scaled[:, None, :, :, :, 0]
    row_im = scaled[:, None, :, :, :, 1]
    prod_re = -jnp.sum(col_re * row_re - col_im * row_im, axis=(2, 3))
    prod_im = -jnp.sum(col_re * row_im + col_im * row_re, axis=(2, 3))
    return jnp.stack([prod_re, prod_im], axis=3)


def body(shot_traces, aperture, taper_index, taper_table):
    line_count = lax.axis_size("line")
    rows = lax.axis_size("gy")
    cols = lax.axis_size("gz")
    my_line = lax.axis_index("line")
    my_row = lax.axis_index("gy")
    my_col = lax.axis_index("gz")
    shots, recv, samples = shot_traces.shape
    sides = 3
    width = recv // (BP * sides)
    blocks = sides * width
    up = [(i, (i + 1) % line_count) for i in range(line_count)]
    down = [((i + 1) % line_count, i) for i in range(line_count)]
    right = [(i, (i + 1) % cols) for i in range(cols)]
    left = [((i + 1) % cols, i) for i in range(cols)]
    spans = [(0, 2 * width), (0, blocks), (width, blocks)]

    taper_rows = taper_table.shape[0]
    pick = taper_index.reshape(sides, rows, cols, CAP)[..., None] == jnp.arange(taper_rows, dtype=jnp.int32)
    src_weight = jnp.sum(jnp.where(pick[..., None], taper_table, 0.0), axis=-2)
    full_table = aperture.reshape(line_count, rows, cols, sides, rows, cols, CAP)
    slot_table = lax.dynamic_index_in_dim(
        lax.dynamic_index_in_dim(
            lax.dynamic_index_in_dim(full_table, my_line, 0, False), my_row, 0, False
        ),
        my_col,
        3,
        False,
    )

    table = dft_matrix(samples)
    own = spectrum(shot_traces, table)

    stacked = own.reshape(shots, sides, rows, cols, BP, 2, NF)
    stacked = jnp.transpose(stacked, (1, 0, 2, 3, 4, 5, 6))
    spread = lax.all_to_all(stacked, "gy", split_axis=2, concat_axis=2, tiled=True)
    spread = jnp.transpose(spread, (0, 2, 1, 3, 4, 5, 6))
    side_cols = [
        lax.ppermute(spread[2], "line", up),
        spread[1],
        lax.ppermute(spread[0], "line", down),
    ]

    lanes = jnp.transpose(own, (0, 2, 3, 1, 4))
    spec_size = lanes.size
    payload = jnp.concatenate([lanes.reshape(-1), src_weight.reshape(-1)])
    carried = [payload]
    offsets = [0]
    forward = payload
    backward = payload
    for step in range(1, cols // 2 + 1):
        forward = lax.ppermute(forward, "gz", right)
        carried.append(forward)
        offsets.append(-step)
        if 2 * step < cols:
            backward = lax.ppermute(backward, "gz", left)
            carried.append(backward)
            offsets.append(step)
    sources = (my_col + jnp.asarray(offsets, dtype=jnp.int32)) % cols
    ring = jnp.stack(carried)
    gathered = ring[:, :spec_size].reshape((len(carried),) + lanes.shape)
    weights = lax.dynamic_index_in_dim(
        ring[:, spec_size:].reshape((len(carried),) + src_weight.shape), my_col, 3, False
    )
    slots = jnp.take(slot_table, sources, axis=0)
    hit = slots[..., None] == jnp.arange(blocks, dtype=jnp.int32)
    dense = jnp.sum(jnp.where(hit[..., None], weights[:, :, :, :, None, :], 0.0), axis=3)
    dense = jnp.transpose(dense, (1, 2, 0, 4, 3))

    total = []
    for s in range(sides):
        lo, hi = spans[s]
        cols_s = jnp.take(side_cols[s], sources, axis=2)
        total.append(combine(cols_s, dense[s, :, :, :, lo:hi], gathered[:, :, :, :, lo:hi]))
    merged = jnp.concatenate(total, axis=4)
    mine = lax.psum_scatter(merged, "gy", scatter_dimension=0, tiled=False)
    first, middle = 2 * width, 2 * width + blocks
    from_up = lax.ppermute(mine[:, :, :, :first], "line", down)
    from_down = lax.ppermute(mine[:, :, :, middle:], "line", up)
    result = mine[:, :, :, first:middle]
    result = result.at[:, :, :, width:].add(from_up)
    result = result.at[:, :, :, : 2 * width].add(from_down)
    result = jnp.transpose(result, (0, 3, 1, 2, 4))
    return result.reshape(shots, recv, 2, NF)


def grid_shape(mesh):
    row = mesh.devices[0]
    try:
        ys = sorted({d.coords[1] for d in row})
        zs = sorted({d.coords[2] for d in row})
        if len(ys) * len(zs) == len(row):
            return len(ys), len(zs)
    except Exception:
        pass
    return 4, len(row) // 4


def solution(mesh):
    rows, cols = grid_shape(mesh)
    lines = mesh.devices.shape[0]
    fine = Mesh(np.asarray(mesh.devices).reshape(lines, rows, cols), ("line", "gy", "gz"))
    split = ("line", "gy", "gz")
    mapped = jax.shard_map(
        body,
        mesh=fine,
        in_specs=(P(split, None, None), P(), P(split, None, None, None), P()),
        out_specs=P(split, None, None, None),
        check_vma=False,
    )
    out_sharding = NamedSharding(mesh, P(("line", "grp"), None, None, None))
    return jax.jit(mapped, out_shardings=out_sharding)
```

profile of v0, /device:TPU:32, one launch (start us, length us, event | category | flops | bytes accessed | tf_op | source)
XLA Modules:
  0.0 200.7 jit_solution(900658413346902837)
XLA Ops:
  7.8 1.1 select_reduce_fusion.1
  10.6 9.0 %fusion.4 = f32[384,256]{0,1:T(8,128)S(1)} fusion(f32[384,4096]{1,0:T(8,128)} %bitcast.98, f32[4096,128]{1,0:T(8,128)S(1)} %bitcast.97, f32[4096,128]{1,0:T(8,128)S(1)} %bitcast.96), kind=kOutput, calls=%fused_computation.28 | convolution fusion | flops 2416967680 | bytes 10878976 | tf_op jit(solution)/jit(body)/shard_map/dot_general | solution.py:36
  20.1 1.9 collective-permute-start.2
  23.3 4.5 %all-to-all-start = ((f32[3,2,4,8,2,2,128]{6,5,4,3,1,0,2:T(2,128)}), f32[3,2,4,8,2,2,128]{6,5,4,3,1,0,2:T(2,128)S(1)}, u32[]{:S(2)}, u32[]{:S(2)}) async-start(f32[3,2,4,8,2,2,128]{6,5,4,3,1,0,2:T(2,128)} %copy.93), calls=%async_computation | async-start | bytes 786432 | tf_op jit(solution)/jit(body)/shard_map/all_to_all | solution.py:86
  27.8 10.5 %copy.101 = s32[256,3,32,16]{3,2,1,0:T(8,128)} copy(s32[256,3,32,16]{0,3,2,1:T(8,128)S(1)} %copy-done.7) | data formatting | bytes 3145728 | tf_op args[1]
  40.3 2.0 collective-permute-start.3
  42.3 2.9 %collective-permute-start.8 = (f32[4,2,8,2,2,128]{5,0,4,3,2,1:T(4,128)S(1)}, f32[4,2,8,2,2,128]{5,0,4,3,2,1:T(4,128)S(1)}, u32[]{:S(2)}, u32[]{:S(2)}) collective-permute-start(f32[4,2,8,2,2,128]{5,0,4,3,2,1:T(4,128)S(1)} %get-tuple-element.49), channel_id=1, source_target_pairs={{32,0},{64,32},{96,64},{128,96},{160,128},{192,160},{224,192},{0,2... | collective-permute-start | bytes 393224 | tf_op jit(solution)/jit(body)/shard_map/ppermute | solution.py:91
  46.2 2.1 %collective-permute-start.4 = (f32[101376]{0:T(1024)S(1)}, f32[101376]{0:T(1024)S(1)}, u32[]{:S(2)}, u32[]{:S(2)}) collective-permute-start(f32[101376]{0:T(1024)S(1)} %collective-permute-done.2), channel_id=1, source_target_pairs={{1,0},{2,1},{3,2},{4,3},{5,4},{6,5},{7,6},{0,7},{9,8},{10,9},{11,1... | collective-permute-start | bytes 1216520 | tf_op jit(solution)/jit(body)/shard_map/ppermute | solution.py:106
  49.6 3.7 %collective-permute-done.3 = f32[101376]{0:T(1024)S(1)} collective-permute-done((f32[101376]{0:T(1024)}, f32[101376]{0:T(1024)S(1)}, u32[]{:S(2)}, u32[]{:S(2)}) %collective-permute-start.3) | collective-permute-done | bytes 405536 | tf_op jit(solution)/jit(body)/shard_map/ppermute | solution.py:102
  55.3 2.3 %collective-permute-done.4 = f32[101376]{0:T(1024)S(1)} collective-permute-done((f32[101376]{0:T(1024)S(1)}, f32[101376]{0:T(1024)S(1)}, u32[]{:S(2)}, u32[]{:S(2)}) %collective-permute-start.4) | collective-permute-done | bytes 405536 | tf_op jit(solution)/jit(body)/shard_map/ppermute | solution.py:106
  57.6 1.4 collective-permute-start.6
  59.0 5.2 %collective-permute-done.5 = f32[101376]{0:T(1024)S(1)} collective-permute-done((f32[101376]{0:T(1024)S(1)}, f32[101376]{0:T(1024)S(1)}, u32[]{:S(2)}, u32[]{:S(2)}) %collective-permute-start.5) | collective-permute-done | bytes 405536 | tf_op jit(solution)/jit(body)/shard_map/ppermute | solution.py:102
  67.1 7.2 %collective-permute-done.7 = f32[101376]{0:T(1024)S(1)} collective-permute-done((f32[101376]{0:T(1024)S(1)}, f32[101376]{0:T(1024)S(1)}, u32[]{:S(2)}, u32[]{:S(2)}) %collective-permute-start.7) | collective-permute-done | bytes 405536 | tf_op jit(solution)/jit(body)/shard_map/ppermute | solution.py:102
  75.1 10.9 %stack.50 = f32[8,101376]{1,0:T(8,128)S(1)} concatenate(f32[1,101376]{1,0:T(1,128)} %bitcast.101, f32[1,101376]{1,0:T(1,128)} %bitcast.13, f32[1,101376]{1,0:T(1,128)} %bitcast.110, f32[1,101376]{1,0:T(1,128)} %bitcast.111, f32[1,101376]{1,0:T(1,128)} %bitcast.112, f32[1,101376]{1,0:T(1,128)} %bitcast.113, f32[1,101376]{1,0:T(1,128)} %bitcast.114, f32[1,101376]{1,0:T(1,128)} %bitcast.115), dimensions={0} | concatenate | bytes 6488064 | tf_op jit(solution)/jit(body)/shard_map/stack | solution.py:110
  86.0 1.7 copy-done
  87.7 2.1 %slice_bitcast_fusion.6 = f32[1,8,768,128]{3,1,2,0:T(8,128)S(1)} fusion(f32[8,101376]{1,0:T(8,128)} %copy-done), kind=kLoop, calls=%fused_computation.24 | loop fusion | bytes 6291456
  89.8 1.7 copy.102
  93.8 2.2 %copy.108 = f32[8,2,2,2,96,128]{5,4,2,1,0,3:T(8,128)} copy(f32[8,2,2,2,96,128]{5,0,4,3,2,1:T(8,128)S(1)} %bitcast.93) | data formatting | bytes 6291456 | tf_op jit(solution)/jit(body)/shard_map/reshape | solution.py:111
  97.8 1.2 broadcast_multiply_fusion.2
  99.0 1.7 slice_bitcast_fusion.5
  100.7 2.7 %subtract_reduce_fusion.2 = (f32[4,2,2,64,128]{4,3,2,1,0:T(8,128)S(1)}, f32[4,2,2,64,128]{4,3,2,1,0:T(8,128)S(1)}) fusion(f32[4,8,2,2,64,128]{5,4,3,2,1,0:T(8,128)S(1)} %get-tuple-element.41, f32[4,2,8,2,128]{4,3,2,1,0:T(2,128)S(1)} %copy-done.18, f32[4,8,2,2,64,128]{5,4,3,2,1,0:T(8,128)S(1)} %get-tuple-element.40, f32[4,2,8,2,128]{4,3,2,1,0:T(2,128)S(1)} %copy-done.17), kind=kLoop, calls=%fused_computation.9 | loop fusion | flops 16515072 | bytes 9568256 | tf_op jit(solution)/jit(body)/shard_map/reduce_sum | solution.py:46
  105.1 1.3 broadcast_multiply_fusion.1
  106.4 1.7 slice_bitcast_fusion.3
  108.1 2.7 %subtract_reduce_fusion.1 = (f32[4,2,2,64,128]{4,3,2,1,0:T(8,128)S(1)}, f32[4,2,2,64,128]{4,3,2,1,0:T(8,128)S(1)}) fusion(f32[4,8,2,2,64,128]{5,4,3,2,1,0:T(8,128)S(1)} %get-tuple-element.43, f32[4,2,8,2,128]{4,3,2,1,0:T(2,128)S(1)} %copy-done.20, f32[4,8,2,2,64,128]{5,4,3,2,1,0:T(8,128)S(1)} %get-tuple-element.42, f32[4,2,8,2,128]{4,3,2,1,0:T(2,128)S(1)} %copy-done.19), kind=kLoop, calls=%fused_computation.7 | loop fusion | flops 16515072 | bytes 9568256 | tf_op jit(solution)/jit(body)/shard_map/reduce_sum | solution.py:46
  112.5 6.2 %broadcast_multiply_fusion = f32[4,8,2,2,2,96,128]{6,5,3,2,1,0,4:T(8,128)} fusion(f32[8,2,2,2,96,128]{5,4,2,1,0,3:T(8,128)S(1)} %copy-done.1, f32[3,4,8,2,96]{4,3,1,0,2:T(2,128)S(1)} %bitcast.117), kind=kLoop, calls=%fused_computation.12 | loop fusion | flops 3145728 | bytes 15761408 | tf_op jit(solution)/jit(body)/shard_map/mul | solution.py:41
  118.8 9.0 %slice_bitcast_fusion.1 = (f32[4,8,2,2,96,128]{5,4,3,2,1,0:T(8,128)S(1)}, f32[4,8,2,2,96,128]{5,4,3,2,1,0:T(8,128)}) fusion(f32[4,8,2,2,2,96,128]{6,5,3,2,1,0,4:T(8,128)} %broadcast_multiply_fusion), kind=kLoop, calls=%fused_computation.11 | loop fusion | bytes 25165824 | tf_op jit(solution)/jit(body)/shard_map/mul | solution.py:46
  127.8 6.2 %subtract_reduce_fusion = (f32[4,2,2,96,128]{4,3,2,1,0:T(8,128)S(1)}, f32[4,2,2,96,128]{4,3,2,1,0:T(8,128)S(1)}) fusion(f32[4,8,2,2,96,128]{5,4,3,2,1,0:T(8,128)} %get-tuple-element.39, f32[4,2,8,2,128]{4,3,2,1,0:T(2,128)S(1)} %copy-done.16, f32[4,8,2,2,96,128]{5,4,3,2,1,0:T(8,128)S(1)} %get-tuple-element.38, f32[4,2,8,2,128]{4,3,2,1,0:T(2,128)S(1)} %copy-done.15), kind=kLoop, calls=%fused_computation.5 | loop fusion | flops 24772608 | bytes 14286848 | tf_op jit(solution)/jit(body)/shard_map/reduce_sum | solution.py:46
  134.5 2.1 %copy.115 = f32[4,2,2,2,224,128]{5,4,3,2,1,0:T(8,128)} copy(f32[4,2,2,2,224,128]{5,4,2,1,0,3:T(8,128)S(1)} %maximum_maximum_fusion) | data formatting | bytes 7340032 | tf_op jit(solution)/jit(body)/shard_map/concatenate | solution.py:125
  136.7 45.6 %reduce-scatter.2.cloned.1.call-done = f32[1,2,2,2,224,128]{5,4,3,2,1,0:T(8,128)} async-done(((f32[4,2,2,2,224,128]{5,4,3,2,1,0:T(8,128)}), f32[1,2,2,2,224,128]{5,4,3,2,1,0:T(8,128)}) %reduce-scatter.2.cloned.1.call-update) | async-done | bytes 917520 | tf_op jit(solution)/jit(body)/shard_map/reduce_scatter | solution.py:126
  183.3 2.1 %collective-permute-start.9 = (f32[2,2,2,64,128]{4,3,2,1,0:T(8,128)S(1)}, f32[2,2,2,64,128]{4,3,2,1,0:T(8,128)S(1)}, u32[]{:S(2)}, u32[]{:S(2)}) collective-permute-start(f32[2,2,2,64,128]{4,3,2,1,0:T(8,128)S(1)} %get-tuple-element.47), channel_id=1, source_target_pairs={{32,0},{64,32},{96,64},{128,96},{160,128},{192,160},{224,192},{0,2... | collective-permute-start | bytes 786440 | tf_op jit(solution)/jit(body)/shard_map/ppermute | solution.py:128
  186.4 2.9 %collective-permute-done.9 = f32[2,2,2,64,128]{4,3,2,1,0:T(8,128)S(1)} collective-permute-done((f32[2,2,2,64,128]{4,3,2,1,0:T(8,128)S(1)}, f32[2,2,2,64,128]{4,3,2,1,0:T(8,128)S(1)}, u32[]{:S(2)}, u32[]{:S(2)}) %collective-permute-start.9) | collective-permute-done | bytes 262176 | tf_op jit(solution)/jit(body)/shard_map/ppermute | solution.py:128
  190.3 2.1 %collective-permute-done.10 = f32[2,2,2,64,128]{4,3,2,1,0:T(8,128)S(1)} collective-permute-done((f32[2,2,2,64,128]{4,3,2,1,0:T(8,128)S(1)}, f32[2,2,2,64,128]{4,3,2,1,0:T(8,128)S(1)}, u32[]{:S(2)}, u32[]{:S(2)}) %collective-permute-start.10) | collective-permute-done | bytes 262176 | tf_op jit(solution)/jit(body)/shard_map/ppermute | solution.py:129
  (112 shorter events, 26.7 us)
Async XLA Ops:
  19.6 8.2 %copy-start.21 = (s32[8]{0:T(128)S(1)}, s32[8]{0:T(128)}, u32[]{:S(2)}) copy-start(s32[8]{0:T(128)} %constant.220.clone) | copy-start | bytes 100
  19.6 8.2 %copy-start.7 = (s32[256,3,32,16]{0,3,2,1:T(8,128)S(1)}, s32[256,3,32,16]{0,3,2,1:T(8,128)}, u32[]{:S(2)}) copy-start(s32[256,3,32,16]{0,3,2,1:T(8,128)} %param.12) | copy-start | bytes 4718596
  20.1 18.2 %copy-start.6 = (f32[101376]{0:T(1024)}, f32[101376]{0:T(1024)S(1)}, u32[]{:S(2)}) copy-start(f32[101376]{0:T(1024)S(1)} %pad_maximum_fusion) | copy-start | bytes 1216516
  20.1 26.1 %collective-permute-start.2 = (f32[101376]{0:T(1024)S(1)}, f32[101376]{0:T(1024)S(1)}, u32[]{:S(2)}, u32[]{:S(2)}) collective-permute-start(f32[101376]{0:T(1024)S(1)} %pad_maximum_fusion), channel_id=1, source_target_pairs={{1,0},{2,1},{3,2},{4,3},{5,4},{6,5},{7,6},{0,7},{9,8},{10,9},{11,1... | collective-permute-start | bytes 1216520 | tf_op jit(solution)/jit(body)/shard_map/ppermute | solution.py:106
  22.0 18.3 %collective-permute-start.1 = (f32[101376]{0:T(1024)S(1)}, f32[101376]{0:T(1024)}, u32[]{:S(2)}, u32[]{:S(2)}) collective-permute-start(f32[101376]{0:T(1024)S(1)} %pad_maximum_fusion), channel_id=1, source_target_pairs={{0,1},{1,2},{2,3},{3,4},{4,5},{5,6},{6,7},{7,0},{8,9},{9,10},{10,1... | collective-permute-start | bytes 1216520 | tf_op jit(solution)/jit(body)/shard_map/ppermute | solution.py:102
  23.3 16.7 %all-to-all-start = ((f32[3,2,4,8,2,2,128]{6,5,4,3,1,0,2:T(2,128)}), f32[3,2,4,8,2,2,128]{6,5,4,3,1,0,2:T(2,128)S(1)}, u32[]{:S(2)}, u32[]{:S(2)}) async-start(f32[3,2,4,8,2,2,128]{6,5,4,3,1,0,2:T(2,128)} %copy.93), calls=%async_computation | async-start | bytes 786432 | tf_op jit(solution)/jit(body)/shard_map/all_to_all | solution.py:86
  27.7 154.5 %reduce-scatter.2.cloned.1.call-start = ((), (), s32[]{:S(2)}) async-start(), calls=%async_computation.2 | async-start | bytes 4587520 | tf_op jit(solution)/jit(body)/shard_map/reduce_scatter | solution.py:126
  40.3 13.0 %collective-permute-start.3 = (f32[101376]{0:T(1024)}, f32[101376]{0:T(1024)S(1)}, u32[]{:S(2)}, u32[]{:S(2)}) collective-permute-start(f32[101376]{0:T(1024)} %collective-permute-done.1), channel_id=1, source_target_pairs={{0,1},{1,2},{2,3},{3,4},{4,5},{5,6},{6,7},{7,0},{8,9},{9,10},{10,1... | collective-permute-start | bytes 1216520 | tf_op jit(solution)/jit(body)/shard_map/ppermute | solution.py:102
  42.3 6.0 %collective-permute-start = (f32[4,2,8,2,2,128]{5,0,4,3,2,1:T(4,128)S(1)}, f32[4,2,8,2,2,128]{5,0,4,3,2,1:T(4,128)S(1)}, u32[]{:S(2)}, u32[]{:S(2)}) collective-permute-start(f32[4,2,8,2,2,128]{5,0,4,3,2,1:T(4,128)S(1)} %get-tuple-element.48), channel_id=1, source_target_pairs={{0,32},{32,64},{64,96},{96,128},{128,160},{160,192},{192,224},{224... | collective-permute-start | bytes 393224 | tf_op jit(solution)/jit(body)/shard_map/ppermute | solution.py:89
  42.3 6.6 %collective-permute-start.8 = (f32[4,2,8,2,2,128]{5,0,4,3,2,1:T(4,128)S(1)}, f32[4,2,8,2,2,128]{5,0,4,3,2,1:T(4,128)S(1)}, u32[]{:S(2)}, u32[]{:S(2)}) collective-permute-start(f32[4,2,8,2,2,128]{5,0,4,3,2,1:T(4,128)S(1)} %get-tuple-element.49), channel_id=1, source_target_pairs={{32,0},{64,32},{96,64},{128,96},{160,128},{192,160},{224,192},{0,2... | collective-permute-start | bytes 393224 | tf_op jit(solution)/jit(body)/shard_map/ppermute | solution.py:91
  46.2 28.1 %copy-start.8 = (f32[101376]{0:T(1024)}, f32[101376]{0:T(1024)S(1)}, u32[]{:S(2)}) copy-start(f32[101376]{0:T(1024)S(1)} %collective-permute-done.2) | copy-start | bytes 1216516
  46.2 11.4 %collective-permute-start.4 = (f32[101376]{0:T(1024)S(1)}, f32[101376]{0:T(1024)S(1)}, u32[]{:S(2)}, u32[]{:S(2)}) collective-permute-start(f32[101376]{0:T(1024)S(1)} %collective-permute-done.2), channel_id=1, source_target_pairs={{1,0},{2,1},{3,2},{4,3},{5,4},{6,5},{7,6},{0,7},{9,8},{10,9},{11,1... | collective-permute-start | bytes 1216520 | tf_op jit(solution)/jit(body)/shard_map/ppermute | solution.py:106
  53.3 21.0 %copy-start.9 = (f32[101376]{0:T(1024)}, f32[101376]{0:T(1024)S(1)}, u32[]{:S(2)}) copy-start(f32[101376]{0:T(1024)S(1)} %collective-permute-done.3) | copy-start | bytes 1216516
  53.3 10.9 %collective-permute-start.5 = (f32[101376]{0:T(1024)S(1)}, f32[101376]{0:T(1024)S(1)}, u32[]{:S(2)}, u32[]{:S(2)}) collective-permute-start(f32[101376]{0:T(1024)S(1)} %collective-permute-done.3), channel_id=1, source_target_pairs={{0,1},{1,2},{2,3},{3,4},{4,5},{5,6},{6,7},{7,0},{8,9},{9,10},{10,1... | collective-permute-start | bytes 1216520 | tf_op jit(solution)/jit(body)/shard_map/ppermute | solution.py:102
  57.6 16.7 %copy-start.10 = (f32[101376]{0:T(1024)}, f32[101376]{0:T(1024)S(1)}, u32[]{:S(2)}) copy-start(f32[101376]{0:T(1024)S(1)} %collective-permute-done.4) | copy-start | bytes 1216516
  57.6 9.4 %collective-permute-start.6 = (f32[101376]{0:T(1024)S(1)}, f32[101376]{0:T(1024)S(1)}, u32[]{:S(2)}, u32[]{:S(2)}) collective-permute-start(f32[101376]{0:T(1024)S(1)} %collective-permute-done.4), channel_id=1, source_target_pairs={{1,0},{2,1},{3,2},{4,3},{5,4},{6,5},{7,6},{0,7},{9,8},{10,9},{11,1... | collective-permute-start | bytes 1216520 | tf_op jit(solution)/jit(body)/shard_map/ppermute | solution.py:106
  64.2 10.1 %copy-start.11 = (f32[101376]{0:T(1024)}, f32[101376]{0:T(1024)S(1)}, u32[]{:S(2)}) copy-start(f32[101376]{0:T(1024)S(1)} %collective-permute-done.5) | copy-start | bytes 1216516
  64.2 10.1 %collective-permute-start.7 = (f32[101376]{0:T(1024)S(1)}, f32[101376]{0:T(1024)S(1)}, u32[]{:S(2)}, u32[]{:S(2)}) collective-permute-start(f32[101376]{0:T(1024)S(1)} %collective-permute-done.5), channel_id=1, source_target_pairs={{0,1},{1,2},{2,3},{3,4},{4,5},{5,6},{6,7},{7,0},{8,9},{9,10},{10,1... | collective-permute-start | bytes 1216520 | tf_op jit(solution)/jit(body)/shard_map/ppermute | solution.py:102
  67.1 7.3 %copy-start.12 = (f32[101376]{0:T(1024)}, f32[101376]{0:T(1024)S(1)}, u32[]{:S(2)}) copy-start(f32[101376]{0:T(1024)S(1)} %collective-permute-done.6) | copy-start | bytes 1216516
  87.7 2.1 %slice-start = ((f32[8,101376]{1,0:T(8,128)}), f32[8,3072]{1,0:T(8,128)S(1)}, s32[]{:S(2)}) async-start(f32[8,101376]{1,0:T(8,128)} %copy-done), calls=%async_computation.3 | async-start | bytes 196608 | tf_op jit(solution)/jit(body)/shard_map/slice | solution.py:113
  99.0 1.7 copy-start.17
  99.0 1.7 copy-start.18
  106.4 1.7 copy-start.19
  108.1 4.4 %copy-start.1 = (f32[8,2,2,2,96,128]{5,4,2,1,0,3:T(8,128)S(1)}, f32[8,2,2,2,96,128]{5,4,2,1,0,3:T(8,128)}, u32[]{:S(2)}) copy-start(f32[8,2,2,2,96,128]{5,4,2,1,0,3:T(8,128)} %copy.108) | copy-start | bytes 9437188
  118.7 9.0 %copy-start.15 = (f32[4,2,8,2,128]{4,3,2,1,0:T(2,128)S(1)}, f32[4,2,8,2,128]{4,3,2,1,0:T(2,128)}, u32[]{:S(2)}) copy-start(f32[4,2,8,2,128]{4,3,2,1,0:T(2,128)} %copy.107) | copy-start | bytes 196612
  118.8 9.0 %copy-start.16 = (f32[4,2,8,2,128]{4,3,2,1,0:T(2,128)S(1)}, f32[4,2,8,2,128]{4,3,2,1,0:T(2,128)}, u32[]{:S(2)}) copy-start(f32[4,2,8,2,128]{4,3,2,1,0:T(2,128)} %copy.110) | copy-start | bytes 196612
  127.8 6.4 %copy-start.2 = (f32[4,2,2,1,64,128]{5,4,2,1,0,3:T(8,128)S(1)}, f32[4,2,2,1,64,128]{5,4,2,1,0,3:T(8,128)}, u32[]{:S(2)}) copy-start(f32[4,2,2,1,64,128]{5,4,2,1,0,3:T(8,128)} %negate_bitcast_fusion.5) | copy-start | bytes 1572868
  127.8 6.4 %copy-start.3 = (f32[4,2,2,1,64,128]{5,4,2,1,0,3:T(8,128)S(1)}, f32[4,2,2,1,64,128]{5,4,2,1,0,3:T(8,128)}, u32[]{:S(2)}) copy-start(f32[4,2,2,1,64,128]{5,4,2,1,0,3:T(8,128)} %negate_bitcast_fusion.4) | copy-start | bytes 1572868
  127.8 6.4 %copy-start.4 = (f32[4,2,2,1,64,128]{5,4,2,1,0,3:T(8,128)S(1)}, f32[4,2,2,1,64,128]{5,4,2,1,0,3:T(8,128)}, u32[]{:S(2)}) copy-start(f32[4,2,2,1,64,128]{5,4,2,1,0,3:T(8,128)} %negate_bitcast_fusion.3) | copy-start | bytes 1572868
  127.8 6.4 %copy-start.5 = (f32[4,2,2,1,64,128]{5,4,2,1,0,3:T(8,128)S(1)}, f32[4,2,2,1,64,128]{5,4,2,1,0,3:T(8,128)}, u32[]{:S(2)}) copy-start(f32[4,2,2,1,64,128]{5,4,2,1,0,3:T(8,128)} %negate_bitcast_fusion.2) | copy-start | bytes 1572868
  183.3 6.0 %collective-permute-start.9 = (f32[2,2,2,64,128]{4,3,2,1,0:T(8,128)S(1)}, f32[2,2,2,64,128]{4,3,2,1,0:T(8,128)S(1)}, u32[]{:S(2)}, u32[]{:S(2)}) collective-permute-start(f32[2,2,2,64,128]{4,3,2,1,0:T(8,128)S(1)} %get-tuple-element.47), channel_id=1, source_target_pairs={{32,0},{64,32},{96,64},{128,96},{160,128},{192,160},{224,192},{0,2... | collective-permute-start | bytes 786440 | tf_op jit(solution)/jit(body)/shard_map/ppermute | solution.py:128
  185.4 7.0 %collective-permute-start.10 = (f32[2,2,2,64,128]{4,3,2,1,0:T(8,128)S(1)}, f32[2,2,2,64,128]{4,3,2,1,0:T(8,128)S(1)}, u32[]{:S(2)}, u32[]{:S(2)}) collective-permute-start(f32[2,2,2,64,128]{4,3,2,1,0:T(8,128)S(1)} %get-tuple-element.46), channel_id=1, source_target_pairs={{0,32},{32,64},{64,96},{96,128},{128,160},{160,192},{192,224},{224... | collective-permute-start | bytes 786440 | tf_op jit(solution)/jit(body)/shard_map/ppermute | solution.py:129
  (4 other events, 5.0 us)
Sparse Core Ops, SparseCore 0:
  136.8 45.4 reduce-scatter.1
where the time goes:
time: 202 us; the launch traced here: 201 us
  waiting for transfers between devices  69.2 us (34%)
  local copies, waits for them, and re-layouts  62.2 us (31%)
  other arithmetic  28.7 us (14%)
  starting transfers between devices  17.6 us (9%)
  between operations  13.9 us (7%)
  matrix products  9.01 us (4%)
    reduce_scatter x1, waiting for transfers between devices, body(): mine = lax.psum_scatter(merged, 'gy', scatter_dimension=0, tiled=False)  45.6 us
    unnamed x48, local copies, waits for them, and re-layouts  17.1 us
    mul x12, local copies, waits for them, and re-layouts, combine(): prod_re = -jnp.sum(col_re * row_re - col_im * row_im, axis=(2, 3))  16.4 us
    ppermute x4, waiting for transfers between devices, body(): forward = lax.ppermute(forward, 'gz', right)  16.2 us
    reduce_sum x3, other arithmetic, combine(): prod_re = -jnp.sum(col_re * row_re - col_im * row_im, axis=(2, 3))  11.6 us
    another operation x1, local copies, waits for them, and re-layouts, body(): ring = jnp.stack(carried)  10.9 us
    dot_general x1, matrix products, spectrum(): out = jnp.dot(traces.reshape(shots * recv, samples), table, precision=HIGH)  9.01 us
    mul x3, other arithmetic, combine(): scaled = block[None] * weight[:, :, :, None, None, :, None]  8.75 us
  transfers between devices with their start and end apart: 13, of which 7 were waited for; matrix products, arithmetic and copies ran while one was open for 11% of the time, Pallas kernels for 0%

commit v1 on v0

--- a/solution.py
+++ b/solution.py
@@ -38,13 +38,13 @@
 
 
 def combine(cols, weight, block):
-    scaled = block[None] * weight[:, :, :, None, None, :, None]
+    w = weight[:, None, :, :, None, :, None]
     col_re = cols[:, :, :, :, None, 0, None, :]
     col_im = cols[:, :, :, :, None, 1, None, :]
-    row_re = scaled[:, None, :, :, :, 0]
-    row_im = scaled[:, None, :, :, :, 1]
-    prod_re = -jnp.sum(col_re * row_re - col_im * row_im, axis=(2, 3))
-    prod_im = -jnp.sum(col_re * row_im + col_im * row_re, axis=(2, 3))
+    row_re = block[None, None, :, :, :, 0]
+    row_im = block[None, None, :, :, :, 1]
+    prod_re = -jnp.sum(w * (col_re * row_re - col_im * row_im), axis=(2, 3))
+    prod_im = -jnp.sum(w * (col_re * row_im + col_im * row_re), axis=(2, 3))
     return jnp.stack([prod_re, prod_im], axis=3)
 
 
@@ -68,14 +68,9 @@
     taper_rows = taper_table.shape[0]
     pick = taper_index.reshape(sides, rows, cols, CAP)[..., None] == jnp.arange(taper_rows, dtype=jnp.int32)
     src_weight = jnp.sum(jnp.where(pick[..., None], taper_table, 0.0), axis=-2)
-    full_table = aperture.reshape(line_count, rows, cols, sides, rows, cols, CAP)
+    own_blocks = lax.dynamic_slice_in_dim(aperture, (my_line * rows + my_row) * cols, cols, axis=0)
     slot_table = lax.dynamic_index_in_dim(
-        lax.dynamic_index_in_dim(
-            lax.dynamic_index_in_dim(full_table, my_line, 0, False), my_row, 0, False
-        ),
-        my_col,
-        3,
-        False,
+        own_blocks.reshape(cols, sides, rows, cols, CAP), my_col, 3, False
     )
 
     table = dft_matrix(samples)
@@ -117,17 +112,17 @@
     dense = jnp.sum(jnp.where(hit[..., None], weights[:, :, :, :, None, :], 0.0), axis=3)
     dense = jnp.transpose(dense, (1, 2, 0, 4, 3))
 
-    total = []
-    for s in range(sides):
+    def side_part(s):
         lo, hi = spans[s]
         cols_s = jnp.take(side_cols[s], sources, axis=2)
-        total.append(combine(cols_s, dense[s, :, :, :, lo:hi], gathered[:, :, :, :, lo:hi]))
-    merged = jnp.concatenate(total, axis=4)
-    mine = lax.psum_scatter(merged, "gy", scatter_dimension=0, tiled=False)
-    first, middle = 2 * width, 2 * width + blocks
-    from_up = lax.ppermute(mine[:, :, :, :first], "line", down)
-    from_down = lax.ppermute(mine[:, :, :, middle:], "line", up)
-    result = mine[:, :, :, first:middle]
+        return combine(cols_s, dense[s, :, :, :, lo:hi], gathered[:, :, :, :, lo:hi])
+
+    outer = jnp.concatenate([side_part(0), side_part(2)], axis=4)
+    outer = lax.psum_scatter(outer, "gy", scatter_dimension=0, tiled=False)
+    first = 2 * width
+    from_up = lax.ppermute(outer[:, :, :, :first], "line", down)
+    from_down = lax.ppermute(outer[:, :, :, first:], "line", up)
+    result = lax.psum_scatter(side_part(1), "gy", scatter_dimension=0, tiled=False)
     result = result.at[:, :, :, width:].add(from_up)
     result = result.at[:, :, :, : 2 * width].add(from_down)
     result = jnp.transpose(result, (0, 3, 1, 2, 4))

time: 202 us -> 170 us (0.84)
  local copies, waits for them, and re-layouts: 62.2 us -> 35.4 us
  other arithmetic: 28.7 us -> 17.6 us
  waiting for transfers between devices: 69.2 us -> 72 us
  starting transfers between devices: 17.6 us -> 20.3 us
    unnamed x48 -> x19, local copies, waits for them, and re-layouts: 17.1 us -> 2.16 us
    mul x3 -> x0, other arithmetic: 8.75 us -> none  [combine(): scaled = block[None] * weight[:, :, :, None, None, :, None]]
    mul x13 -> x18, local copies, waits for them, and re-layouts: 16.5 us -> 8.24 us  [combine(): prod_re = -jnp.sum(w * (col_re * row_re - col_im * row_im), axis=(2, 3))]
    reduce_scatter x1 -> x2, waiting for transfers between devices: 45.6 us -> 52.2 us  [the longest x1 27.4 us: body(): lax.psum_scatter(side_part(1), 'gy', scatter_dimension=0, tiled=False)]
    ppermute x2, waiting for transfers between devices: 4.98 us -> 0.01 us  [the longest x1 0.01 us: body(): from_up = lax.ppermute(outer[:, :, :, :first], 'line', down)]
    neg x6, other arithmetic: 3.51 us -> 0.28 us  [the longest x3 0.14 us: combine(): prod_re = -jnp.sum(w * (col_re * row_re - col_im * row_im), axis=(2, 3))]
    ppermute x4, waiting for transfers between devices: 16.2 us -> 13.6 us  [body(): forward = lax.ppermute(forward, 'gz', right)]
    slice x3 -> x2, local copies, waits for them, and re-layouts: 2.4 us -> 4.82 us  [the longest x1 3.75 us: body(): gathered = ring[:, :spec_size].reshape((len(carried),) + lanes.shape)]
  transfers between devices with their start and end apart: 13 -> 14, of which waited for: 7 -> 9; matrix products, arithmetic and copies ran while one was open for 11% -> 12% of each run, Pallas kernels for 0% -> 0%
where the time goes in v1:
time: 170 us; the launch traced here: 168 us
  waiting for transfers between devices  72 us (42%)
  local copies, waits for them, and re-layouts  35.4 us (21%)
  starting transfers between devices  20.3 us (12%)
  other arithmetic  17.6 us (10%)
  between operations  13.9 us (8%)
  matrix products  9.01 us (5%)
    reduce_scatter x1, waiting for transfers between devices, body(): lax.psum_scatter(side_part(1), 'gy', scatter_dimension=0, tiled=False)  27.4 us
    reduce_scatter x1, waiting for transfers between devices, body(): outer = lax.psum_scatter(outer, 'gy', scatter_dimension=0, tiled=False)  24.9 us
    ppermute x4, waiting for transfers between devices, body(): forward = lax.ppermute(forward, 'gz', right)  13.6 us
    reduce_sum x3, other arithmetic, combine(): prod_re = -jnp.sum(w * (col_re * row_re - col_im * row_im), axis=(2, 3))  10.8 us
    another operation x1, local copies, waits for them, and re-layouts, body(): ring = jnp.stack(carried)  9.89 us
    dot_general x1, matrix products, spectrum(): out = jnp.dot(traces.reshape(shots * recv, samples), table, precision=HIGH)  9.01 us
    mul x18, local copies, waits for them, and re-layouts, combine(): prod_re = -jnp.sum(w * (col_re * row_re - col_im * row_im), axis=(2, 3))  8.24 us
    ppermute x3, starting transfers between devices, body(): backward = lax.ppermute(backward, 'gz', left)  6.62 us
  transfers between devices with their start and end apart: 14, of which 9 were waited for; matrix products, arithmetic and copies ran while one was open for 12% of the time, Pallas kernels for 0%

profile of v1, /device:TPU:32, one launch (start us, length us, event | category | flops | bytes accessed | tf_op | source)
XLA Modules:
  0.0 168.3 jit_solution(5818493908548478615)
XLA Ops:
  7.6 9.0 %fusion.4 = f32[384,256]{0,1:T(8,128)S(1)} fusion(f32[384,4096]{1,0:T(8,128)} %bitcast.100, f32[4096,128]{1,0:T(8,128)S(1)} %bitcast.99, f32[4096,128]{1,0:T(8,128)S(1)} %bitcast.98), kind=kOutput, calls=%fused_computation.21 | convolution fusion | flops 2416967680 | bytes 10878976 | tf_op jit(solution)/jit(body)/shard_map/dot_general | solution.py:36
  18.7 2.0 %collective-permute-start = (f32[101376]{0:T(1024)S(1)}, f32[101376]{0:T(1024)}, u32[]{:S(2)}, u32[]{:S(2)}) collective-permute-start(f32[101376]{0:T(1024)S(1)} %pad_maximum_fusion.1), channel_id=1, source_target_pairs={{0,1},{1,2},{2,3},{3,4},{4,5},{5,6},{6,7},{7,0},{8,9},{9,10},{10,1... | collective-permute-start | bytes 1216520 | tf_op jit(solution)/jit(body)/shard_map/ppermute | solution.py:97
  21.9 4.5 %all-to-all-start = ((f32[3,2,4,8,2,2,128]{6,5,4,3,1,0,2:T(2,128)}), f32[3,2,4,8,2,2,128]{6,5,4,3,1,0,2:T(2,128)S(1)}, u32[]{:S(2)}, u32[]{:S(2)}) async-start(f32[3,2,4,8,2,2,128]{6,5,4,3,1,0,2:T(2,128)} %copy.133), calls=%async_computation | async-start | bytes 786432 | tf_op jit(solution)/jit(body)/shard_map/all_to_all | solution.py:81
  27.6 2.3 %collective-permute-done = f32[101376]{0:T(1024)} collective-permute-done((f32[101376]{0:T(1024)S(1)}, f32[101376]{0:T(1024)}, u32[]{:S(2)}, u32[]{:S(2)}) %collective-permute-start) | collective-permute-done | bytes 405536 | tf_op jit(solution)/jit(body)/shard_map/ppermute | solution.py:97
  30.0 1.9 %collective-permute-start.2 = (f32[101376]{0:T(1024)}, f32[101376]{0:T(1024)}, u32[]{:S(2)}, u32[]{:S(2)}) collective-permute-start(f32[101376]{0:T(1024)} %collective-permute-done), channel_id=1, source_target_pairs={{0,1},{1,2},{2,3},{3,4},{4,5},{5,6},{6,7},{7,0},{8,9},{9,10},{10,1... | collective-permute-start | bytes 1216520 | tf_op jit(solution)/jit(body)/shard_map/ppermute | solution.py:97
  31.9 2.1 %all-to-all-done = f32[3,2,4,8,2,2,128]{6,5,4,3,1,0,2:T(2,128)S(1)} async-done(((f32[3,2,4,8,2,2,128]{6,5,4,3,1,0,2:T(2,128)}), f32[3,2,4,8,2,2,128]{6,5,4,3,1,0,2:T(2,128)S(1)}, u32[]{:S(2)}, u32[]{:S(2)}) %all-to-all-start) | async-done | bytes 393248 | tf_op jit(solution)/jit(body)/shard_map/all_to_all | solution.py:81
  34.3 2.9 %collective-permute-start.8 = (f32[4,2,8,2,2,128]{5,0,4,3,2,1:T(4,128)S(1)}, f32[4,2,8,2,2,128]{5,0,4,3,2,1:T(4,128)S(1)}, u32[]{:S(2)}, u32[]{:S(2)}) collective-permute-start(f32[4,2,8,2,2,128]{5,0,4,3,2,1:T(4,128)S(1)} %get-tuple-element.47), channel_id=1, source_target_pairs={{32,0},{64,32},{96,64},{128,96},{160,128},{192,160},{224,192},{0,2... | collective-permute-start | bytes 393224 | tf_op jit(solution)/jit(body)/shard_map/ppermute | solution.py:86
  37.3 4.1 %collective-permute-start.3 = (f32[101376]{0:T(1024)}, f32[101376]{0:T(1024)S(1)}, u32[]{:S(2)}, u32[]{:S(2)}) collective-permute-start(f32[101376]{0:T(1024)} %collective-permute-done.1), channel_id=1, source_target_pairs={{1,0},{2,1},{3,2},{4,3},{5,4},{6,5},{7,6},{0,7},{9,8},{10,9},{11,1... | collective-permute-start | bytes 1216520 | tf_op jit(solution)/jit(body)/shard_map/ppermute | solution.py:101
  41.4 1.9 %collective-permute-done.2 = f32[101376]{0:T(1024)} collective-permute-done((f32[101376]{0:T(1024)}, f32[101376]{0:T(1024)}, u32[]{:S(2)}, u32[]{:S(2)}) %collective-permute-start.2) | collective-permute-done | bytes 405536 | tf_op jit(solution)/jit(body)/shard_map/ppermute | solution.py:97
  43.3 0.9 iota_compare_fusion
  47.0 2.2 %collective-permute-done.3 = f32[101376]{0:T(1024)S(1)} collective-permute-done((f32[101376]{0:T(1024)}, f32[101376]{0:T(1024)S(1)}, u32[]{:S(2)}, u32[]{:S(2)}) %collective-permute-start.3) | collective-permute-done | bytes 405536 | tf_op jit(solution)/jit(body)/shard_map/ppermute | solution.py:101
  49.2 2.4 %collective-permute-start.5 = (f32[101376]{0:T(1024)S(1)}, f32[101376]{0:T(1024)S(1)}, u32[]{:S(2)}, u32[]{:S(2)}) collective-permute-start(f32[101376]{0:T(1024)S(1)} %collective-permute-done.3), channel_id=1, source_target_pairs={{1,0},{2,1},{3,2},{4,3},{5,4},{6,5},{7,6},{0,7},{9,8},{10,9},{11,1... | collective-permute-start | bytes 1216520 | tf_op jit(solution)/jit(body)/shard_map/ppermute | solution.py:101
  51.6 2.9 %collective-permute-done.4 = f32[101376]{0:T(1024)} collective-permute-done((f32[101376]{0:T(1024)}, f32[101376]{0:T(1024)}, u32[]{:S(2)}, u32[]{:S(2)}) %collective-permute-start.4) | collective-permute-done | bytes 405536 | tf_op jit(solution)/jit(body)/shard_map/ppermute | solution.py:97
  56.6 1.9 %collective-permute-done.5 = f32[101376]{0:T(1024)S(1)} collective-permute-done((f32[101376]{0:T(1024)S(1)}, f32[101376]{0:T(1024)S(1)}, u32[]{:S(2)}, u32[]{:S(2)}) %collective-permute-start.5) | collective-permute-done | bytes 405536 | tf_op jit(solution)/jit(body)/shard_map/ppermute | solution.py:101
  58.4 6.4 %collective-permute-done.6 = f32[101376]{0:T(1024)} collective-permute-done((f32[101376]{0:T(1024)}, f32[101376]{0:T(1024)}, u32[]{:S(2)}, u32[]{:S(2)}) %collective-permute-start.6) | collective-permute-done | bytes 405536 | tf_op jit(solution)/jit(body)/shard_map/ppermute | solution.py:97
  64.9 9.9 %stack.50 = f32[8,101376]{1,0:T(8,128)} concatenate(f32[1,101376]{1,0:T(1,128)S(1)} %bitcast.103, f32[1,101376]{1,0:T(1,128)} %bitcast.10, f32[1,101376]{1,0:T(1,128)} %bitcast.11, f32[1,101376]{1,0:T(1,128)} %bitcast.12, f32[1,101376]{1,0:T(1,128)S(1)} %bitcast.112, f32[1,101376]{1,0:T(1,128)} %bitcast.14, f32[1,101376]{1,0:T(1,128)S(1)} %bitcast.113, f32[1,101376]{1,0:T(1,128)} %bitcast.16), dimensions={0} | concatenate | bytes 6488064 | tf_op jit(solution)/jit(body)/shard_map/stack | solution.py:105
  74.8 3.8 %slice.176 = f32[8,98304]{1,0:T(8,128)} slice(f32[8,101376]{1,0:T(8,128)} %stack.50), slice={[0:8], [0:98304]} | slice | bytes 6291456 | tf_op jit(solution)/jit(body)/shard_map/slice | solution.py:106
  79.2 1.7 %select_reduce_fusion = f32[8,3,4,96,2]{3,4,2,1,0:T(2,128)S(1)} fusion(f32[8,3,4,16,2]{3,4,2,1,0:T(2,128)S(1)} %copy.130, pred[8,3,4,16,96]{4,3,2,1,0:T(8,128)(4,1)} %iota_compare_fusion), kind=kLoop, calls=%fused_computation.20 | loop fusion | flops 571392 | bytes 233472 | tf_op jit(solution)/jit(body)/shard_map/reduce_sum | solution.py:112
  81.0 2.5 %slice_bitcast_fusion.5 = (f32[8,2,2,64,128]{4,0,3,2,1:T(8,128)S(1)}, f32[8,2,2,64,128]{4,0,3,2,1:T(8,128)S(1)}, f32[8,2,2,64,128]{4,0,3,2,1:T(8,128)S(1)}, f32[8,2,2,64,128]{4,0,3,2,1:T(8,128)S(1)}) fusion(f32[8,2,2,2,96,128]{5,0,4,3,2,1:T(8,128)} %bitcast.96), kind=kLoop, calls=%fused_computation.25 | loop fusion | bytes 8388608 | tf_op jit(solution)/jit(body)/shard_map/mul | solution.py:46
  84.3 3.2 %multiply_reduce_fusion.5 = (f32[4,2,2,64,128]{4,3,2,1,0:T(8,128)S(1)}, f32[4,2,2,64,128]{4,3,2,1,0:T(8,128)S(1)}) fusion(f32[8,2,2,64,128]{4,3,2,1,0:T(8,128)S(1)} %copy.144, f32[4,2,8,2,128]{4,3,2,1,0:T(2,128)S(1)} %copy-done.4, f32[8,2,2,64,128]{4,3,2,1,0:T(8,128)S(1)} %copy.142, f32[4,2,8,2,128]{4,3,2,1,0:T(2,128)S(1)} %copy-done.3, ...), kind=kLoop, calls=%fused_computation.9 | loop fusion | flops 20709376 | bytes 3293184 | tf_op jit(solution)/jit(body)/shard_map/reduce_sum | solution.py:46
  88.3 3.2 %multiply_reduce_fusion.3 = (f32[4,2,2,64,128]{4,3,2,1,0:T(8,128)S(1)}, f32[4,2,2,64,128]{4,3,2,1,0:T(8,128)S(1)}) fusion(f32[8,2,2,64,128]{4,3,2,1,0:T(8,128)S(1)} %copy.149, f32[4,2,8,2,128]{4,3,2,1,0:T(2,128)S(1)} %copy-done.2, f32[8,2,2,64,128]{4,3,2,1,0:T(8,128)S(1)} %copy.147, f32[4,2,8,2,128]{4,3,2,1,0:T(2,128)S(1)} %copy.146, ...), kind=kLoop, calls=%fused_computation.7 | loop fusion | flops 20709376 | bytes 3293184 | tf_op jit(solution)/jit(body)/shard_map/reduce_sum | solution.py:46
  91.8 1.5 copy.150
  93.7 2.1 %slice_bitcast_fusion.1 = (f32[8,2,2,96,128]{4,0,3,2,1:T(8,128)S(1)}, f32[8,2,2,96,128]{4,0,3,2,1:T(8,128)S(1)}) fusion(f32[8,2,2,2,96,128]{5,0,4,3,2,1:T(8,128)} %bitcast.97), kind=kLoop, calls=%fused_computation.18 | loop fusion | bytes 6291456 | tf_op jit(solution)/jit(body)/shard_map/mul | solution.py:46
  96.5 4.5 %multiply_reduce_fusion.1 = (f32[4,2,2,96,128]{4,3,2,1,0:T(8,128)S(1)}, f32[4,2,2,96,128]{4,3,2,1,0:T(8,128)S(1)}) fusion(f32[8,2,2,96,128]{4,3,2,1,0:T(8,128)S(1)} %copy.138, f32[4,2,8,2,128]{4,3,2,1,0:T(2,128)S(1)} %copy.137, f32[8,2,2,96,128]{4,3,2,1,0:T(8,128)S(1)} %copy.136, f32[4,2,8,2,128]{4,3,2,1,0:T(2,128)S(1)} %copy.135, ...), kind=kLoop, calls=%fused_computation.5 | loop fusion | flops 31064064 | bytes 4882432 | tf_op jit(solution)/jit(body)/shard_map/reduce_sum | solution.py:46
  101.3 1.3 copy.139
  102.6 24.9 %reduce-scatter.5.cloned.1.call-done = f32[1,2,2,2,128,128]{5,4,3,2,1,0:T(8,128)} async-done(((f32[4,2,2,2,128,128]{5,4,3,2,1,0:T(8,128)}), f32[1,2,2,2,128,128]{5,4,3,2,1,0:T(8,128)}) %reduce-scatter.5.cloned.1.call-update) | async-done | bytes 524304 | tf_op jit(solution)/jit(body)/shard_map/reduce_scatter | solution.py:121
  127.5 1.1 fusion.26
  128.5 2.1 %collective-permute-start.9 = (f32[2,2,2,64,128]{4,3,2,1,0:T(8,128)S(1)}, f32[2,2,2,64,128]{4,3,2,1,0:T(8,128)S(1)}, u32[]{:S(2)}, u32[]{:S(2)}) collective-permute-start(f32[2,2,2,64,128]{4,3,2,1,0:T(8,128)S(1)} %get-tuple-element.45), channel_id=1, source_target_pairs={{32,0},{64,32},{96,64},{128,96},{160,128},{192,160},{224,192},{0,2... | collective-permute-start | bytes 786440 | tf_op jit(solution)/jit(body)/shard_map/ppermute | solution.py:123
  130.6 27.4 %reduce-scatter.3.cloned.1.call-done = f32[1,2,2,2,96,128]{5,4,3,2,1,0:T(8,128)} async-done(((f32[4,2,2,2,96,128]{5,4,3,2,1,0:T(8,128)}), f32[1,2,2,2,96,128]{5,4,3,2,1,0:T(8,128)}) %reduce-scatter.3.cloned.1.call-update) | async-done | bytes 393232 | tf_op jit(solution)/jit(body)/shard_map/reduce_scatter | solution.py:125
  158.0 1.0 copy.164
  159.0 1.0 fusion.9
  160.4 1.1 copy.152
  (89 shorter events, 14.9 us)
Async XLA Ops:
  6.5 19.8 %copy-start = (s32[256,3,32,16]{0,3,2,1:T(8,128)S(1)}, s32[256,3,32,16]{0,3,2,1:T(8,128)}, u32[]{:S(2)}) copy-start(s32[256,3,32,16]{0,3,2,1:T(8,128)} %param.12) | copy-start | bytes 4718596
  7.6 9.5 %copy-start.5 = (s32[1,3,32,16]{2,3,1,0:T(8,128)S(1)}, s32[1,3,32,16]{2,3,1,0:T(8,128)}, u32[]{:S(2)}) copy-start(s32[1,3,32,16]{2,3,1,0:T(8,128)} %param.13) | copy-start | bytes 18436
  7.6 9.6 %copy-start.6 = (f32[8,2]{0,1:T(2,128)S(1)}, f32[8,2]{0,1:T(2,128)}, u32[]{:S(2)}) copy-start(f32[8,2]{0,1:T(2,128)} %param.14) | copy-start | bytes 196
  18.6 8.4 %copy-start.7 = (s32[8]{0:T(128)S(1)}, s32[8]{0:T(128)}, u32[]{:S(2)}) copy-start(s32[8]{0:T(128)} %constant.148.clone) | copy-start | bytes 100
  18.7 11.3 %collective-permute-start = (f32[101376]{0:T(1024)S(1)}, f32[101376]{0:T(1024)}, u32[]{:S(2)}, u32[]{:S(2)}) collective-permute-start(f32[101376]{0:T(1024)S(1)} %pad_maximum_fusion.1), channel_id=1, source_target_pairs={{0,1},{1,2},{2,3},{3,4},{4,5},{5,6},{6,7},{7,0},{8,9},{9,10},{10,1... | collective-permute-start | bytes 1216520 | tf_op jit(solution)/jit(body)/shard_map/ppermute | solution.py:97
  20.6 16.6 %collective-permute-start.1 = (f32[101376]{0:T(1024)S(1)}, f32[101376]{0:T(1024)}, u32[]{:S(2)}, u32[]{:S(2)}) collective-permute-start(f32[101376]{0:T(1024)S(1)} %pad_maximum_fusion.1), channel_id=1, source_target_pairs={{1,0},{2,1},{3,2},{4,3},{5,4},{6,5},{7,6},{0,7},{9,8},{10,9},{11,1... | collective-permute-start | bytes 1216520 | tf_op jit(solution)/jit(body)/shard_map/ppermute | solution.py:101
  21.9 12.2 %all-to-all-start = ((f32[3,2,4,8,2,2,128]{6,5,4,3,1,0,2:T(2,128)}), f32[3,2,4,8,2,2,128]{6,5,4,3,1,0,2:T(2,128)S(1)}, u32[]{:S(2)}, u32[]{:S(2)}) async-start(f32[3,2,4,8,2,2,128]{6,5,4,3,1,0,2:T(2,128)} %copy.133), calls=%async_computation | async-start | bytes 786432 | tf_op jit(solution)/jit(body)/shard_map/all_to_all | solution.py:81
  26.3 101.1 %reduce-scatter.5.cloned.1.call-start = ((), (), s32[]{:S(2)}) async-start(), calls=%async_computation.4 | async-start | bytes 2621440 | tf_op jit(solution)/jit(body)/shard_map/reduce_scatter | solution.py:121
  30.0 13.3 %collective-permute-start.2 = (f32[101376]{0:T(1024)}, f32[101376]{0:T(1024)}, u32[]{:S(2)}, u32[]{:S(2)}) collective-permute-start(f32[101376]{0:T(1024)} %collective-permute-done), channel_id=1, source_target_pairs={{0,1},{1,2},{2,3},{3,4},{4,5},{5,6},{6,7},{7,0},{8,9},{9,10},{10,1... | collective-permute-start | bytes 1216520 | tf_op jit(solution)/jit(body)/shard_map/ppermute | solution.py:97
  34.3 10.6 %collective-permute-start.7 = (f32[4,2,8,2,2,128]{5,0,4,3,2,1:T(4,128)S(1)}, f32[4,2,8,2,2,128]{5,0,4,3,2,1:T(4,128)S(1)}, u32[]{:S(2)}, u32[]{:S(2)}) collective-permute-start(f32[4,2,8,2,2,128]{5,0,4,3,2,1:T(4,128)S(1)} %get-tuple-element.46), channel_id=1, source_target_pairs={{0,32},{32,64},{64,96},{96,128},{128,160},{160,192},{192,224},{224... | collective-permute-start | bytes 393224 | tf_op jit(solution)/jit(body)/shard_map/ppermute | solution.py:84
  34.3 11.2 %collective-permute-start.8 = (f32[4,2,8,2,2,128]{5,0,4,3,2,1:T(4,128)S(1)}, f32[4,2,8,2,2,128]{5,0,4,3,2,1:T(4,128)S(1)}, u32[]{:S(2)}, u32[]{:S(2)}) collective-permute-start(f32[4,2,8,2,2,128]{5,0,4,3,2,1:T(4,128)S(1)} %get-tuple-element.47), channel_id=1, source_target_pairs={{32,0},{64,32},{96,64},{128,96},{160,128},{192,160},{224,192},{0,2... | collective-permute-start | bytes 393224 | tf_op jit(solution)/jit(body)/shard_map/ppermute | solution.py:86
  37.3 11.9 %collective-permute-start.3 = (f32[101376]{0:T(1024)}, f32[101376]{0:T(1024)S(1)}, u32[]{:S(2)}, u32[]{:S(2)}) collective-permute-start(f32[101376]{0:T(1024)} %collective-permute-done.1), channel_id=1, source_target_pairs={{1,0},{2,1},{3,2},{4,3},{5,4},{6,5},{7,6},{0,7},{9,8},{10,9},{11,1... | collective-permute-start | bytes 1216520 | tf_op jit(solution)/jit(body)/shard_map/ppermute | solution.py:101
  43.3 11.2 %collective-permute-start.4 = (f32[101376]{0:T(1024)}, f32[101376]{0:T(1024)}, u32[]{:S(2)}, u32[]{:S(2)}) collective-permute-start(f32[101376]{0:T(1024)} %collective-permute-done.2), channel_id=1, source_target_pairs={{0,1},{1,2},{2,3},{3,4},{4,5},{5,6},{6,7},{7,0},{8,9},{9,10},{10,1... | collective-permute-start | bytes 1216520 | tf_op jit(solution)/jit(body)/shard_map/ppermute | solution.py:97
  49.2 9.3 %collective-permute-start.5 = (f32[101376]{0:T(1024)S(1)}, f32[101376]{0:T(1024)S(1)}, u32[]{:S(2)}, u32[]{:S(2)}) collective-permute-start(f32[101376]{0:T(1024)S(1)} %collective-permute-done.3), channel_id=1, source_target_pairs={{1,0},{2,1},{3,2},{4,3},{5,4},{6,5},{7,6},{0,7},{9,8},{10,9},{11,1... | collective-permute-start | bytes 1216520 | tf_op jit(solution)/jit(body)/shard_map/ppermute | solution.py:101
  54.5 10.4 %collective-permute-start.6 = (f32[101376]{0:T(1024)}, f32[101376]{0:T(1024)}, u32[]{:S(2)}, u32[]{:S(2)}) collective-permute-start(f32[101376]{0:T(1024)} %collective-permute-done.4), channel_id=1, source_target_pairs={{0,1},{1,2},{2,3},{3,4},{4,5},{5,6},{6,7},{7,0},{8,9},{9,10},{10,1... | collective-permute-start | bytes 1216520 | tf_op jit(solution)/jit(body)/shard_map/ppermute | solution.py:97
  74.8 3.8 %slice-start = ((f32[8,101376]{1,0:T(8,128)}), f32[8,3072]{1,0:T(8,128)S(1)}, s32[]{:S(2)}) async-start(f32[8,101376]{1,0:T(8,128)} %stack.50), calls=%async_computation.5 | async-start | bytes 196608 | tf_op jit(solution)/jit(body)/shard_map/slice | solution.py:108
  83.4 0.8 copy-start.3
  83.5 0.9 copy-start.4
  87.5 0.8 copy-start.2
  91.8 1.8 %copy-start.1 = (f32[4,2,8,2,2,128]{5,0,4,3,1,2:T(4,128)S(1)}, f32[4,2,8,2,2,128]{5,0,4,3,1,2:T(4,128)}, u32[]{:S(2)}) copy-start(f32[4,2,8,2,2,128]{5,0,4,3,1,2:T(4,128)} %get-tuple-element.61) | copy-start | bytes 393220
  93.3 64.6 %reduce-scatter.3.cloned.1.call-start = ((), (), s32[]{:S(2)}) async-start(), calls=%async_computation.3 | async-start | bytes 1966080 | tf_op jit(solution)/jit(body)/shard_map/reduce_scatter | solution.py:125
  128.5 30.4 %collective-permute-start.9 = (f32[2,2,2,64,128]{4,3,2,1,0:T(8,128)S(1)}, f32[2,2,2,64,128]{4,3,2,1,0:T(8,128)S(1)}, u32[]{:S(2)}, u32[]{:S(2)}) collective-permute-start(f32[2,2,2,64,128]{4,3,2,1,0:T(8,128)S(1)} %get-tuple-element.45), channel_id=1, source_target_pairs={{32,0},{64,32},{96,64},{128,96},{160,128},{192,160},{224,192},{0,2... | collective-permute-start | bytes 786440 | tf_op jit(solution)/jit(body)/shard_map/ppermute | solution.py:123
  130.6 29.3 %collective-permute-start.10 = (f32[2,2,2,64,128]{4,3,2,1,0:T(8,128)S(1)}, f32[2,2,2,64,128]{4,3,2,1,0:T(8,128)S(1)}, u32[]{:S(2)}, u32[]{:S(2)}) collective-permute-start(f32[2,2,2,64,128]{4,3,2,1,0:T(8,128)S(1)} %get-tuple-element.44), channel_id=1, source_target_pairs={{0,32},{32,64},{64,96},{96,128},{128,160},{160,192},{192,224},{224... | collective-permute-start | bytes 786440 | tf_op jit(solution)/jit(body)/shard_map/ppermute | solution.py:124
Sparse Core Ops, SparseCore 0:
  93.5 33.9 reduce-scatter.4
  130.0 27.9 reduce-scatter.2

commit v2 on v1

--- a/solution.py
+++ b/solution.py
@@ -76,16 +76,6 @@
     table = dft_matrix(samples)
     own = spectrum(shot_traces, table)
 
-    stacked = own.reshape(shots, sides, rows, cols, BP, 2, NF)
-    stacked = jnp.transpose(stacked, (1, 0, 2, 3, 4, 5, 6))
-    spread = lax.all_to_all(stacked, "gy", split_axis=2, concat_axis=2, tiled=True)
-    spread = jnp.transpose(spread, (0, 2, 1, 3, 4, 5, 6))
-    side_cols = [
-        lax.ppermute(spread[2], "line", up),
-        spread[1],
-        lax.ppermute(spread[0], "line", down),
-    ]
-
     lanes = jnp.transpose(own, (0, 2, 3, 1, 4))
     spec_size = lanes.size
     payload = jnp.concatenate([lanes.reshape(-1), src_weight.reshape(-1)])
@@ -101,6 +91,19 @@
             backward = lax.ppermute(backward, "gz", left)
             carried.append(backward)
             offsets.append(step)
+    first_arrival = carried[1][0]
+
+    stacked = own.reshape(shots, sides, rows, cols, BP, 2, NF)
+    stacked = jnp.transpose(stacked, (1, 0, 2, 3, 4, 5, 6))
+    stacked = stacked + 0.0 * first_arrival
+    spread = lax.all_to_all(stacked, "gy", split_axis=2, concat_axis=2, tiled=True)
+    spread = jnp.transpose(spread, (0, 2, 1, 3, 4, 5, 6))
+    side_cols = [
+        lax.ppermute(spread[2], "line", up),
+        spread[1],
+        lax.ppermute(spread[0], "line", down),
+    ]
+
     sources = (my_col + jnp.asarray(offsets, dtype=jnp.int32)) % cols
     ring = jnp.stack(carried)
     gathered = ring[:, :spec_size].reshape((len(carried),) + lanes.shape)
@@ -117,12 +120,12 @@
         cols_s = jnp.take(side_cols[s], sources, axis=2)
         return combine(cols_s, dense[s, :, :, :, lo:hi], gathered[:, :, :, :, lo:hi])
 
-    outer = jnp.concatenate([side_part(0), side_part(2)], axis=4)
-    outer = lax.psum_scatter(outer, "gy", scatter_dimension=0, tiled=False)
-    first = 2 * width
-    from_up = lax.ppermute(outer[:, :, :, :first], "line", down)
-    from_down = lax.ppermute(outer[:, :, :, first:], "line", up)
-    result = lax.psum_scatter(side_part(1), "gy", scatter_dimension=0, tiled=False)
+    merged = jnp.concatenate([side_part(0), side_part(1), side_part(2)], axis=4)
+    mine = lax.psum_scatter(merged, "gy", scatter_dimension=0, tiled=False)
+    first, middle = 2 * width, 2 * width + blocks
+    from_up = lax.ppermute(mine[:, :, :, :first], "line", down)
+    from_down = lax.ppermute(mine[:, :, :, middle:], "line", up)
+    result = mine[:, :, :, first:middle]
     result = result.at[:, :, :, width:].add(from_up)
     result = result.at[:, :, :, : 2 * width].add(from_down)
     result = jnp.transpose(result, (0, 3, 1, 2, 4))

time: 170 us -> 179 us (1.053)
  waiting for transfers between devices: 72 us -> 76.8 us
  local copies, waits for them, and re-layouts: 35.4 us -> 39.9 us
    ppermute x4, waiting for transfers between devices: 13.6 us -> 23.8 us  [body(): forward = lax.ppermute(forward, 'gz', right)]
    reduce_scatter x2 -> x1, waiting for transfers between devices: 52.2 us -> 45.7 us  [body(): mine = lax.psum_scatter(merged, 'gy', scatter_dimension=0, tiled=False)]
    ppermute x2, waiting for transfers between devices: 0.01 us -> 4.98 us  [the longest x1 2.86 us: body(): from_up = lax.ppermute(mine[:, :, :, :first], 'line', down)]
    ppermute x3, waiting for transfers between devices: 4.09 us -> 0.01 us  [body(): backward = lax.ppermute(backward, 'gz', left)]
    mul x18, local copies, waits for them, and re-layouts: 8.24 us -> 10.9 us  [combine(): prod_re = -jnp.sum(w * (col_re * row_re - col_im * row_im), axis=(2, 3))]
    slice x1 -> x3, local copies, waits for them, and re-layouts: 1.07 us -> 3.27 us  [the longest x1 1.18 us: body(): first_arrival = carried[1][0]]
  transfers between devices with their start and end apart: 14 -> 13, of which waited for: 9 -> 8; matrix products, arithmetic and copies ran while one was open for 12% -> 7% of each run, Pallas kernels for 0% -> 0%
where the time goes in v2:
time: 179 us; the launch traced here: 177 us
  waiting for transfers between devices  76.8 us (43%)
  local copies, waits for them, and re-layouts  39.9 us (22%)
  starting transfers between devices  19.2 us (11%)
  other arithmetic  17.7 us (10%)
  between operations  14.6 us (8%)
  matrix products  9.01 us (5%)
    reduce_scatter x1, waiting for transfers between devices, body(): mine = lax.psum_scatter(merged, 'gy', scatter_dimension=0, tiled=False)  45.7 us
    ppermute x4, waiting for transfers between devices, body(): forward = lax.ppermute(forward, 'gz', right)  23.8 us
    mul x18, local copies, waits for them, and re-layouts, combine(): prod_re = -jnp.sum(w * (col_re * row_re - col_im * row_im), axis=(2, 3))  10.9 us
    reduce_sum x3, other arithmetic, combine(): prod_re = -jnp.sum(w * (col_re * row_re - col_im * row_im), axis=(2, 3))  10.9 us
    another operation x1, local copies, waits for them, and re-layouts, body(): ring = jnp.stack(carried)  9.66 us
    dot_general x1, matrix products, spectrum(): out = jnp.dot(traces.reshape(shots * recv, samples), table, precision=HIGH)  9.01 us
    ppermute x3, starting transfers between devices, body(): backward = lax.ppermute(backward, 'gz', left)  5.27 us
    all_to_all x1, starting transfers between devices, body(): lax.all_to_all(stacked, 'gy', split_axis=2, concat_axis=2, tiled=True)  4.46 us
  transfers between devices with their start and end apart: 13, of which 8 were waited for; matrix products, arithmetic and copies ran while one was open for 7% of the time, Pallas kernels for 0%

profile of v2, /device:TPU:32, one launch (start us, length us, event | category | flops | bytes accessed | tf_op | source)
XLA Modules:
  0.0 177.2 jit_solution(5935649513832547167)
XLA Ops:
  7.6 9.0 %fusion.4 = f32[384,256]{0,1:T(8,128)S(1)} fusion(f32[384,4096]{1,0:T(8,128)} %bitcast.94, f32[4096,128]{1,0:T(8,128)S(1)} %bitcast.93, f32[4096,128]{1,0:T(8,128)S(1)} %bitcast.92), kind=kOutput, calls=%fused_computation.20 | convolution fusion | flops 2416967680 | bytes 10878976 | tf_op jit(solution)/jit(body)/shard_map/dot_general | solution.py:36
  20.0 2.0 %collective-permute-start = (f32[101376]{0:T(1024)S(1)}, f32[101376]{0:T(1024)}, u32[]{:S(2)}, u32[]{:S(2)}) collective-permute-start(f32[101376]{0:T(1024)S(1)} %pad_maximum_fusion), channel_id=1, source_target_pairs={{0,1},{1,2},{2,3},{3,4},{4,5},{5,6},{6,7},{7,0},{8,9},{9,10},{10,1... | collective-permute-start | bytes 1216520 | tf_op jit(solution)/jit(body)/shard_map/ppermute | solution.py:87
  22.7 8.5 %collective-permute-done = f32[101376]{0:T(1024)} collective-permute-done((f32[101376]{0:T(1024)S(1)}, f32[101376]{0:T(1024)}, u32[]{:S(2)}, u32[]{:S(2)}) %collective-permute-start) | collective-permute-done | bytes 405536 | tf_op jit(solution)/jit(body)/shard_map/ppermute | solution.py:87
  31.3 1.2 slice.183
  34.4 4.5 %all-to-all-start = ((f32[3,2,4,8,2,2,128]{6,5,4,3,1,0,2:T(2,128)}), f32[3,2,4,8,2,2,128]{6,5,4,3,1,0,2:T(2,128)S(1)}, u32[]{:S(2)}, u32[]{:S(2)}) async-start(f32[3,2,4,8,2,2,128]{6,5,4,3,1,0,2:T(2,128)} %copy.133), calls=%async_computation | async-start | bytes 786432 | tf_op jit(solution)/jit(body)/shard_map/all_to_all | solution.py:99
  39.5 2.0 %collective-permute-start.2 = (f32[101376]{0:T(1024)}, f32[101376]{0:T(1024)}, u32[]{:S(2)}, u32[]{:S(2)}) collective-permute-start(f32[101376]{0:T(1024)} %collective-permute-done), channel_id=1, source_target_pairs={{0,1},{1,2},{2,3},{3,4},{4,5},{5,6},{6,7},{7,0},{8,9},{9,10},{10,1... | collective-permute-start | bytes 1216520 | tf_op jit(solution)/jit(body)/shard_map/ppermute | solution.py:87
  41.5 2.4 %collective-permute-start.3 = (f32[101376]{0:T(1024)}, f32[101376]{0:T(1024)}, u32[]{:S(2)}, u32[]{:S(2)}) collective-permute-start(f32[101376]{0:T(1024)} %collective-permute-done.1), channel_id=1, source_target_pairs={{1,0},{2,1},{3,2},{4,3},{5,4},{6,5},{7,6},{0,7},{9,8},{10,9},{11,1... | collective-permute-start | bytes 1216520 | tf_op jit(solution)/jit(body)/shard_map/ppermute | solution.py:91
  44.0 2.3 %all-to-all-done = f32[3,2,4,8,2,2,128]{6,5,4,3,1,0,2:T(2,128)S(1)} async-done(((f32[3,2,4,8,2,2,128]{6,5,4,3,1,0,2:T(2,128)}), f32[3,2,4,8,2,2,128]{6,5,4,3,1,0,2:T(2,128)S(1)}, u32[]{:S(2)}, u32[]{:S(2)}) %all-to-all-start) | async-done | bytes 393248 | tf_op jit(solution)/jit(body)/shard_map/all_to_all | solution.py:99
  46.6 2.9 %collective-permute-start.8 = (f32[4,2,8,2,2,128]{5,0,4,3,2,1:T(4,128)S(1)}, f32[4,2,8,2,2,128]{5,0,4,3,2,1:T(4,128)S(1)}, u32[]{:S(2)}, u32[]{:S(2)}) collective-permute-start(f32[4,2,8,2,2,128]{5,0,4,3,2,1:T(4,128)S(1)} %get-tuple-element.47), channel_id=1, source_target_pairs={{32,0},{64,32},{96,64},{128,96},{160,128},{192,160},{224,192},{0,2... | collective-permute-start | bytes 393224 | tf_op jit(solution)/jit(body)/shard_map/ppermute | solution.py:104
  51.1 1.6 collective-permute-done.2
  53.1 2.7 %collective-permute-start.5 = (f32[101376]{0:T(1024)}, f32[101376]{0:T(1024)}, u32[]{:S(2)}, u32[]{:S(2)}) collective-permute-start(f32[101376]{0:T(1024)} %collective-permute-done.3), channel_id=1, source_target_pairs={{1,0},{2,1},{3,2},{4,3},{5,4},{6,5},{7,6},{0,7},{9,8},{10,9},{11,1... | collective-permute-start | bytes 1216520 | tf_op jit(solution)/jit(body)/shard_map/ppermute | solution.py:91
  58.6 5.4 %collective-permute-done.4 = f32[101376]{0:T(1024)} collective-permute-done((f32[101376]{0:T(1024)}, f32[101376]{0:T(1024)}, u32[]{:S(2)}, u32[]{:S(2)}) %collective-permute-start.4) | collective-permute-done | bytes 405536 | tf_op jit(solution)/jit(body)/shard_map/ppermute | solution.py:87
  66.1 8.3 %collective-permute-done.6 = f32[101376]{0:T(1024)S(1)} collective-permute-done((f32[101376]{0:T(1024)}, f32[101376]{0:T(1024)S(1)}, u32[]{:S(2)}, u32[]{:S(2)}) %collective-permute-start.6) | collective-permute-done | bytes 405536 | tf_op jit(solution)/jit(body)/shard_map/ppermute | solution.py:87
  74.4 9.7 %stack.50 = f32[8,101376]{1,0:T(8,128)} concatenate(f32[1,101376]{1,0:T(1,128)S(1)} %bitcast.97, f32[1,101376]{1,0:T(1,128)} %bitcast.10, f32[1,101376]{1,0:T(1,128)} %bitcast.11, f32[1,101376]{1,0:T(1,128)} %bitcast.12, f32[1,101376]{1,0:T(1,128)} %bitcast.13, f32[1,101376]{1,0:T(1,128)} %bitcast.14, f32[1,101376]{1,0:T(1,128)} %bitcast.15, f32[1,101376]{1,0:T(1,128)S(1)} %bitcast.107), dimensions={0} | concatenate | bytes 6488064 | tf_op jit(solution)/jit(body)/shard_map/stack | solution.py:108
  84.1 2.1 %slice.186 = f32[8,98304]{1,0:T(8,128)S(1)} slice(f32[8,101376]{1,0:T(8,128)} %stack.50), slice={[0:8], [0:98304]} | slice | bytes 6291456 | tf_op jit(solution)/jit(body)/shard_map/slice | solution.py:109
  86.2 2.1 %slice_bitcast_fusion.5 = (f32[8,2,2,64,128]{4,0,3,2,1:T(8,128)}, f32[8,2,2,64,128]{4,0,3,2,1:T(8,128)}, f32[8,2,2,64,128]{4,0,3,2,1:T(8,128)}, f32[8,2,2,64,128]{4,0,3,2,1:T(8,128)}) fusion(f32[8,2,2,2,96,128]{5,0,4,3,2,1:T(8,128)S(1)} %bitcast.90), kind=kLoop, calls=%fused_computation.24 | loop fusion | bytes 8388608 | tf_op jit(solution)/jit(body)/shard_map/mul | solution.py:46
  88.3 1.4 slice_bitcast_fusion.1
  89.7 1.7 copy.128
  92.4 1.7 select_reduce_fusion
  94.2 1.4 copy.136
  95.7 1.5 copy.138
  97.3 3.2 %multiply_reduce_fusion.5 = (f32[4,2,2,64,128]{4,3,2,1,0:T(8,128)S(1)}, f32[4,2,2,64,128]{4,3,2,1,0:T(8,128)S(1)}) fusion(f32[8,2,2,64,128]{4,3,2,1,0:T(8,128)S(1)} %copy.138, f32[4,2,8,2,128]{4,3,2,1,0:T(2,128)S(1)} %copy-done.8, f32[8,2,2,64,128]{4,3,2,1,0:T(8,128)S(1)} %copy.136, f32[4,2,8,2,128]{4,3,2,1,0:T(2,128)S(1)} %copy-done.7, ...), kind=kLoop, calls=%fused_computation.9 | loop fusion | flops 20709376 | bytes 3293184 | tf_op jit(solution)/jit(body)/shard_map/reduce_sum | solution.py:46
  101.3 4.6 %multiply_reduce_fusion.1 = (f32[4,2,2,96,128]{4,3,2,1,0:T(8,128)S(1)}, f32[4,2,2,96,128]{4,3,2,1,0:T(8,128)S(1)}) fusion(f32[8,2,2,96,128]{4,3,2,1,0:T(8,128)S(1)} %copy.143, f32[4,2,8,2,128]{4,3,2,1,0:T(2,128)S(1)} %copy-done.4, f32[8,2,2,96,128]{4,3,2,1,0:T(8,128)S(1)} %copy.141, f32[4,2,8,2,128]{4,3,2,1,0:T(2,128)S(1)} %copy.140, ...), kind=kLoop, calls=%fused_computation.5 | loop fusion | flops 31064064 | bytes 4882432 | tf_op jit(solution)/jit(body)/shard_map/reduce_sum | solution.py:46
  107.3 3.1 %multiply_reduce_fusion.3 = (f32[4,2,2,64,128]{4,3,2,1,0:T(8,128)S(1)}, f32[4,2,2,64,128]{4,3,2,1,0:T(8,128)S(1)}) fusion(f32[8,2,2,64,128]{4,3,2,1,0:T(8,128)S(1)} %copy.148, f32[4,2,8,2,128]{4,3,2,1,0:T(2,128)S(1)} %copy-done.6, f32[8,2,2,64,128]{4,3,2,1,0:T(8,128)S(1)} %copy.146, f32[4,2,8,2,128]{4,3,2,1,0:T(2,128)S(1)} %copy-done.5, ...), kind=kLoop, calls=%fused_computation.7 | loop fusion | flops 20709376 | bytes 3293184 | tf_op jit(solution)/jit(body)/shard_map/reduce_sum | solution.py:46
  110.9 2.1 %copy.149 = f32[4,2,2,2,224,128]{5,4,3,2,1,0:T(8,128)} copy(f32[4,2,2,2,224,128]{5,4,2,1,0,3:T(8,128)S(1)} %maximum_maximum_fusion) | data formatting | bytes 7340032 | tf_op jit(solution)/jit(body)/shard_map/concatenate | solution.py:123
  113.1 45.7 %reduce-scatter.2.cloned.1.call-done = f32[1,2,2,2,224,128]{5,4,3,2,1,0:T(8,128)} async-done(((f32[4,2,2,2,224,128]{5,4,3,2,1,0:T(8,128)}), f32[1,2,2,2,224,128]{5,4,3,2,1,0:T(8,128)}) %reduce-scatter.2.cloned.1.call-update) | async-done | bytes 917520 | tf_op jit(solution)/jit(body)/shard_map/reduce_scatter | solution.py:124
  158.7 1.1 fusion.25
  159.8 2.1 %collective-permute-start.9 = (f32[2,2,2,64,128]{4,3,2,1,0:T(8,128)S(1)}, f32[2,2,2,64,128]{4,3,2,1,0:T(8,128)S(1)}, u32[]{:S(2)}, u32[]{:S(2)}) collective-permute-start(f32[2,2,2,64,128]{4,3,2,1,0:T(8,128)S(1)} %get-tuple-element.45), channel_id=1, source_target_pairs={{32,0},{64,32},{96,64},{128,96},{160,128},{192,160},{224,192},{0,2... | collective-permute-start | bytes 786440 | tf_op jit(solution)/jit(body)/shard_map/ppermute | solution.py:126
  161.9 1.0 slice.202
  162.9 2.9 %collective-permute-done.9 = f32[2,2,2,64,128]{4,3,2,1,0:T(8,128)S(1)} collective-permute-done((f32[2,2,2,64,128]{4,3,2,1,0:T(8,128)S(1)}, f32[2,2,2,64,128]{4,3,2,1,0:T(8,128)S(1)}, u32[]{:S(2)}, u32[]{:S(2)}) %collective-permute-start.9) | collective-permute-done | bytes 262176 | tf_op jit(solution)/jit(body)/shard_map/ppermute | solution.py:126
  166.8 2.1 %collective-permute-done.10 = f32[2,2,2,64,128]{4,3,2,1,0:T(8,128)S(1)} collective-permute-done((f32[2,2,2,64,128]{4,3,2,1,0:T(8,128)S(1)}, f32[2,2,2,64,128]{4,3,2,1,0:T(8,128)S(1)}, u32[]{:S(2)}, u32[]{:S(2)}) %collective-permute-start.10) | collective-permute-done | bytes 262176 | tf_op jit(solution)/jit(body)/shard_map/ppermute | solution.py:127
  169.3 1.1 copy.151
  (95 shorter events, 19.3 us)
Async XLA Ops:
  6.5 15.5 %copy-start = (s32[256,3,32,16]{0,3,2,1:T(8,128)S(1)}, s32[256,3,32,16]{0,3,2,1:T(8,128)}, u32[]{:S(2)}) copy-start(s32[256,3,32,16]{0,3,2,1:T(8,128)} %param.12) | copy-start | bytes 4718596
  7.6 9.5 %copy-start.9 = (s32[1,3,32,16]{2,3,1,0:T(8,128)S(1)}, s32[1,3,32,16]{2,3,1,0:T(8,128)}, u32[]{:S(2)}) copy-start(s32[1,3,32,16]{2,3,1,0:T(8,128)} %param.13) | copy-start | bytes 18436
  7.6 9.6 %copy-start.10 = (f32[8,2]{0,1:T(2,128)S(1)}, f32[8,2]{0,1:T(2,128)}, u32[]{:S(2)}) copy-start(f32[8,2]{0,1:T(2,128)} %param.14) | copy-start | bytes 196
  16.8 5.9 %copy-start.11 = (s32[8]{0:T(128)S(1)}, s32[8]{0:T(128)}, u32[]{:S(2)}) copy-start(s32[8]{0:T(128)} %constant.149.clone) | copy-start | bytes 100
  20.0 11.3 %collective-permute-start = (f32[101376]{0:T(1024)S(1)}, f32[101376]{0:T(1024)}, u32[]{:S(2)}, u32[]{:S(2)}) collective-permute-start(f32[101376]{0:T(1024)S(1)} %pad_maximum_fusion), channel_id=1, source_target_pairs={{0,1},{1,2},{2,3},{3,4},{4,5},{5,6},{6,7},{7,0},{8,9},{9,10},{10,1... | collective-permute-start | bytes 1216520 | tf_op jit(solution)/jit(body)/shard_map/ppermute | solution.py:87
  22.0 19.6 %collective-permute-start.1 = (f32[101376]{0:T(1024)S(1)}, f32[101376]{0:T(1024)}, u32[]{:S(2)}, u32[]{:S(2)}) collective-permute-start(f32[101376]{0:T(1024)S(1)} %pad_maximum_fusion), channel_id=1, source_target_pairs={{1,0},{2,1},{3,2},{4,3},{5,4},{6,5},{7,6},{0,7},{9,8},{10,9},{11,1... | collective-permute-start | bytes 1216520 | tf_op jit(solution)/jit(body)/shard_map/ppermute | solution.py:91
  34.4 11.8 %all-to-all-start = ((f32[3,2,4,8,2,2,128]{6,5,4,3,1,0,2:T(2,128)}), f32[3,2,4,8,2,2,128]{6,5,4,3,1,0,2:T(2,128)S(1)}, u32[]{:S(2)}, u32[]{:S(2)}) async-start(f32[3,2,4,8,2,2,128]{6,5,4,3,1,0,2:T(2,128)} %copy.133), calls=%async_computation | async-start | bytes 786432 | tf_op jit(solution)/jit(body)/shard_map/all_to_all | solution.py:99
  38.9 119.9 %reduce-scatter.2.cloned.1.call-start = ((), (), s32[]{:S(2)}) async-start(), calls=%async_computation.2 | async-start | bytes 4587520 | tf_op jit(solution)/jit(body)/shard_map/reduce_scatter | solution.py:124
  39.5 13.1 %collective-permute-start.2 = (f32[101376]{0:T(1024)}, f32[101376]{0:T(1024)}, u32[]{:S(2)}, u32[]{:S(2)}) collective-permute-start(f32[101376]{0:T(1024)} %collective-permute-done), channel_id=1, source_target_pairs={{0,1},{1,2},{2,3},{3,4},{4,5},{5,6},{6,7},{7,0},{8,9},{9,10},{10,1... | collective-permute-start | bytes 1216520 | tf_op jit(solution)/jit(body)/shard_map/ppermute | solution.py:87
  41.5 11.6 %collective-permute-start.3 = (f32[101376]{0:T(1024)}, f32[101376]{0:T(1024)}, u32[]{:S(2)}, u32[]{:S(2)}) collective-permute-start(f32[101376]{0:T(1024)} %collective-permute-done.1), channel_id=1, source_target_pairs={{1,0},{2,1},{3,2},{4,3},{5,4},{6,5},{7,6},{0,7},{9,8},{10,9},{11,1... | collective-permute-start | bytes 1216520 | tf_op jit(solution)/jit(body)/shard_map/ppermute | solution.py:91
  46.5 9.3 %collective-permute-start.7 = (f32[4,2,8,2,2,128]{5,0,4,3,2,1:T(4,128)S(1)}, f32[4,2,8,2,2,128]{5,0,4,3,2,1:T(4,128)S(1)}, u32[]{:S(2)}, u32[]{:S(2)}) collective-permute-start(f32[4,2,8,2,2,128]{5,0,4,3,2,1:T(4,128)S(1)} %get-tuple-element.46), channel_id=1, source_target_pairs={{0,32},{32,64},{64,96},{96,128},{128,160},{160,192},{192,224},{224... | collective-permute-start | bytes 393224 | tf_op jit(solution)/jit(body)/shard_map/ppermute | solution.py:102
  46.6 9.9 %collective-permute-start.8 = (f32[4,2,8,2,2,128]{5,0,4,3,2,1:T(4,128)S(1)}, f32[4,2,8,2,2,128]{5,0,4,3,2,1:T(4,128)S(1)}, u32[]{:S(2)}, u32[]{:S(2)}) collective-permute-start(f32[4,2,8,2,2,128]{5,0,4,3,2,1:T(4,128)S(1)} %get-tuple-element.47), channel_id=1, source_target_pairs={{32,0},{64,32},{96,64},{128,96},{160,128},{192,160},{224,192},{0,2... | collective-permute-start | bytes 393224 | tf_op jit(solution)/jit(body)/shard_map/ppermute | solution.py:104
  52.7 11.3 %collective-permute-start.4 = (f32[101376]{0:T(1024)}, f32[101376]{0:T(1024)}, u32[]{:S(2)}, u32[]{:S(2)}) collective-permute-start(f32[101376]{0:T(1024)} %collective-permute-done.2), channel_id=1, source_target_pairs={{0,1},{1,2},{2,3},{3,4},{4,5},{5,6},{6,7},{7,0},{8,9},{9,10},{10,1... | collective-permute-start | bytes 1216520 | tf_op jit(solution)/jit(body)/shard_map/ppermute | solution.py:87
  53.1 13.0 %collective-permute-start.5 = (f32[101376]{0:T(1024)}, f32[101376]{0:T(1024)}, u32[]{:S(2)}, u32[]{:S(2)}) collective-permute-start(f32[101376]{0:T(1024)} %collective-permute-done.3), channel_id=1, source_target_pairs={{1,0},{2,1},{3,2},{4,3},{5,4},{6,5},{7,6},{0,7},{9,8},{10,9},{11,1... | collective-permute-start | bytes 1216520 | tf_op jit(solution)/jit(body)/shard_map/ppermute | solution.py:91
  64.0 10.4 %collective-permute-start.6 = (f32[101376]{0:T(1024)}, f32[101376]{0:T(1024)S(1)}, u32[]{:S(2)}, u32[]{:S(2)}) collective-permute-start(f32[101376]{0:T(1024)} %collective-permute-done.4), channel_id=1, source_target_pairs={{0,1},{1,2},{2,3},{3,4},{4,5},{5,6},{6,7},{7,0},{8,9},{9,10},{10,1... | collective-permute-start | bytes 1216520 | tf_op jit(solution)/jit(body)/shard_map/ppermute | solution.py:87
  88.3 1.4 slice-start
  92.4 4.8 %copy-start.7 = (f32[4,2,8,2,128]{4,3,2,1,0:T(2,128)S(1)}, f32[4,2,8,2,128]{4,3,2,1,0:T(2,128)}, u32[]{:S(2)}) copy-start(f32[4,2,8,2,128]{4,3,2,1,0:T(2,128)} %copy.135) | copy-start | bytes 196612
  92.4 4.8 %copy-start.8 = (f32[4,2,8,2,128]{4,3,2,1,0:T(2,128)S(1)}, f32[4,2,8,2,128]{4,3,2,1,0:T(2,128)}, u32[]{:S(2)}) copy-start(f32[4,2,8,2,128]{4,3,2,1,0:T(2,128)} %copy.137) | copy-start | bytes 196612
  95.7 4.9 %copy-start.1 = (f32[8,2,2,96,128]{4,0,3,2,1:T(8,128)S(1)}, f32[8,2,2,96,128]{4,0,3,2,1:T(8,128)}, u32[]{:S(2)}) copy-start(f32[8,2,2,96,128]{4,0,3,2,1:T(8,128)} %get-tuple-element.42) | copy-start | bytes 4718596
  100.5 0.8 copy-start.4
  101.3 4.7 %copy-start.3 = (f32[8,2,2,64,128]{4,0,3,2,1:T(8,128)S(1)}, f32[8,2,2,64,128]{4,0,3,2,1:T(8,128)}, u32[]{:S(2)}) copy-start(f32[8,2,2,64,128]{4,0,3,2,1:T(8,128)} %get-tuple-element.40) | copy-start | bytes 3145732
  105.9 1.2 copy-start.2
  105.9 1.4 copy-start.5
  105.9 1.4 copy-start.6
  159.8 6.0 %collective-permute-start.9 = (f32[2,2,2,64,128]{4,3,2,1,0:T(8,128)S(1)}, f32[2,2,2,64,128]{4,3,2,1,0:T(8,128)S(1)}, u32[]{:S(2)}, u32[]{:S(2)}) collective-permute-start(f32[2,2,2,64,128]{4,3,2,1,0:T(8,128)S(1)} %get-tuple-element.45), channel_id=1, source_target_pairs={{32,0},{64,32},{96,64},{128,96},{160,128},{192,160},{224,192},{0,2... | collective-permute-start | bytes 786440 | tf_op jit(solution)/jit(body)/shard_map/ppermute | solution.py:126
  161.9 7.0 %collective-permute-start.10 = (f32[2,2,2,64,128]{4,3,2,1,0:T(8,128)S(1)}, f32[2,2,2,64,128]{4,3,2,1,0:T(8,128)S(1)}, u32[]{:S(2)}, u32[]{:S(2)}) collective-permute-start(f32[2,2,2,64,128]{4,3,2,1,0:T(8,128)S(1)} %get-tuple-element.44), channel_id=1, source_target_pairs={{0,32},{32,64},{64,96},{96,128},{128,160},{160,192},{192,224},{224... | collective-permute-start | bytes 786440 | tf_op jit(solution)/jit(body)/shard_map/ppermute | solution.py:127
Sparse Core Ops, SparseCore 0:
  113.2 45.4 reduce-scatter.1

commit v3 on v2

--- a/solution.py
+++ b/solution.py
@@ -91,7 +91,7 @@
             backward = lax.ppermute(backward, "gz", left)
             carried.append(backward)
             offsets.append(step)
-    first_arrival = carried[1][0]
+    first_arrival = carried[-1][0] + carried[-2][0]
 
     stacked = own.reshape(shots, sides, rows, cols, BP, 2, NF)
     stacked = jnp.transpose(stacked, (1, 0, 2, 3, 4, 5, 6))

time: 179 us -> 197 us (1.10)
  local copies, waits for them, and re-layouts: 39.9 us -> 48.5 us
  waiting for transfers between devices: 76.8 us -> 84.3 us
  other arithmetic: 17.7 us -> 19.8 us
    ppermute x4, waiting for transfers between devices: 23.8 us -> 31.7 us  [body(): forward = lax.ppermute(forward, 'gz', right)]
    mul x18, local copies, waits for them, and re-layouts: 10.9 us -> 14.8 us  [combine(): prod_re = -jnp.sum(w * (col_re * row_re - col_im * row_im), axis=(2, 3))]
    all_to_all x1, waiting for transfers between devices: 2.3 us -> 0.01 us  [body(): lax.all_to_all(stacked, 'gy', split_axis=2, concat_axis=2, tiled=True)]
    reduce_sum x3, other arithmetic: 10.9 us -> 13 us  [combine(): prod_re = -jnp.sum(w * (col_re * row_re - col_im * row_im), axis=(2, 3))]
  transfers between devices with their start and end apart: 13 -> 13, of which waited for: 8 -> 9; matrix products, arithmetic and copies ran while one was open for 7% -> 11% of each run, Pallas kernels for 0% -> 0%
where the time goes in v3:
time: 197 us; the launch traced here: 196 us
  waiting for transfers between devices  84.3 us (43%)
  local copies, waits for them, and re-layouts  48.5 us (25%)
  other arithmetic  19.8 us (10%)
  starting transfers between devices  18.9 us (10%)
  between operations  15.2 us (8%)
  matrix products  9.01 us (5%)
    reduce_scatter x1, waiting for transfers between devices, body(): mine = lax.psum_scatter(merged, 'gy', scatter_dimension=0, tiled=False)  46.8 us
    ppermute x4, waiting for transfers between devices, body(): forward = lax.ppermute(forward, 'gz', right)  31.7 us
    mul x18, local copies, waits for them, and re-layouts, combine(): prod_re = -jnp.sum(w * (col_re * row_re - col_im * row_im), axis=(2, 3))  14.8 us
    reduce_sum x3, other arithmetic, combine(): prod_re = -jnp.sum(w * (col_re * row_re - col_im * row_im), axis=(2, 3))  13 us
    another operation x1, local copies, waits for them, and re-layouts, body(): ring = jnp.stack(carried)  9.95 us
    dot_general x1, matrix products, spectrum(): out = jnp.dot(traces.reshape(shots * recv, samples), table, precision=HIGH)  9.01 us
    ppermute x3, starting transfers between devices, body(): backward = lax.ppermute(backward, 'gz', left)  5.45 us
    all_to_all x1, starting transfers between devices, body(): lax.all_to_all(stacked, 'gy', split_axis=2, concat_axis=2, tiled=True)  4.46 us
  transfers between devices with their start and end apart: 13, of which 9 were waited for; matrix products, arithmetic and copies ran while one was open for 11% of the time, Pallas kernels for 0%

profile of v3, /device:TPU:32, one launch (start us, length us, event | category | flops | bytes accessed | tf_op | source)
XLA Modules:
  0.0 195.7 jit_solution(6371630219324164844)
XLA Ops:
  7.6 9.0 %fusion.4 = f32[384,256]{0,1:T(8,128)S(1)} fusion(f32[384,4096]{1,0:T(8,128)} %bitcast.94, f32[4096,128]{1,0:T(8,128)S(1)} %bitcast.93, f32[4096,128]{1,0:T(8,128)S(1)} %bitcast.92), kind=kOutput, calls=%fused_computation.20 | convolution fusion | flops 2416967680 | bytes 10878976 | tf_op jit(solution)/jit(body)/shard_map/dot_general | solution.py:36
  20.4 2.0 %collective-permute-start = (f32[101376]{0:T(1024)S(1)}, f32[101376]{0:T(1024)}, u32[]{:S(2)}, u32[]{:S(2)}) collective-permute-start(f32[101376]{0:T(1024)S(1)} %pad_maximum_fusion), channel_id=1, source_target_pairs={{0,1},{1,2},{2,3},{3,4},{4,5},{5,6},{6,7},{7,0},{8,9},{9,10},{10,1... | collective-permute-start | bytes 1216520 | tf_op jit(solution)/jit(body)/shard_map/ppermute | solution.py:87
  22.5 9.2 %collective-permute-done = f32[101376]{0:T(1024)} collective-permute-done((f32[101376]{0:T(1024)S(1)}, f32[101376]{0:T(1024)}, u32[]{:S(2)}, u32[]{:S(2)}) %collective-permute-start) | collective-permute-done | bytes 405536 | tf_op jit(solution)/jit(body)/shard_map/ppermute | solution.py:87
  31.7 1.9 collective-permute-start.2
  34.9 2.3 %collective-permute-start.3 = (f32[101376]{0:T(1024)}, f32[101376]{0:T(1024)S(1)}, u32[]{:S(2)}, u32[]{:S(2)}) collective-permute-start(f32[101376]{0:T(1024)} %collective-permute-done.1), channel_id=1, source_target_pairs={{1,0},{2,1},{3,2},{4,3},{5,4},{6,5},{7,6},{0,7},{9,8},{10,9},{11,1... | collective-permute-start | bytes 1216520 | tf_op jit(solution)/jit(body)/shard_map/ppermute | solution.py:91
  37.2 7.8 %collective-permute-done.2 = f32[101376]{0:T(1024)} collective-permute-done((f32[101376]{0:T(1024)}, f32[101376]{0:T(1024)}, u32[]{:S(2)}, u32[]{:S(2)}) %collective-permute-start.2) | collective-permute-done | bytes 405536 | tf_op jit(solution)/jit(body)/shard_map/ppermute | solution.py:87
  46.7 3.0 %collective-permute-start.5 = (f32[101376]{0:T(1024)S(1)}, f32[101376]{0:T(1024)S(1)}, u32[]{:S(2)}, u32[]{:S(2)}) collective-permute-start(f32[101376]{0:T(1024)S(1)} %collective-permute-done.3), channel_id=1, source_target_pairs={{1,0},{2,1},{3,2},{4,3},{5,4},{6,5},{7,6},{0,7},{9,8},{10,9},{11,1... | collective-permute-start | bytes 1216520 | tf_op jit(solution)/jit(body)/shard_map/ppermute | solution.py:91
  49.7 6.4 %collective-permute-done.4 = f32[101376]{0:T(1024)S(1)} collective-permute-done((f32[101376]{0:T(1024)}, f32[101376]{0:T(1024)S(1)}, u32[]{:S(2)}, u32[]{:S(2)}) %collective-permute-start.4) | collective-permute-done | bytes 405536 | tf_op jit(solution)/jit(body)/shard_map/ppermute | solution.py:87
  57.9 8.3 %collective-permute-done.6 = f32[101376]{0:T(1024)S(1)} collective-permute-done((f32[101376]{0:T(1024)S(1)}, f32[101376]{0:T(1024)S(1)}, u32[]{:S(2)}, u32[]{:S(2)}) %collective-permute-start.6) | collective-permute-done | bytes 405536 | tf_op jit(solution)/jit(body)/shard_map/ppermute | solution.py:87
  66.9 10.0 %stack.50 = f32[8,101376]{1,0:T(8,128)} concatenate(f32[1,101376]{1,0:T(1,128)S(1)} %bitcast.97, f32[1,101376]{1,0:T(1,128)} %bitcast.10, f32[1,101376]{1,0:T(1,128)} %bitcast.11, f32[1,101376]{1,0:T(1,128)} %bitcast.12, f32[1,101376]{1,0:T(1,128)S(1)} %bitcast.107, f32[1,101376]{1,0:T(1,128)S(1)} %bitcast.108, f32[1,101376]{1,0:T(1,128)} %bitcast.110, f32[1,101376]{1,0:T(1,128)} %bitcast.109), dimensions={0} | concatenate | bytes 6488064 | tf_op jit(solution)/jit(body)/shard_map/stack | solution.py:108
  76.9 2.1 %slice.191 = f32[8,98304]{1,0:T(8,128)S(1)} slice(f32[8,101376]{1,0:T(8,128)} %stack.50), slice={[0:8], [0:98304]} | slice | bytes 6291456 | tf_op jit(solution)/jit(body)/shard_map/slice | solution.py:109
  79.0 1.8 slice_bitcast_fusion.5
  80.8 1.9 slice_bitcast_fusion.1
  82.7 1.6 copy.128
  84.3 1.2 slice.187
  88.1 4.5 %all-to-all-start = ((f32[3,2,4,8,2,2,128]{6,5,4,3,1,0,2:T(2,128)}), f32[3,2,4,8,2,2,128]{6,5,4,3,1,0,2:T(2,128)S(1)}, u32[]{:S(2)}, u32[]{:S(2)}) async-start(f32[3,2,4,8,2,2,128]{6,5,4,3,1,0,2:T(2,128)} %copy.133), calls=%async_computation | async-start | bytes 786432 | tf_op jit(solution)/jit(body)/shard_map/all_to_all | solution.py:99
  94.3 2.5 %copy.136 = f32[8,2,2,64,128]{4,3,2,1,0:T(8,128)} copy(f32[8,2,2,64,128]{4,0,3,2,1:T(8,128)} %get-tuple-element.38) | data formatting | bytes 2097152 | tf_op jit(solution)/jit(body)/shard_map/mul | solution.py:46
  98.0 1.9 copy.141
  99.9 1.4 copy.143
  102.5 1.2 copy.148
  103.6 1.4 select_reduce_fusion
  106.0 3.0 %collective-permute-start.8 = (f32[4,2,8,2,2,128]{5,0,4,3,2,1:T(4,128)}, f32[4,2,8,2,2,128]{5,0,4,3,2,1:T(4,128)}, u32[]{:S(2)}, u32[]{:S(2)}) collective-permute-start(f32[4,2,8,2,2,128]{5,0,4,3,2,1:T(4,128)} %get-tuple-element.47), channel_id=1, source_target_pairs={{32,0},{64,32},{96,64},{128,96},{160,128},{192,160},{224,192},{0,2... | collective-permute-start | bytes 393224 | tf_op jit(solution)/jit(body)/shard_map/ppermute | solution.py:104
  109.0 1.5 slice_bitcast_fusion.17
  112.5 1.5 gather_fusion.3
  114.3 4.4 %multiply_reduce_fusion.5 = (f32[4,2,2,64,128]{4,3,2,1,0:T(8,128)S(1)}, f32[4,2,2,64,128]{4,3,2,1,0:T(8,128)S(1)}) fusion(f32[8,2,2,64,128]{4,3,2,1,0:T(8,128)} %copy.138, f32[4,2,8,2,128]{4,3,2,1,0:T(2,128)S(1)} %copy.137, f32[8,2,2,64,128]{4,3,2,1,0:T(8,128)} %copy.136, f32[4,2,8,2,128]{4,3,2,1,0:T(2,128)S(1)} %copy.135, f32[4,8,2,64]{3,2,0,1:T(2,128)} %get-tuple-element.57), kind=kLoop, calls=%fused_computation.9 | loop fusion | flops 20709376 | bytes 3293184 | tf_op jit(solution)/jit(body)/shard_map/reduce_sum | solution.py:46
  119.0 5.4 %multiply_reduce_fusion.1 = (f32[4,2,2,96,128]{4,3,2,1,0:T(8,128)S(1)}, f32[4,2,2,96,128]{4,3,2,1,0:T(8,128)S(1)}) fusion(f32[8,2,2,96,128]{4,3,2,1,0:T(8,128)S(1)} %copy-done.1, f32[4,2,8,2,128]{4,3,2,1,0:T(2,128)S(1)} %copy.142, f32[8,2,2,96,128]{4,3,2,1,0:T(8,128)S(1)} %copy.141, f32[4,2,8,2,128]{4,3,2,1,0:T(2,128)S(1)} %copy.140, ...), kind=kLoop, calls=%fused_computation.5 | loop fusion | flops 31064064 | bytes 4882432 | tf_op jit(solution)/jit(body)/shard_map/reduce_sum | solution.py:46
  124.8 3.1 %multiply_reduce_fusion.3 = (f32[4,2,2,64,128]{4,3,2,1,0:T(8,128)S(1)}, f32[4,2,2,64,128]{4,3,2,1,0:T(8,128)S(1)}) fusion(f32[8,2,2,64,128]{4,3,2,1,0:T(8,128)S(1)} %copy-done.4, f32[4,2,8,2,128]{4,3,2,1,0:T(2,128)S(1)} %copy.147, f32[8,2,2,64,128]{4,3,2,1,0:T(8,128)S(1)} %copy-done.3, f32[4,2,8,2,128]{4,3,2,1,0:T(2,128)S(1)} %copy.145, ...), kind=kLoop, calls=%fused_computation.7 | loop fusion | flops 20709376 | bytes 3293184 | tf_op jit(solution)/jit(body)/shard_map/reduce_sum | solution.py:46
  128.3 2.1 %copy.149 = f32[4,2,2,2,224,128]{5,4,3,2,1,0:T(8,128)} copy(f32[4,2,2,2,224,128]{5,4,2,1,0,3:T(8,128)S(1)} %maximum_maximum_fusion) | data formatting | bytes 7340032 | tf_op jit(solution)/jit(body)/shard_map/concatenate | solution.py:123
  130.5 46.8 %reduce-scatter.2.cloned.1.call-done = f32[1,2,2,2,224,128]{5,4,3,2,1,0:T(8,128)} async-done(((f32[4,2,2,2,224,128]{5,4,3,2,1,0:T(8,128)}), f32[1,2,2,2,224,128]{5,4,3,2,1,0:T(8,128)}) %reduce-scatter.2.cloned.1.call-update) | async-done | bytes 917520 | tf_op jit(solution)/jit(body)/shard_map/reduce_scatter | solution.py:124
  178.3 2.1 %collective-permute-start.9 = (f32[2,2,2,64,128]{4,3,2,1,0:T(8,128)S(1)}, f32[2,2,2,64,128]{4,3,2,1,0:T(8,128)S(1)}, u32[]{:S(2)}, u32[]{:S(2)}) collective-permute-start(f32[2,2,2,64,128]{4,3,2,1,0:T(8,128)S(1)} %get-tuple-element.45), channel_id=1, source_target_pairs={{32,0},{64,32},{96,64},{128,96},{160,128},{192,160},{224,192},{0,2... | collective-permute-start | bytes 786440 | tf_op jit(solution)/jit(body)/shard_map/ppermute | solution.py:126
  181.4 2.9 %collective-permute-done.9 = f32[2,2,2,64,128]{4,3,2,1,0:T(8,128)S(1)} collective-permute-done((f32[2,2,2,64,128]{4,3,2,1,0:T(8,128)S(1)}, f32[2,2,2,64,128]{4,3,2,1,0:T(8,128)S(1)}, u32[]{:S(2)}, u32[]{:S(2)}) %collective-permute-start.9) | collective-permute-done | bytes 262176 | tf_op jit(solution)/jit(body)/shard_map/ppermute | solution.py:126
  185.3 2.1 %collective-permute-done.10 = f32[2,2,2,64,128]{4,3,2,1,0:T(8,128)S(1)} collective-permute-done((f32[2,2,2,64,128]{4,3,2,1,0:T(8,128)S(1)}, f32[2,2,2,64,128]{4,3,2,1,0:T(8,128)S(1)}, u32[]{:S(2)}, u32[]{:S(2)}) %collective-permute-start.10) | collective-permute-done | bytes 262176 | tf_op jit(solution)/jit(body)/shard_map/ppermute | solution.py:127
  (102 shorter events, 24.2 us)
Async XLA Ops:
  6.5 27.1 %copy-start = (s32[256,3,32,16]{0,3,2,1:T(8,128)S(1)}, s32[256,3,32,16]{0,3,2,1:T(8,128)}, u32[]{:S(2)}) copy-start(s32[256,3,32,16]{0,3,2,1:T(8,128)} %param.12) | copy-start | bytes 4718596
  7.6 10.2 %copy-start.12 = (s32[1,3,32,16]{2,3,1,0:T(8,128)S(1)}, s32[1,3,32,16]{2,3,1,0:T(8,128)}, u32[]{:S(2)}) copy-start(s32[1,3,32,16]{2,3,1,0:T(8,128)} %param.13) | copy-start | bytes 18436
  7.6 10.4 %copy-start.13 = (f32[8,2]{0,1:T(2,128)S(1)}, f32[8,2]{0,1:T(2,128)}, u32[]{:S(2)}) copy-start(f32[8,2]{0,1:T(2,128)} %param.14) | copy-start | bytes 196
  16.8 28.3 %copy-start.14 = (s32[8]{0:T(128)S(1)}, s32[8]{0:T(128)}, u32[]{:S(2)}) copy-start(s32[8]{0:T(128)} %constant.149.clone) | copy-start | bytes 100
  20.4 11.3 %collective-permute-start = (f32[101376]{0:T(1024)S(1)}, f32[101376]{0:T(1024)}, u32[]{:S(2)}, u32[]{:S(2)}) collective-permute-start(f32[101376]{0:T(1024)S(1)} %pad_maximum_fusion), channel_id=1, source_target_pairs={{0,1},{1,2},{2,3},{3,4},{4,5},{5,6},{6,7},{7,0},{8,9},{9,10},{10,1... | collective-permute-start | bytes 1216520 | tf_op jit(solution)/jit(body)/shard_map/ppermute | solution.py:87
  22.4 12.5 %collective-permute-start.1 = (f32[101376]{0:T(1024)S(1)}, f32[101376]{0:T(1024)}, u32[]{:S(2)}, u32[]{:S(2)}) collective-permute-start(f32[101376]{0:T(1024)S(1)} %pad_maximum_fusion), channel_id=1, source_target_pairs={{1,0},{2,1},{3,2},{4,3},{5,4},{6,5},{7,6},{0,7},{9,8},{10,9},{11,1... | collective-permute-start | bytes 1216520 | tf_op jit(solution)/jit(body)/shard_map/ppermute | solution.py:91
  31.7 13.3 %collective-permute-start.2 = (f32[101376]{0:T(1024)}, f32[101376]{0:T(1024)}, u32[]{:S(2)}, u32[]{:S(2)}) collective-permute-start(f32[101376]{0:T(1024)} %collective-permute-done), channel_id=1, source_target_pairs={{0,1},{1,2},{2,3},{3,4},{4,5},{5,6},{6,7},{7,0},{8,9},{9,10},{10,1... | collective-permute-start | bytes 1216520 | tf_op jit(solution)/jit(body)/shard_map/ppermute | solution.py:87
  34.9 11.8 %collective-permute-start.3 = (f32[101376]{0:T(1024)}, f32[101376]{0:T(1024)S(1)}, u32[]{:S(2)}, u32[]{:S(2)}) collective-permute-start(f32[101376]{0:T(1024)} %collective-permute-done.1), channel_id=1, source_target_pairs={{1,0},{2,1},{3,2},{4,3},{5,4},{6,5},{7,6},{0,7},{9,8},{10,9},{11,1... | collective-permute-start | bytes 1216520 | tf_op jit(solution)/jit(body)/shard_map/ppermute | solution.py:91
  45.0 11.1 %collective-permute-start.4 = (f32[101376]{0:T(1024)}, f32[101376]{0:T(1024)S(1)}, u32[]{:S(2)}, u32[]{:S(2)}) collective-permute-start(f32[101376]{0:T(1024)} %collective-permute-done.2), channel_id=1, source_target_pairs={{0,1},{1,2},{2,3},{3,4},{4,5},{5,6},{6,7},{7,0},{8,9},{9,10},{10,1... | collective-permute-start | bytes 1216520 | tf_op jit(solution)/jit(body)/shard_map/ppermute | solution.py:87
  46.7 10.6 %collective-permute-start.5 = (f32[101376]{0:T(1024)S(1)}, f32[101376]{0:T(1024)S(1)}, u32[]{:S(2)}, u32[]{:S(2)}) collective-permute-start(f32[101376]{0:T(1024)S(1)} %collective-permute-done.3), channel_id=1, source_target_pairs={{1,0},{2,1},{3,2},{4,3},{5,4},{6,5},{7,6},{0,7},{9,8},{10,9},{11,1... | collective-permute-start | bytes 1216520 | tf_op jit(solution)/jit(body)/shard_map/ppermute | solution.py:91
  56.1 10.0 %collective-permute-start.6 = (f32[101376]{0:T(1024)S(1)}, f32[101376]{0:T(1024)S(1)}, u32[]{:S(2)}, u32[]{:S(2)}) collective-permute-start(f32[101376]{0:T(1024)S(1)} %collective-permute-done.4), channel_id=1, source_target_pairs={{0,1},{1,2},{2,3},{3,4},{4,5},{5,6},{6,7},{7,0},{8,9},{9,10},{10,1... | collective-permute-start | bytes 1216520 | tf_op jit(solution)/jit(body)/shard_map/ppermute | solution.py:87
  57.3 9.7 %copy-start.9 = (f32[101376]{0:T(1024)}, f32[101376]{0:T(1024)S(1)}, u32[]{:S(2)}) copy-start(f32[101376]{0:T(1024)S(1)} %collective-permute-done.5) | copy-start | bytes 1216516
  66.2 0.7 copy-start.8
  80.8 1.9 slice-start
  88.1 16.9 %all-to-all-start = ((f32[3,2,4,8,2,2,128]{6,5,4,3,1,0,2:T(2,128)}), f32[3,2,4,8,2,2,128]{6,5,4,3,1,0,2:T(2,128)S(1)}, u32[]{:S(2)}, u32[]{:S(2)}) async-start(f32[3,2,4,8,2,2,128]{6,5,4,3,1,0,2:T(2,128)} %copy.133), calls=%async_computation | async-start | bytes 786432 | tf_op jit(solution)/jit(body)/shard_map/all_to_all | solution.py:99
  92.6 84.7 %reduce-scatter.2.cloned.1.call-start = ((), (), s32[]{:S(2)}) async-start(), calls=%async_computation.2 | async-start | bytes 4587520 | tf_op jit(solution)/jit(body)/shard_map/reduce_scatter | solution.py:124
  94.3 5.5 %copy-start.2 = (f32[8,2,2,96,128]{4,0,3,2,1:T(8,128)S(1)}, f32[8,2,2,96,128]{4,0,3,2,1:T(8,128)}, u32[]{:S(2)}) copy-start(f32[8,2,2,96,128]{4,0,3,2,1:T(8,128)} %get-tuple-element.43) | copy-start | bytes 4718596
  98.0 3.3 %copy-start.6 = (f32[8,2,2,64,128]{4,0,3,2,1:T(8,128)S(1)}, f32[8,2,2,64,128]{4,0,3,2,1:T(8,128)}, u32[]{:S(2)}) copy-start(f32[8,2,2,64,128]{4,0,3,2,1:T(8,128)} %get-tuple-element.40) | copy-start | bytes 3145732
  98.0 4.5 %copy-start.5 = (f32[8,2,2,64,128]{4,0,3,2,1:T(8,128)S(1)}, f32[8,2,2,64,128]{4,0,3,2,1:T(8,128)}, u32[]{:S(2)}) copy-start(f32[8,2,2,64,128]{4,0,3,2,1:T(8,128)} %get-tuple-element.39) | copy-start | bytes 3145732
  99.8 3.8 %copy-start.7 = (pred[8,3,4,16,96]{4,3,2,1,0:T(8,128)(4,1)S(1)}, pred[8,3,4,16,96]{4,3,2,1,0:T(8,128)(4,1)}, u32[]{:S(2)}) copy-start(pred[8,3,4,16,96]{4,3,2,1,0:T(8,128)(4,1)} %iota_compare_fusion) | copy-start | bytes 442372
  99.9 3.8 %copy-start.10 = (f32[8,3,4,16,2]{3,4,2,1,0:T(2,128)S(1)}, f32[8,3,4,16,2]{3,4,2,1,0:T(2,128)}, u32[]{:S(2)}) copy-start(f32[8,3,4,16,2]{3,4,2,1,0:T(2,128)} %copy.130) | copy-start | bytes 36868
  106.0 5.8 %collective-permute-start.7 = (f32[4,2,8,2,2,128]{5,0,4,3,2,1:T(4,128)}, f32[4,2,8,2,2,128]{5,0,4,3,2,1:T(4,128)S(1)}, u32[]{:S(2)}, u32[]{:S(2)}) collective-permute-start(f32[4,2,8,2,2,128]{5,0,4,3,2,1:T(4,128)} %get-tuple-element.46), channel_id=1, source_target_pairs={{0,32},{32,64},{64,96},{96,128},{128,160},{160,192},{192,224},{224... | collective-permute-start | bytes 393224 | tf_op jit(solution)/jit(body)/shard_map/ppermute | solution.py:102
  106.0 6.4 %collective-permute-start.8 = (f32[4,2,8,2,2,128]{5,0,4,3,2,1:T(4,128)}, f32[4,2,8,2,2,128]{5,0,4,3,2,1:T(4,128)}, u32[]{:S(2)}, u32[]{:S(2)}) collective-permute-start(f32[4,2,8,2,2,128]{5,0,4,3,2,1:T(4,128)} %get-tuple-element.47), channel_id=1, source_target_pairs={{32,0},{64,32},{96,64},{128,96},{160,128},{192,160},{224,192},{0,2... | collective-permute-start | bytes 393224 | tf_op jit(solution)/jit(body)/shard_map/ppermute | solution.py:104
  114.0 5.0 %copy-start.1 = (f32[8,2,2,96,128]{4,3,2,1,0:T(8,128)S(1)}, f32[8,2,2,96,128]{4,3,2,1,0:T(8,128)}, u32[]{:S(2)}) copy-start(f32[8,2,2,96,128]{4,3,2,1,0:T(8,128)} %copy.143) | copy-start | bytes 4718596
  119.0 5.7 %copy-start.3 = (f32[8,2,2,64,128]{4,3,2,1,0:T(8,128)S(1)}, f32[8,2,2,64,128]{4,3,2,1,0:T(8,128)}, u32[]{:S(2)}) copy-start(f32[8,2,2,64,128]{4,3,2,1,0:T(8,128)} %copy.146) | copy-start | bytes 3145732
  119.0 5.7 %copy-start.4 = (f32[8,2,2,64,128]{4,3,2,1,0:T(8,128)S(1)}, f32[8,2,2,64,128]{4,3,2,1,0:T(8,128)}, u32[]{:S(2)}) copy-start(f32[8,2,2,64,128]{4,3,2,1,0:T(8,128)} %copy.148) | copy-start | bytes 3145732
  119.0 5.7 %copy-start.11 = (f32[4,8,2,64]{3,2,0,1:T(2,128)S(1)}, f32[4,8,2,64]{3,2,0,1:T(2,128)}, u32[]{:S(2)}) copy-start(f32[4,8,2,64]{3,2,0,1:T(2,128)} %get-tuple-element.58) | copy-start | bytes 49156
  178.3 6.0 %collective-permute-start.9 = (f32[2,2,2,64,128]{4,3,2,1,0:T(8,128)S(1)}, f32[2,2,2,64,128]{4,3,2,1,0:T(8,128)S(1)}, u32[]{:S(2)}, u32[]{:S(2)}) collective-permute-start(f32[2,2,2,64,128]{4,3,2,1,0:T(8,128)S(1)} %get-tuple-element.45), channel_id=1, source_target_pairs={{32,0},{64,32},{96,64},{128,96},{160,128},{192,160},{224,192},{0,2... | collective-permute-start | bytes 786440 | tf_op jit(solution)/jit(body)/shard_map/ppermute | solution.py:126
  180.4 7.0 %collective-permute-start.10 = (f32[2,2,2,64,128]{4,3,2,1,0:T(8,128)S(1)}, f32[2,2,2,64,128]{4,3,2,1,0:T(8,128)S(1)}, u32[]{:S(2)}, u32[]{:S(2)}) collective-permute-start(f32[2,2,2,64,128]{4,3,2,1,0:T(8,128)S(1)} %get-tuple-element.44), channel_id=1, source_target_pairs={{0,32},{32,64},{64,96},{96,128},{128,160},{160,192},{192,224},{224... | collective-permute-start | bytes 786440 | tf_op jit(solution)/jit(body)/shard_map/ppermute | solution.py:127
Sparse Core Ops, SparseCore 0:
  130.6 46.6 reduce-scatter.1

commit v4 on v1

--- a/solution.py
+++ b/solution.py
@@ -87,25 +87,31 @@
     ]
 
     lanes = jnp.transpose(own, (0, 2, 3, 1, 4))
-    spec_size = lanes.size
-    payload = jnp.concatenate([lanes.reshape(-1), src_weight.reshape(-1)])
+    spec_rows = lanes.size // NF
+    payload = jnp.concatenate([lanes.reshape(spec_rows, NF), src_weight.reshape(-1, NF)], axis=0)
     carried = [payload]
     offsets = [0]
     forward = payload
     backward = payload
+    split = payload.shape[0] // 16 * 8
     for step in range(1, cols // 2 + 1):
+        if 2 * step == cols:
+            head = lax.ppermute(forward[:split], "gz", right)
+            tail = lax.ppermute(backward[split:], "gz", left)
+            carried.append(jnp.concatenate([head, tail], axis=0))
+            offsets.append(step)
+            break
         forward = lax.ppermute(forward, "gz", right)
         carried.append(forward)
         offsets.append(-step)
-        if 2 * step < cols:
-            backward = lax.ppermute(backward, "gz", left)
-            carried.append(backward)
-            offsets.append(step)
+        backward = lax.ppermute(backward, "gz", left)
+        carried.append(backward)
+        offsets.append(step)
     sources = (my_col + jnp.asarray(offsets, dtype=jnp.int32)) % cols
     ring = jnp.stack(carried)
-    gathered = ring[:, :spec_size].reshape((len(carried),) + lanes.shape)
+    gathered = ring[:, :spec_rows].reshape((len(carried),) + lanes.shape)
     weights = lax.dynamic_index_in_dim(
-        ring[:, spec_size:].reshape((len(carried),) + src_weight.shape), my_col, 3, False
+        ring[:, spec_rows:].reshape((len(carried),) + src_weight.shape), my_col, 3, False
     )
     slots = jnp.take(slot_table, sources, axis=0)
     hit = slots[..., None] == jnp.arange(blocks, dtype=jnp.int32)

time: 170 us -> 166 us (0.976)
  local copies, waits for them, and re-layouts: 35.4 us -> 31.8 us
    ppermute x4 -> x3, waiting for transfers between devices: 13.6 us -> 0.01 us  [body(): forward = lax.ppermute(forward, 'gz', right)]
    another operation x1 -> x0, local copies, waits for them, and re-layouts: 9.89 us -> none  [body(): ring = jnp.stack(carried)]
    unnamed x19 -> x29, local copies, waits for them, and re-layouts: 2.16 us -> 8.2 us
    ppermute x0 -> x2, waiting for transfers between devices: none -> 4.34 us  [the longest x1 4.34 us: body(): head = lax.ppermute(forward[:split], 'gz', right)]
    ppermute x3, waiting for transfers between devices: 4.09 us -> 8.02 us  [body(): backward = lax.ppermute(backward, 'gz', left)]
    all_to_all x1, waiting for transfers between devices: 2.06 us -> 5.25 us  [body(): lax.all_to_all(stacked, 'gy', split_axis=2, concat_axis=2, tiled=True)]
    ppermute x0 -> x2, starting transfers between devices: none -> 2.85 us  [the longest x1 1.56 us: body(): head = lax.ppermute(forward[:split], 'gz', right)]
    ppermute x3, starting transfers between devices: 6.62 us -> 3.85 us  [body(): backward = lax.ppermute(backward, 'gz', left)]
  transfers between devices with their start and end apart: 14 -> 15, of which waited for: 9 -> 6; matrix products, arithmetic and copies ran while one was open for 12% -> 17% of each run, Pallas kernels for 0% -> 0%
where the time goes in v4:
time: 166 us; the launch traced here: 165 us
  waiting for transfers between devices  70.5 us (42%)
  local copies, waits for them, and re-layouts  31.8 us (19%)
  starting transfers between devices  21.2 us (13%)
  other arithmetic  18.9 us (11%)
  between operations  13.9 us (8%)
  matrix products  9.01 us (5%)
    reduce_scatter x1, waiting for transfers between devices, body(): lax.psum_scatter(side_part(1), 'gy', scatter_dimension=0, tiled=False)  27.4 us
    reduce_scatter x1, waiting for transfers between devices, body(): outer = lax.psum_scatter(outer, 'gy', scatter_dimension=0, tiled=False)  25.4 us
    reduce_sum x3, other arithmetic, combine(): prod_re = -jnp.sum(w * (col_re * row_re - col_im * row_im), axis=(2, 3))  10.8 us
    dot_general x1, matrix products, spectrum(): out = jnp.dot(traces.reshape(shots * recv, samples), table, precision=HIGH)  9.01 us
    unnamed x29, local copies, waits for them, and re-layouts  8.2 us
    ppermute x3, waiting for transfers between devices, body(): backward = lax.ppermute(backward, 'gz', left)  8.02 us
    mul x12, local copies, waits for them, and re-layouts, combine(): prod_re = -jnp.sum(w * (col_re * row_re - col_im * row_im), axis=(2, 3))  7.49 us
    all_to_all x1, waiting for transfers between devices, body(): lax.all_to_all(stacked, 'gy', split_axis=2, concat_axis=2, tiled=True)  5.25 us
  transfers between devices with their start and end apart: 15, of which 6 were waited for; matrix products, arithmetic and copies ran while one was open for 17% of the time, Pallas kernels for 0%

profile of v4, /device:TPU:32, one launch (start us, length us, event | category | flops | bytes accessed | tf_op | source)
XLA Modules:
  0.0 165.3 jit_solution(1612299797381386777)
XLA Ops:
  7.6 9.0 %fusion.4 = f32[384,256]{0,1:T(8,128)S(1)} fusion(f32[384,4096]{1,0:T(8,128)} %bitcast.110, f32[4096,128]{1,0:T(8,128)S(1)} %bitcast.109, f32[4096,128]{1,0:T(8,128)S(1)} %bitcast.108), kind=kOutput, calls=%fused_computation.21 | convolution fusion | flops 2416967680 | bytes 10878976 | tf_op jit(solution)/jit(body)/shard_map/dot_general | solution.py:36
  19.4 1.9 %collective-permute-start = (f32[792,128]{1,0:T(8,128)}, f32[792,128]{1,0:T(8,128)}, u32[]{:S(2)}, u32[]{:S(2)}) collective-permute-start(f32[792,128]{1,0:T(8,128)} %pad_maximum_fusion.1), channel_id=1, source_target_pairs={{0,1},{1,2},{2,3},{3,4},{4,5},{5,6},{6,7},{7,0},{8,9},{9,10},{10,1... | collective-permute-start | bytes 1216520 | tf_op jit(solution)/jit(body)/shard_map/ppermute | solution.py:104
  22.5 4.5 %all-to-all-start = ((f32[3,2,4,8,2,2,128]{6,5,4,3,1,0,2:T(2,128)}), f32[3,2,4,8,2,2,128]{6,5,4,3,1,0,2:T(2,128)S(1)}, u32[]{:S(2)}, u32[]{:S(2)}) async-start(f32[3,2,4,8,2,2,128]{6,5,4,3,1,0,2:T(2,128)} %copy.104), calls=%async_computation | async-start | bytes 786432 | tf_op jit(solution)/jit(body)/shard_map/all_to_all | solution.py:81
  29.4 5.2 %all-to-all-done = f32[3,2,4,8,2,2,128]{6,5,4,3,1,0,2:T(2,128)S(1)} async-done(((f32[3,2,4,8,2,2,128]{6,5,4,3,1,0,2:T(2,128)}), f32[3,2,4,8,2,2,128]{6,5,4,3,1,0,2:T(2,128)S(1)}, u32[]{:S(2)}, u32[]{:S(2)}) %all-to-all-start) | async-done | bytes 393248 | tf_op jit(solution)/jit(body)/shard_map/all_to_all | solution.py:81
  35.0 2.9 %collective-permute-start.9 = (f32[4,2,8,2,2,128]{5,0,4,3,2,1:T(4,128)S(1)}, f32[4,2,8,2,2,128]{5,0,4,3,2,1:T(4,128)S(1)}, u32[]{:S(2)}, u32[]{:S(2)}) collective-permute-start(f32[4,2,8,2,2,128]{5,0,4,3,2,1:T(4,128)S(1)} %get-tuple-element.47), channel_id=1, source_target_pairs={{32,0},{64,32},{96,64},{128,96},{160,128},{192,160},{224,192},{0,2... | collective-permute-start | bytes 393224 | tf_op jit(solution)/jit(body)/shard_map/ppermute | solution.py:86
  38.6 2.0 %collective-permute-start.2 = (f32[792,128]{1,0:T(8,128)}, f32[792,128]{1,0:T(8,128)S(1)}, u32[]{:S(2)}, u32[]{:S(2)}) collective-permute-start(f32[792,128]{1,0:T(8,128)} %collective-permute-done), channel_id=1, source_target_pairs={{0,1},{1,2},{2,3},{3,4},{4,5},{5,6},{6,7},{7,0},{8,9},{9,10},{10,1... | collective-permute-start | bytes 1216520 | tf_op jit(solution)/jit(body)/shard_map/ppermute | solution.py:104
  40.6 1.8 %bitcast_dynamic-update-slice_fusion.5 = f32[8,792,128]{2,1,0:T(8,128)} fusion(f32[8,792,128]{2,1,0:T(8,128)} %bitcast_dynamic-update-slice_fusion.6, f32[792,128]{1,0:T(8,128)} %collective-permute-done), kind=kLoop, calls=%fused_computation.42 | loop fusion | bytes 811008
  42.4 2.1 %collective-permute-start.3 = (f32[792,128]{1,0:T(8,128)}, f32[792,128]{1,0:T(8,128)S(1)}, u32[]{:S(2)}, u32[]{:S(2)}) collective-permute-start(f32[792,128]{1,0:T(8,128)} %collective-permute-done.1), channel_id=1, source_target_pairs={{1,0},{2,1},{3,2},{4,3},{5,4},{6,5},{7,6},{0,7},{9,8},{10,9},{11,1... | collective-permute-start | bytes 1216520 | tf_op jit(solution)/jit(body)/shard_map/ppermute | solution.py:107
  44.5 1.8 %bitcast_dynamic-update-slice_fusion.4 = f32[8,792,128]{2,1,0:T(8,128)} fusion(f32[8,792,128]{2,1,0:T(8,128)} %bitcast_dynamic-update-slice_fusion.5, f32[792,128]{1,0:T(8,128)} %collective-permute-done.1), kind=kLoop, calls=%fused_computation.41 | loop fusion | bytes 811008
  47.6 1.4 select_bitcast_fusion.1
  51.8 1.0 collective-permute-start.4
  53.6 1.6 collective-permute-start.5
  56.8 7.1 %collective-permute-done.5 = f32[792,128]{1,0:T(8,128)S(1)} collective-permute-done((f32[792,128]{1,0:T(8,128)S(1)}, f32[792,128]{1,0:T(8,128)S(1)}, u32[]{:S(2)}, u32[]{:S(2)}) %collective-permute-start.5) | collective-permute-done | bytes 405536 | tf_op jit(solution)/jit(body)/shard_map/ppermute | solution.py:107
  64.0 1.3 collective-permute-start.7
  65.3 1.6 collective-permute-start.6
  68.4 4.3 %collective-permute-done.6 = f32[392,128]{1,0:T(8,128)S(1)} collective-permute-done((f32[392,128]{1,0:T(8,128)S(1)}, f32[392,128]{1,0:T(8,128)S(1)}, u32[]{:S(2)}, u32[]{:S(2)}) %collective-permute-start.6) | collective-permute-done | bytes 200736 | tf_op jit(solution)/jit(body)/shard_map/ppermute | solution.py:99
  73.5 0.9 slice.182
  74.4 3.8 %slice.186 = f32[8,768,128]{2,1,0:T(8,128)} slice(f32[8,792,128]{2,1,0:T(8,128)} %fusion.7), slice={[0:8], [0:768], [0:128]} | slice | bytes 6291456 | tf_op jit(solution)/jit(body)/shard_map/slice | solution.py:112
  79.8 2.5 %slice_bitcast_fusion.5 = (f32[8,2,2,64,128]{4,3,2,1,0:T(8,128)S(1)}, f32[8,2,2,64,128]{4,3,2,1,0:T(8,128)S(1)}, f32[8,2,2,64,128]{4,3,2,1,0:T(8,128)S(1)}, f32[8,2,2,64,128]{4,3,2,1,0:T(8,128)S(1)}) fusion(f32[8,2,2,2,96,128]{5,4,3,2,1,0:T(8,128)} %bitcast.106), kind=kLoop, calls=%fused_computation.25 | loop fusion | bytes 8388608 | tf_op jit(solution)/jit(body)/shard_map/mul | solution.py:46
  82.3 3.1 %multiply_reduce_fusion.5 = (f32[4,2,2,64,128]{4,3,2,1,0:T(8,128)S(1)}, f32[4,2,2,64,128]{4,3,2,1,0:T(8,128)S(1)}) fusion(f32[8,2,2,64,128]{4,3,2,1,0:T(8,128)S(1)} %get-tuple-element.41, f32[4,2,8,2,128]{4,3,2,1,0:T(2,128)S(1)} %copy-done.5, f32[8,2,2,64,128]{4,3,2,1,0:T(8,128)S(1)} %get-tuple-element.38, f32[4,2,8,2,128]{4,3,2,1,0:T(2,128)S(1)} %copy-done.4, ...), kind=kLoop, calls=%fused_computation.9 | loop fusion | flops 20709376 | bytes 3293184 | tf_op jit(solution)/jit(body)/shard_map/reduce_sum | solution.py:46
  85.6 3.1 %multiply_reduce_fusion.3 = (f32[4,2,2,64,128]{4,3,2,1,0:T(8,128)S(1)}, f32[4,2,2,64,128]{4,3,2,1,0:T(8,128)S(1)}) fusion(f32[8,2,2,64,128]{4,3,2,1,0:T(8,128)S(1)} %get-tuple-element.39, f32[4,2,8,2,128]{4,3,2,1,0:T(2,128)S(1)} %copy-done.3, f32[8,2,2,64,128]{4,3,2,1,0:T(8,128)S(1)} %get-tuple-element.40, f32[4,2,8,2,128]{4,3,2,1,0:T(2,128)S(1)} %copy-done.2, ...), kind=kLoop, calls=%fused_computation.7 | loop fusion | flops 20709376 | bytes 3293184 | tf_op jit(solution)/jit(body)/shard_map/reduce_sum | solution.py:46
  89.1 1.5 copy.115
  90.8 2.1 %slice_bitcast_fusion.1 = (f32[8,2,2,96,128]{4,3,2,1,0:T(8,128)S(1)}, f32[8,2,2,96,128]{4,3,2,1,0:T(8,128)S(1)}) fusion(f32[8,2,2,2,96,128]{5,4,3,2,1,0:T(8,128)} %bitcast.107), kind=kLoop, calls=%fused_computation.18 | loop fusion | bytes 6291456 | tf_op jit(solution)/jit(body)/shard_map/mul | solution.py:46
  92.9 4.5 %multiply_reduce_fusion.1 = (f32[4,2,2,96,128]{4,3,2,1,0:T(8,128)S(1)}, f32[4,2,2,96,128]{4,3,2,1,0:T(8,128)S(1)}) fusion(f32[8,2,2,96,128]{4,3,2,1,0:T(8,128)S(1)} %get-tuple-element.43, f32[4,2,8,2,128]{4,3,2,1,0:T(2,128)S(1)} %copy.107, f32[8,2,2,96,128]{4,3,2,1,0:T(8,128)S(1)} %get-tuple-element.42, f32[4,2,8,2,128]{4,3,2,1,0:T(2,128)S(1)} %copy.106, ...), kind=kLoop, calls=%fused_computation.5 | loop fusion | flops 31064064 | bytes 4882432 | tf_op jit(solution)/jit(body)/shard_map/reduce_sum | solution.py:46
  97.7 1.3 copy.108
  99.0 25.4 %reduce-scatter.5.cloned.1.call-done = f32[1,2,2,2,128,128]{5,4,3,2,1,0:T(8,128)} async-done(((f32[4,2,2,2,128,128]{5,4,3,2,1,0:T(8,128)}), f32[1,2,2,2,128,128]{5,4,3,2,1,0:T(8,128)}) %reduce-scatter.5.cloned.1.call-update) | async-done | bytes 524304 | tf_op jit(solution)/jit(body)/shard_map/reduce_scatter | solution.py:127
  124.4 1.1 fusion.27
  125.5 2.1 %collective-permute-start.10 = (f32[2,2,2,64,128]{4,3,2,1,0:T(8,128)S(1)}, f32[2,2,2,64,128]{4,3,2,1,0:T(8,128)S(1)}, u32[]{:S(2)}, u32[]{:S(2)}) collective-permute-start(f32[2,2,2,64,128]{4,3,2,1,0:T(8,128)S(1)} %get-tuple-element.45), channel_id=1, source_target_pairs={{32,0},{64,32},{96,64},{128,96},{160,128},{192,160},{224,192},{0,2... | collective-permute-start | bytes 786440 | tf_op jit(solution)/jit(body)/shard_map/ppermute | solution.py:129
  127.6 27.4 %reduce-scatter.3.cloned.1.call-done = f32[1,2,2,2,96,128]{5,4,3,2,1,0:T(8,128)} async-done(((f32[4,2,2,2,96,128]{5,4,3,2,1,0:T(8,128)}), f32[1,2,2,2,96,128]{5,4,3,2,1,0:T(8,128)}) %reduce-scatter.3.cloned.1.call-update) | async-done | bytes 393232 | tf_op jit(solution)/jit(body)/shard_map/reduce_scatter | solution.py:131
  155.0 1.0 copy.136
  156.0 1.0 fusion.10
  157.4 1.1 copy.117
  (97 shorter events, 19.7 us)
Async XLA Ops:
  6.5 20.5 %copy-start = (s32[256,3,32,16]{0,3,2,1:T(8,128)S(1)}, s32[256,3,32,16]{0,3,2,1:T(8,128)}, u32[]{:S(2)}) copy-start(s32[256,3,32,16]{0,3,2,1:T(8,128)} %param.12) | copy-start | bytes 4718596
  7.6 9.5 %copy-start.6 = (s32[1,3,32,16]{2,3,1,0:T(8,128)S(1)}, s32[1,3,32,16]{2,3,1,0:T(8,128)}, u32[]{:S(2)}) copy-start(s32[1,3,32,16]{2,3,1,0:T(8,128)} %param.13) | copy-start | bytes 18436
  7.6 9.6 %copy-start.8 = (f32[8,2]{0,1:T(2,128)S(1)}, f32[8,2]{0,1:T(2,128)}, u32[]{:S(2)}) copy-start(f32[8,2]{0,1:T(2,128)} %param.14) | copy-start | bytes 196
  18.2 9.3 %copy-start.9 = (s32[8]{0:T(128)S(1)}, s32[8]{0:T(128)}, u32[]{:S(2)}) copy-start(s32[8]{0:T(128)} %constant.148.clone) | copy-start | bytes 100
  19.4 19.2 %collective-permute-start = (f32[792,128]{1,0:T(8,128)}, f32[792,128]{1,0:T(8,128)}, u32[]{:S(2)}, u32[]{:S(2)}) collective-permute-start(f32[792,128]{1,0:T(8,128)} %pad_maximum_fusion.1), channel_id=1, source_target_pairs={{0,1},{1,2},{2,3},{3,4},{4,5},{5,6},{6,7},{7,0},{8,9},{9,10},{10,1... | collective-permute-start | bytes 1216520 | tf_op jit(solution)/jit(body)/shard_map/ppermute | solution.py:104
  21.3 21.1 %collective-permute-start.1 = (f32[792,128]{1,0:T(8,128)}, f32[792,128]{1,0:T(8,128)}, u32[]{:S(2)}, u32[]{:S(2)}) collective-permute-start(f32[792,128]{1,0:T(8,128)} %pad_maximum_fusion.1), channel_id=1, source_target_pairs={{1,0},{2,1},{3,2},{4,3},{5,4},{6,5},{7,6},{0,7},{9,8},{10,9},{11,1... | collective-permute-start | bytes 1216520 | tf_op jit(solution)/jit(body)/shard_map/ppermute | solution.py:107
  22.5 12.2 %all-to-all-start = ((f32[3,2,4,8,2,2,128]{6,5,4,3,1,0,2:T(2,128)}), f32[3,2,4,8,2,2,128]{6,5,4,3,1,0,2:T(2,128)S(1)}, u32[]{:S(2)}, u32[]{:S(2)}) async-start(f32[3,2,4,8,2,2,128]{6,5,4,3,1,0,2:T(2,128)} %copy.104), calls=%async_computation | async-start | bytes 786432 | tf_op jit(solution)/jit(body)/shard_map/all_to_all | solution.py:81
  27.0 97.5 %reduce-scatter.5.cloned.1.call-start = ((), (), s32[]{:S(2)}) async-start(), calls=%async_computation.4 | async-start | bytes 2621440 | tf_op jit(solution)/jit(body)/shard_map/reduce_scatter | solution.py:127
  27.6 7.4 %copy-start.7 = (pred[8]{0:T(512)(128)(4,1)}, pred[8]{0:T(512)(128)(4,1)S(1)}, u32[]{:S(2)}) copy-start(pred[8]{0:T(512)(128)(4,1)S(1)} %get-tuple-element.36) | copy-start | bytes 28
  35.0 11.4 %collective-permute-start.8 = (f32[4,2,8,2,2,128]{5,0,4,3,2,1:T(4,128)S(1)}, f32[4,2,8,2,2,128]{5,0,4,3,2,1:T(4,128)S(1)}, u32[]{:S(2)}, u32[]{:S(2)}) collective-permute-start(f32[4,2,8,2,2,128]{5,0,4,3,2,1:T(4,128)S(1)} %get-tuple-element.46), channel_id=1, source_target_pairs={{0,32},{32,64},{64,96},{96,128},{128,160},{160,192},{192,224},{224... | collective-permute-start | bytes 393224 | tf_op jit(solution)/jit(body)/shard_map/ppermute | solution.py:84
  35.0 12.0 %collective-permute-start.9 = (f32[4,2,8,2,2,128]{5,0,4,3,2,1:T(4,128)S(1)}, f32[4,2,8,2,2,128]{5,0,4,3,2,1:T(4,128)S(1)}, u32[]{:S(2)}, u32[]{:S(2)}) collective-permute-start(f32[4,2,8,2,2,128]{5,0,4,3,2,1:T(4,128)S(1)} %get-tuple-element.47), channel_id=1, source_target_pairs={{32,0},{64,32},{96,64},{128,96},{160,128},{192,160},{224,192},{0,2... | collective-permute-start | bytes 393224 | tf_op jit(solution)/jit(body)/shard_map/ppermute | solution.py:86
  38.6 13.2 %collective-permute-start.2 = (f32[792,128]{1,0:T(8,128)}, f32[792,128]{1,0:T(8,128)S(1)}, u32[]{:S(2)}, u32[]{:S(2)}) collective-permute-start(f32[792,128]{1,0:T(8,128)} %collective-permute-done), channel_id=1, source_target_pairs={{0,1},{1,2},{2,3},{3,4},{4,5},{5,6},{6,7},{7,0},{8,9},{9,10},{10,1... | collective-permute-start | bytes 1216520 | tf_op jit(solution)/jit(body)/shard_map/ppermute | solution.py:104
  42.4 11.3 %collective-permute-start.3 = (f32[792,128]{1,0:T(8,128)}, f32[792,128]{1,0:T(8,128)S(1)}, u32[]{:S(2)}, u32[]{:S(2)}) collective-permute-start(f32[792,128]{1,0:T(8,128)} %collective-permute-done.1), channel_id=1, source_target_pairs={{1,0},{2,1},{3,2},{4,3},{5,4},{6,5},{7,6},{0,7},{9,8},{10,9},{11,1... | collective-permute-start | bytes 1216520 | tf_op jit(solution)/jit(body)/shard_map/ppermute | solution.py:107
  51.8 13.5 %collective-permute-start.4 = (f32[792,128]{1,0:T(8,128)S(1)}, f32[792,128]{1,0:T(8,128)S(1)}, u32[]{:S(2)}, u32[]{:S(2)}) collective-permute-start(f32[792,128]{1,0:T(8,128)S(1)} %collective-permute-done.2), channel_id=1, source_target_pairs={{0,1},{1,2},{2,3},{3,4},{4,5},{5,6},{6,7},{7,0},{8,9},{9,10},{10,1... | collective-permute-start | bytes 1216520 | tf_op jit(solution)/jit(body)/shard_map/ppermute | solution.py:104
  53.6 10.3 %collective-permute-start.5 = (f32[792,128]{1,0:T(8,128)S(1)}, f32[792,128]{1,0:T(8,128)S(1)}, u32[]{:S(2)}, u32[]{:S(2)}) collective-permute-start(f32[792,128]{1,0:T(8,128)S(1)} %collective-permute-done.3), channel_id=1, source_target_pairs={{1,0},{2,1},{3,2},{4,3},{5,4},{6,5},{7,6},{0,7},{9,8},{10,9},{11,1... | collective-permute-start | bytes 1216520 | tf_op jit(solution)/jit(body)/shard_map/ppermute | solution.py:107
  64.0 8.8 %collective-permute-start.7 = (f32[400,128]{1,0:T(8,128)S(1)}, f32[400,128]{1,0:T(8,128)S(1)}, u32[]{:S(2)}, u32[]{:S(2)}) collective-permute-start(f32[400,128]{1,0:T(8,128)S(1)} %slice.181), channel_id=1, source_target_pairs={{1,0},{2,1},{3,2},{4,3},{5,4},{6,5},{7,6},{0,7},{9,8},{10,9},{11,1... | collective-permute-start | bytes 614408 | tf_op jit(solution)/jit(body)/shard_map/ppermute | solution.py:100
  65.3 7.5 %collective-permute-start.6 = (f32[392,128]{1,0:T(8,128)S(1)}, f32[392,128]{1,0:T(8,128)S(1)}, u32[]{:S(2)}, u32[]{:S(2)}) collective-permute-start(f32[392,128]{1,0:T(8,128)S(1)} %slice.180), channel_id=1, source_target_pairs={{0,1},{1,2},{2,3},{3,4},{4,5},{5,6},{6,7},{7,0},{8,9},{9,10},{10,1... | collective-permute-start | bytes 602120 | tf_op jit(solution)/jit(body)/shard_map/ppermute | solution.py:99
  79.7 2.6 %copy-start.4 = (f32[4,2,8,2,128]{4,3,2,1,0:T(2,128)S(1)}, f32[4,2,8,2,128]{4,3,2,1,0:T(2,128)}, u32[]{:S(2)}) copy-start(f32[4,2,8,2,128]{4,3,2,1,0:T(2,128)} %copy.110) | copy-start | bytes 196612
  79.7 2.6 %copy-start.5 = (f32[4,2,8,2,128]{4,3,2,1,0:T(2,128)S(1)}, f32[4,2,8,2,128]{4,3,2,1,0:T(2,128)}, u32[]{:S(2)}) copy-start(f32[4,2,8,2,128]{4,3,2,1,0:T(2,128)} %copy.111) | copy-start | bytes 196612
  82.3 3.3 %copy-start.2 = (f32[4,2,8,2,128]{4,3,2,1,0:T(2,128)S(1)}, f32[4,2,8,2,128]{4,3,2,1,0:T(2,128)}, u32[]{:S(2)}) copy-start(f32[4,2,8,2,128]{4,3,2,1,0:T(2,128)} %copy.113) | copy-start | bytes 196612
  82.3 3.3 %copy-start.3 = (f32[4,2,8,2,128]{4,3,2,1,0:T(2,128)S(1)}, f32[4,2,8,2,128]{4,3,2,1,0:T(2,128)}, u32[]{:S(2)}) copy-start(f32[4,2,8,2,128]{4,3,2,1,0:T(2,128)} %copy.114) | copy-start | bytes 196612
  89.1 1.6 copy-start.1
  90.6 64.4 %reduce-scatter.3.cloned.1.call-start = ((), (), s32[]{:S(2)}) async-start(), calls=%async_computation.3 | async-start | bytes 1966080 | tf_op jit(solution)/jit(body)/shard_map/reduce_scatter | solution.py:131
  125.5 30.5 %collective-permute-start.10 = (f32[2,2,2,64,128]{4,3,2,1,0:T(8,128)S(1)}, f32[2,2,2,64,128]{4,3,2,1,0:T(8,128)S(1)}, u32[]{:S(2)}, u32[]{:S(2)}) collective-permute-start(f32[2,2,2,64,128]{4,3,2,1,0:T(8,128)S(1)} %get-tuple-element.45), channel_id=1, source_target_pairs={{32,0},{64,32},{96,64},{128,96},{160,128},{192,160},{224,192},{0,2... | collective-permute-start | bytes 786440 | tf_op jit(solution)/jit(body)/shard_map/ppermute | solution.py:129
  127.6 29.4 %collective-permute-start.11 = (f32[2,2,2,64,128]{4,3,2,1,0:T(8,128)S(1)}, f32[2,2,2,64,128]{4,3,2,1,0:T(8,128)S(1)}, u32[]{:S(2)}, u32[]{:S(2)}) collective-permute-start(f32[2,2,2,64,128]{4,3,2,1,0:T(8,128)S(1)} %get-tuple-element.44), channel_id=1, source_target_pairs={{0,32},{32,64},{64,96},{96,128},{128,160},{160,192},{192,224},{224... | collective-permute-start | bytes 786440 | tf_op jit(solution)/jit(body)/shard_map/ppermute | solution.py:130
Sparse Core Ops, SparseCore 0:
  90.7 33.6 reduce-scatter.4
  127.0 27.9 reduce-scatter.2

commit v5 on v4

--- a/solution.py
+++ b/solution.py
@@ -123,12 +123,12 @@
         cols_s = jnp.take(side_cols[s], sources, axis=2)
         return combine(cols_s, dense[s, :, :, :, lo:hi], gathered[:, :, :, :, lo:hi])
 
-    outer = jnp.concatenate([side_part(0), side_part(2)], axis=4)
-    outer = lax.psum_scatter(outer, "gy", scatter_dimension=0, tiled=False)
-    first = 2 * width
-    from_up = lax.ppermute(outer[:, :, :, :first], "line", down)
-    from_down = lax.ppermute(outer[:, :, :, first:], "line", up)
-    result = lax.psum_scatter(side_part(1), "gy", scatter_dimension=0, tiled=False)
+    merged = jnp.concatenate([side_part(0), side_part(1), side_part(2)], axis=4)
+    mine = lax.psum_scatter(merged, "gy", scatter_dimension=0, tiled=False)
+    first, middle = 2 * width, 2 * width + blocks
+    from_up = lax.ppermute(mine[:, :, :, :first], "line", down)
+    from_down = lax.ppermute(mine[:, :, :, middle:], "line", up)
+    result = mine[:, :, :, first:middle]
     result = result.at[:, :, :, width:].add(from_up)
     result = result.at[:, :, :, : 2 * width].add(from_down)
     result = jnp.transpose(result, (0, 3, 1, 2, 4))

time: 166 us -> 166 us (level)
  waiting for transfers between devices: 70.5 us -> 67.7 us
  other arithmetic: 18.9 us -> 20.6 us
    reduce_scatter x2 -> x1, waiting for transfers between devices: 52.8 us -> 46.3 us  [body(): mine = lax.psum_scatter(merged, 'gy', scatter_dimension=0, tiled=False)]
    ppermute x2, waiting for transfers between devices: 0.01 us -> 4.98 us  [the longest x1 2.86 us: body(): from_up = lax.ppermute(mine[:, :, :, :first], 'line', down)]
    slice x1, local copies, waits for them, and re-layouts: 3.8 us -> 2.11 us  [body(): gathered = ring[:, :spec_rows].reshape((len(carried),) + lanes.shape)]
    unnamed x29 -> x32, local copies, waits for them, and re-layouts: 8.2 us -> 7.2 us
  transfers between devices with their start and end apart: 15 -> 14, of which waited for: 6 -> 7; matrix products, arithmetic and copies ran while one was open for 17% -> 12% of each run, Pallas kernels for 0% -> 0%
where the time goes in v5:
time: 166 us; the launch traced here: 165 us
  waiting for transfers between devices  67.7 us (41%)
  local copies, waits for them, and re-layouts  32.2 us (19%)
  starting transfers between devices  22 us (13%)
  other arithmetic  20.6 us (12%)
  between operations  13.9 us (8%)
  matrix products  9.01 us (5%)
    reduce_scatter x1, waiting for transfers between devices, body(): mine = lax.psum_scatter(merged, 'gy', scatter_dimension=0, tiled=False)  46.3 us
    reduce_sum x3, other arithmetic, combine(): prod_re = -jnp.sum(w * (col_re * row_re - col_im * row_im), axis=(2, 3))  12.1 us
    dot_general x1, matrix products, spectrum(): out = jnp.dot(traces.reshape(shots * recv, samples), table, precision=HIGH)  9.01 us
    mul x12, local copies, waits for them, and re-layouts, combine(): prod_re = -jnp.sum(w * (col_re * row_re - col_im * row_im), axis=(2, 3))  7.55 us
    unnamed x32, local copies, waits for them, and re-layouts  7.2 us
    ppermute x3, waiting for transfers between devices, body(): backward = lax.ppermute(backward, 'gz', left)  6.84 us
    all_to_all x1, waiting for transfers between devices, body(): lax.all_to_all(stacked, 'gy', split_axis=2, concat_axis=2, tiled=True)  5.26 us
    ppermute x3, starting transfers between devices, body(): forward = lax.ppermute(forward, 'gz', right)  4.91 us
  transfers between devices with their start and end apart: 14, of which 7 were waited for; matrix products, arithmetic and copies ran while one was open for 12% of the time, Pallas kernels for 0%

profile of v5, /device:TPU:32, one launch (start us, length us, event | category | flops | bytes accessed | tf_op | source)
XLA Modules:
  0.0 165.4 jit_solution(13069541961112080491)
XLA Ops:
  7.6 9.0 %fusion.4 = f32[384,256]{0,1:T(8,128)S(1)} fusion(f32[384,4096]{1,0:T(8,128)} %bitcast.103, f32[4096,128]{1,0:T(8,128)S(1)} %bitcast.102, f32[4096,128]{1,0:T(8,128)S(1)} %bitcast.101), kind=kOutput, calls=%fused_computation.20 | convolution fusion | flops 2416967680 | bytes 10878976 | tf_op jit(solution)/jit(body)/shard_map/dot_general | solution.py:36
  19.4 1.9 %collective-permute-start = (f32[792,128]{1,0:T(8,128)}, f32[792,128]{1,0:T(8,128)}, u32[]{:S(2)}, u32[]{:S(2)}) collective-permute-start(f32[792,128]{1,0:T(8,128)} %pad_maximum_fusion), channel_id=1, source_target_pairs={{0,1},{1,2},{2,3},{3,4},{4,5},{5,6},{6,7},{7,0},{8,9},{9,10},{10,1... | collective-permute-start | bytes 1216520 | tf_op jit(solution)/jit(body)/shard_map/ppermute | solution.py:104
  22.5 4.5 %all-to-all-start = ((f32[3,2,4,8,2,2,128]{6,5,4,3,1,0,2:T(2,128)}), f32[3,2,4,8,2,2,128]{6,5,4,3,1,0,2:T(2,128)S(1)}, u32[]{:S(2)}, u32[]{:S(2)}) async-start(f32[3,2,4,8,2,2,128]{6,5,4,3,1,0,2:T(2,128)} %copy.104), calls=%async_computation | async-start | bytes 786432 | tf_op jit(solution)/jit(body)/shard_map/all_to_all | solution.py:81
  29.4 5.3 %all-to-all-done = f32[3,2,4,8,2,2,128]{6,5,4,3,1,0,2:T(2,128)S(1)} async-done(((f32[3,2,4,8,2,2,128]{6,5,4,3,1,0,2:T(2,128)}), f32[3,2,4,8,2,2,128]{6,5,4,3,1,0,2:T(2,128)S(1)}, u32[]{:S(2)}, u32[]{:S(2)}) %all-to-all-start) | async-done | bytes 393248 | tf_op jit(solution)/jit(body)/shard_map/all_to_all | solution.py:81
  35.0 2.9 %collective-permute-start.9 = (f32[4,2,8,2,2,128]{5,0,4,3,2,1:T(4,128)S(1)}, f32[4,2,8,2,2,128]{5,0,4,3,2,1:T(4,128)S(1)}, u32[]{:S(2)}, u32[]{:S(2)}) collective-permute-start(f32[4,2,8,2,2,128]{5,0,4,3,2,1:T(4,128)S(1)} %get-tuple-element.47), channel_id=1, source_target_pairs={{32,0},{64,32},{96,64},{128,96},{160,128},{192,160},{224,192},{0,2... | collective-permute-start | bytes 393224 | tf_op jit(solution)/jit(body)/shard_map/ppermute | solution.py:86
  38.6 2.0 %collective-permute-start.2 = (f32[792,128]{1,0:T(8,128)}, f32[792,128]{1,0:T(8,128)S(1)}, u32[]{:S(2)}, u32[]{:S(2)}) collective-permute-start(f32[792,128]{1,0:T(8,128)} %collective-permute-done), channel_id=1, source_target_pairs={{0,1},{1,2},{2,3},{3,4},{4,5},{5,6},{6,7},{7,0},{8,9},{9,10},{10,1... | collective-permute-start | bytes 1216520 | tf_op jit(solution)/jit(body)/shard_map/ppermute | solution.py:104
  40.6 1.8 %bitcast_dynamic-update-slice_fusion.5 = f32[8,792,128]{2,1,0:T(8,128)} fusion(f32[8,792,128]{2,1,0:T(8,128)} %bitcast_dynamic-update-slice_fusion.6, f32[792,128]{1,0:T(8,128)} %collective-permute-done), kind=kLoop, calls=%fused_computation.41 | loop fusion | bytes 811008
  42.4 2.1 %collective-permute-start.3 = (f32[792,128]{1,0:T(8,128)}, f32[792,128]{1,0:T(8,128)S(1)}, u32[]{:S(2)}, u32[]{:S(2)}) collective-permute-start(f32[792,128]{1,0:T(8,128)} %collective-permute-done.1), channel_id=1, source_target_pairs={{1,0},{2,1},{3,2},{4,3},{5,4},{6,5},{7,6},{0,7},{9,8},{10,9},{11,1... | collective-permute-start | bytes 1216520 | tf_op jit(solution)/jit(body)/shard_map/ppermute | solution.py:107
  44.5 1.8 %bitcast_dynamic-update-slice_fusion.4 = f32[8,792,128]{2,1,0:T(8,128)} fusion(f32[8,792,128]{2,1,0:T(8,128)} %bitcast_dynamic-update-slice_fusion.5, f32[792,128]{1,0:T(8,128)} %collective-permute-done.1), kind=kLoop, calls=%fused_computation.40 | loop fusion | bytes 811008
  52.5 1.0 collective-permute-start.4
  53.6 2.2 %collective-permute-start.5 = (f32[792,128]{1,0:T(8,128)S(1)}, f32[792,128]{1,0:T(8,128)S(1)}, u32[]{:S(2)}, u32[]{:S(2)}) collective-permute-start(f32[792,128]{1,0:T(8,128)S(1)} %collective-permute-done.3), channel_id=1, source_target_pairs={{1,0},{2,1},{3,2},{4,3},{5,4},{6,5},{7,6},{0,7},{9,8},{10,9},{11,1... | collective-permute-start | bytes 1216520 | tf_op jit(solution)/jit(body)/shard_map/ppermute | solution.py:107
  57.4 6.7 %collective-permute-done.5 = f32[792,128]{1,0:T(8,128)S(1)} collective-permute-done((f32[792,128]{1,0:T(8,128)S(1)}, f32[792,128]{1,0:T(8,128)S(1)}, u32[]{:S(2)}, u32[]{:S(2)}) %collective-permute-start.5) | collective-permute-done | bytes 405536 | tf_op jit(solution)/jit(body)/shard_map/ppermute | solution.py:107
  64.1 1.6 collective-permute-start.7
  65.7 1.6 collective-permute-start.6
  68.8 4.3 %collective-permute-done.6 = f32[392,128]{1,0:T(8,128)S(1)} collective-permute-done((f32[392,128]{1,0:T(8,128)S(1)}, f32[392,128]{1,0:T(8,128)S(1)}, u32[]{:S(2)}, u32[]{:S(2)}) %collective-permute-start.6) | collective-permute-done | bytes 200736 | tf_op jit(solution)/jit(body)/shard_map/ppermute | solution.py:99
  74.9 2.1 %slice.191 = f32[8,768,128]{2,1,0:T(8,128)S(1)} slice(f32[8,792,128]{2,1,0:T(8,128)} %fusion.7), slice={[0:8], [0:768], [0:128]} | slice | bytes 6291456 | tf_op jit(solution)/jit(body)/shard_map/slice | solution.py:112
  77.0 2.1 %slice_bitcast_fusion.5 = (f32[8,2,2,64,128]{4,3,2,1,0:T(8,128)}, f32[8,2,2,64,128]{4,3,2,1,0:T(8,128)}, f32[8,2,2,64,128]{4,3,2,1,0:T(8,128)}, f32[8,2,2,64,128]{4,3,2,1,0:T(8,128)}) fusion(f32[8,2,2,2,96,128]{5,4,3,2,1,0:T(8,128)S(1)} %bitcast.99), kind=kLoop, calls=%fused_computation.24 | loop fusion | bytes 8388608 | tf_op jit(solution)/jit(body)/shard_map/mul | solution.py:46
  79.1 1.4 slice_bitcast_fusion.1
  80.4 1.6 copy.99
  83.8 1.8 %select_reduce_fusion = f32[8,3,4,96,2]{3,4,2,1,0:T(2,128)S(1)} fusion(f32[8,3,4,16,2]{3,4,2,1,0:T(2,128)} %copy.101, pred[8,3,4,16,96]{4,3,2,1,0:T(8,128)(4,1)S(1)} %iota_compare_fusion), kind=kLoop, calls=%fused_computation.19 | loop fusion | flops 571392 | bytes 233472 | tf_op jit(solution)/jit(body)/shard_map/reduce_sum | solution.py:118
  85.6 4.3 %multiply_reduce_fusion.5 = (f32[4,2,2,64,128]{4,3,2,1,0:T(8,128)S(1)}, f32[4,2,2,64,128]{4,3,2,1,0:T(8,128)S(1)}) fusion(f32[8,2,2,64,128]{4,3,2,1,0:T(8,128)} %get-tuple-element.41, f32[4,2,8,2,128]{4,3,2,1,0:T(2,128)} %copy.107, f32[8,2,2,64,128]{4,3,2,1,0:T(8,128)} %get-tuple-element.38, f32[4,2,8,2,128]{4,3,2,1,0:T(2,128)} %copy.106, ...), kind=kLoop, calls=%fused_computation.9 | loop fusion | flops 20709376 | bytes 3293184 | tf_op jit(solution)/jit(body)/shard_map/reduce_sum | solution.py:46
  90.1 4.6 %multiply_reduce_fusion.1 = (f32[4,2,2,96,128]{4,3,2,1,0:T(8,128)S(1)}, f32[4,2,2,96,128]{4,3,2,1,0:T(8,128)S(1)}) fusion(f32[8,2,2,96,128]{4,3,2,1,0:T(8,128)S(1)} %copy-done.1, f32[4,2,8,2,128]{4,3,2,1,0:T(2,128)S(1)} %copy-done.5, f32[8,2,2,96,128]{4,3,2,1,0:T(8,128)S(1)} %get-tuple-element.42, f32[4,2,8,2,128]{4,3,2,1,0:T(2,128)S(1)} %copy-done.4, ...), kind=kLoop, calls=%fused_computation.5 | loop fusion | flops 31064064 | bytes 4882432 | tf_op jit(solution)/jit(body)/shard_map/reduce_sum | solution.py:46
  94.9 3.1 %multiply_reduce_fusion.3 = (f32[4,2,2,64,128]{4,3,2,1,0:T(8,128)S(1)}, f32[4,2,2,64,128]{4,3,2,1,0:T(8,128)S(1)}) fusion(f32[8,2,2,64,128]{4,3,2,1,0:T(8,128)S(1)} %copy-done.2, f32[4,2,8,2,128]{4,3,2,1,0:T(2,128)S(1)} %copy-done.7, f32[8,2,2,64,128]{4,3,2,1,0:T(8,128)S(1)} %copy-done.3, f32[4,2,8,2,128]{4,3,2,1,0:T(2,128)S(1)} %copy-done.6, ...), kind=kLoop, calls=%fused_computation.7 | loop fusion | flops 20709376 | bytes 3293184 | tf_op jit(solution)/jit(body)/shard_map/reduce_sum | solution.py:46
  98.5 2.1 %copy.114 = f32[4,2,2,2,224,128]{5,4,3,2,1,0:T(8,128)} copy(f32[4,2,2,2,224,128]{5,4,2,1,0,3:T(8,128)S(1)} %maximum_maximum_fusion) | data formatting | bytes 7340032 | tf_op jit(solution)/jit(body)/shard_map/concatenate | solution.py:126
  100.7 46.3 %reduce-scatter.2.cloned.1.call-done = f32[1,2,2,2,224,128]{5,4,3,2,1,0:T(8,128)} async-done(((f32[4,2,2,2,224,128]{5,4,3,2,1,0:T(8,128)}), f32[1,2,2,2,224,128]{5,4,3,2,1,0:T(8,128)}) %reduce-scatter.2.cloned.1.call-update) | async-done | bytes 917520 | tf_op jit(solution)/jit(body)/shard_map/reduce_scatter | solution.py:127
  146.9 1.1 fusion.26
  148.0 2.1 %collective-permute-start.10 = (f32[2,2,2,64,128]{4,3,2,1,0:T(8,128)S(1)}, f32[2,2,2,64,128]{4,3,2,1,0:T(8,128)S(1)}, u32[]{:S(2)}, u32[]{:S(2)}) collective-permute-start(f32[2,2,2,64,128]{4,3,2,1,0:T(8,128)S(1)} %get-tuple-element.45), channel_id=1, source_target_pairs={{32,0},{64,32},{96,64},{128,96},{160,128},{192,160},{224,192},{0,2... | collective-permute-start | bytes 786440 | tf_op jit(solution)/jit(body)/shard_map/ppermute | solution.py:129
  150.1 1.0 slice.207
  151.1 2.9 %collective-permute-done.10 = f32[2,2,2,64,128]{4,3,2,1,0:T(8,128)S(1)} collective-permute-done((f32[2,2,2,64,128]{4,3,2,1,0:T(8,128)S(1)}, f32[2,2,2,64,128]{4,3,2,1,0:T(8,128)S(1)}, u32[]{:S(2)}, u32[]{:S(2)}) %collective-permute-start.10) | collective-permute-done | bytes 262176 | tf_op jit(solution)/jit(body)/shard_map/ppermute | solution.py:129
  154.0 1.0 fusion.9
  155.0 2.1 %collective-permute-done.11 = f32[2,2,2,64,128]{4,3,2,1,0:T(8,128)S(1)} collective-permute-done((f32[2,2,2,64,128]{4,3,2,1,0:T(8,128)S(1)}, f32[2,2,2,64,128]{4,3,2,1,0:T(8,128)S(1)}, u32[]{:S(2)}, u32[]{:S(2)}) %collective-permute-start.11) | collective-permute-done | bytes 262176 | tf_op jit(solution)/jit(body)/shard_map/ppermute | solution.py:130
  157.5 1.1 copy.116
  (96 shorter events, 22.2 us)
Async XLA Ops:
  6.5 20.5 %copy-start = (s32[256,3,32,16]{0,3,2,1:T(8,128)S(1)}, s32[256,3,32,16]{0,3,2,1:T(8,128)}, u32[]{:S(2)}) copy-start(s32[256,3,32,16]{0,3,2,1:T(8,128)} %param.12) | copy-start | bytes 4718596
  7.6 9.5 %copy-start.8 = (s32[1,3,32,16]{2,3,1,0:T(8,128)S(1)}, s32[1,3,32,16]{2,3,1,0:T(8,128)}, u32[]{:S(2)}) copy-start(s32[1,3,32,16]{2,3,1,0:T(8,128)} %param.13) | copy-start | bytes 18436
  7.6 9.6 %copy-start.10 = (f32[8,2]{0,1:T(2,128)S(1)}, f32[8,2]{0,1:T(2,128)}, u32[]{:S(2)}) copy-start(f32[8,2]{0,1:T(2,128)} %param.14) | copy-start | bytes 196
  17.6 10.0 %copy-start.11 = (s32[8]{0:T(128)S(1)}, s32[8]{0:T(128)}, u32[]{:S(2)}) copy-start(s32[8]{0:T(128)} %constant.147.clone) | copy-start | bytes 100
  19.4 19.2 %collective-permute-start = (f32[792,128]{1,0:T(8,128)}, f32[792,128]{1,0:T(8,128)}, u32[]{:S(2)}, u32[]{:S(2)}) collective-permute-start(f32[792,128]{1,0:T(8,128)} %pad_maximum_fusion), channel_id=1, source_target_pairs={{0,1},{1,2},{2,3},{3,4},{4,5},{5,6},{6,7},{7,0},{8,9},{9,10},{10,1... | collective-permute-start | bytes 1216520 | tf_op jit(solution)/jit(body)/shard_map/ppermute | solution.py:104
  21.3 21.1 %collective-permute-start.1 = (f32[792,128]{1,0:T(8,128)}, f32[792,128]{1,0:T(8,128)}, u32[]{:S(2)}, u32[]{:S(2)}) collective-permute-start(f32[792,128]{1,0:T(8,128)} %pad_maximum_fusion), channel_id=1, source_target_pairs={{1,0},{2,1},{3,2},{4,3},{5,4},{6,5},{7,6},{0,7},{9,8},{10,9},{11,1... | collective-permute-start | bytes 1216520 | tf_op jit(solution)/jit(body)/shard_map/ppermute | solution.py:107
  22.5 12.2 %all-to-all-start = ((f32[3,2,4,8,2,2,128]{6,5,4,3,1,0,2:T(2,128)}), f32[3,2,4,8,2,2,128]{6,5,4,3,1,0,2:T(2,128)S(1)}, u32[]{:S(2)}, u32[]{:S(2)}) async-start(f32[3,2,4,8,2,2,128]{6,5,4,3,1,0,2:T(2,128)} %copy.104), calls=%async_computation | async-start | bytes 786432 | tf_op jit(solution)/jit(body)/shard_map/all_to_all | solution.py:81
  27.0 120.0 %reduce-scatter.2.cloned.1.call-start = ((), (), s32[]{:S(2)}) async-start(), calls=%async_computation.2 | async-start | bytes 4587520 | tf_op jit(solution)/jit(body)/shard_map/reduce_scatter | solution.py:127
  27.6 7.3 %copy-start.9 = (pred[8]{0:T(512)(128)(4,1)}, pred[8]{0:T(512)(128)(4,1)S(1)}, u32[]{:S(2)}) copy-start(pred[8]{0:T(512)(128)(4,1)S(1)} %get-tuple-element.36) | copy-start | bytes 28
  35.0 11.4 %collective-permute-start.8 = (f32[4,2,8,2,2,128]{5,0,4,3,2,1:T(4,128)S(1)}, f32[4,2,8,2,2,128]{5,0,4,3,2,1:T(4,128)S(1)}, u32[]{:S(2)}, u32[]{:S(2)}) collective-permute-start(f32[4,2,8,2,2,128]{5,0,4,3,2,1:T(4,128)S(1)} %get-tuple-element.46), channel_id=1, source_target_pairs={{0,32},{32,64},{64,96},{96,128},{128,160},{160,192},{192,224},{224... | collective-permute-start | bytes 393224 | tf_op jit(solution)/jit(body)/shard_map/ppermute | solution.py:84
  35.0 12.0 %collective-permute-start.9 = (f32[4,2,8,2,2,128]{5,0,4,3,2,1:T(4,128)S(1)}, f32[4,2,8,2,2,128]{5,0,4,3,2,1:T(4,128)S(1)}, u32[]{:S(2)}, u32[]{:S(2)}) collective-permute-start(f32[4,2,8,2,2,128]{5,0,4,3,2,1:T(4,128)S(1)} %get-tuple-element.47), channel_id=1, source_target_pairs={{32,0},{64,32},{96,64},{128,96},{160,128},{192,160},{224,192},{0,2... | collective-permute-start | bytes 393224 | tf_op jit(solution)/jit(body)/shard_map/ppermute | solution.py:86
  38.6 13.9 %collective-permute-start.2 = (f32[792,128]{1,0:T(8,128)}, f32[792,128]{1,0:T(8,128)S(1)}, u32[]{:S(2)}, u32[]{:S(2)}) collective-permute-start(f32[792,128]{1,0:T(8,128)} %collective-permute-done), channel_id=1, source_target_pairs={{0,1},{1,2},{2,3},{3,4},{4,5},{5,6},{6,7},{7,0},{8,9},{9,10},{10,1... | collective-permute-start | bytes 1216520 | tf_op jit(solution)/jit(body)/shard_map/ppermute | solution.py:104
  42.4 11.3 %collective-permute-start.3 = (f32[792,128]{1,0:T(8,128)}, f32[792,128]{1,0:T(8,128)S(1)}, u32[]{:S(2)}, u32[]{:S(2)}) collective-permute-start(f32[792,128]{1,0:T(8,128)} %collective-permute-done.1), channel_id=1, source_target_pairs={{1,0},{2,1},{3,2},{4,3},{5,4},{6,5},{7,6},{0,7},{9,8},{10,9},{11,1... | collective-permute-start | bytes 1216520 | tf_op jit(solution)/jit(body)/shard_map/ppermute | solution.py:107
  52.5 13.2 %collective-permute-start.4 = (f32[792,128]{1,0:T(8,128)S(1)}, f32[792,128]{1,0:T(8,128)S(1)}, u32[]{:S(2)}, u32[]{:S(2)}) collective-permute-start(f32[792,128]{1,0:T(8,128)S(1)} %collective-permute-done.2), channel_id=1, source_target_pairs={{0,1},{1,2},{2,3},{3,4},{4,5},{5,6},{6,7},{7,0},{8,9},{9,10},{10,1... | collective-permute-start | bytes 1216520 | tf_op jit(solution)/jit(body)/shard_map/ppermute | solution.py:104
  53.6 10.5 %collective-permute-start.5 = (f32[792,128]{1,0:T(8,128)S(1)}, f32[792,128]{1,0:T(8,128)S(1)}, u32[]{:S(2)}, u32[]{:S(2)}) collective-permute-start(f32[792,128]{1,0:T(8,128)S(1)} %collective-permute-done.3), channel_id=1, source_target_pairs={{1,0},{2,1},{3,2},{4,3},{5,4},{6,5},{7,6},{0,7},{9,8},{10,9},{11,1... | collective-permute-start | bytes 1216520 | tf_op jit(solution)/jit(body)/shard_map/ppermute | solution.py:107
  64.1 9.1 %collective-permute-start.7 = (f32[400,128]{1,0:T(8,128)S(1)}, f32[400,128]{1,0:T(8,128)S(1)}, u32[]{:S(2)}, u32[]{:S(2)}) collective-permute-start(f32[400,128]{1,0:T(8,128)S(1)} %slice.186), channel_id=1, source_target_pairs={{1,0},{2,1},{3,2},{4,3},{5,4},{6,5},{7,6},{0,7},{9,8},{10,9},{11,1... | collective-permute-start | bytes 614408 | tf_op jit(solution)/jit(body)/shard_map/ppermute | solution.py:100
  65.7 7.5 %collective-permute-start.6 = (f32[392,128]{1,0:T(8,128)S(1)}, f32[392,128]{1,0:T(8,128)S(1)}, u32[]{:S(2)}, u32[]{:S(2)}) collective-permute-start(f32[392,128]{1,0:T(8,128)S(1)} %slice.185), channel_id=1, source_target_pairs={{0,1},{1,2},{2,3},{3,4},{4,5},{5,6},{6,7},{7,0},{8,9},{9,10},{10,1... | collective-permute-start | bytes 602120 | tf_op jit(solution)/jit(body)/shard_map/ppermute | solution.py:99
  83.8 6.3 %copy-start.1 = (f32[8,2,2,96,128]{4,3,2,1,0:T(8,128)S(1)}, f32[8,2,2,96,128]{4,3,2,1,0:T(8,128)}, u32[]{:S(2)}) copy-start(f32[8,2,2,96,128]{4,3,2,1,0:T(8,128)} %get-tuple-element.43) | copy-start | bytes 4718596
  83.8 6.3 %copy-start.4 = (f32[4,2,8,2,128]{4,3,2,1,0:T(2,128)S(1)}, f32[4,2,8,2,128]{4,3,2,1,0:T(2,128)}, u32[]{:S(2)}) copy-start(f32[4,2,8,2,128]{4,3,2,1,0:T(2,128)} %copy.109) | copy-start | bytes 196612
  83.8 6.3 %copy-start.5 = (f32[4,2,8,2,128]{4,3,2,1,0:T(2,128)S(1)}, f32[4,2,8,2,128]{4,3,2,1,0:T(2,128)}, u32[]{:S(2)}) copy-start(f32[4,2,8,2,128]{4,3,2,1,0:T(2,128)} %copy.110) | copy-start | bytes 196612
  90.1 4.8 %copy-start.2 = (f32[8,2,2,64,128]{4,3,2,1,0:T(8,128)S(1)}, f32[8,2,2,64,128]{4,3,2,1,0:T(8,128)}, u32[]{:S(2)}) copy-start(f32[8,2,2,64,128]{4,3,2,1,0:T(8,128)} %get-tuple-element.39) | copy-start | bytes 3145732
  90.1 4.8 %copy-start.3 = (f32[8,2,2,64,128]{4,3,2,1,0:T(8,128)S(1)}, f32[8,2,2,64,128]{4,3,2,1,0:T(8,128)}, u32[]{:S(2)}) copy-start(f32[8,2,2,64,128]{4,3,2,1,0:T(8,128)} %get-tuple-element.40) | copy-start | bytes 3145732
  90.1 4.8 %copy-start.6 = (f32[4,2,8,2,128]{4,3,2,1,0:T(2,128)S(1)}, f32[4,2,8,2,128]{4,3,2,1,0:T(2,128)}, u32[]{:S(2)}) copy-start(f32[4,2,8,2,128]{4,3,2,1,0:T(2,128)} %copy.112) | copy-start | bytes 196612
  90.1 4.8 %copy-start.7 = (f32[4,2,8,2,128]{4,3,2,1,0:T(2,128)S(1)}, f32[4,2,8,2,128]{4,3,2,1,0:T(2,128)}, u32[]{:S(2)}) copy-start(f32[4,2,8,2,128]{4,3,2,1,0:T(2,128)} %copy.113) | copy-start | bytes 196612
  148.0 6.0 %collective-permute-start.10 = (f32[2,2,2,64,128]{4,3,2,1,0:T(8,128)S(1)}, f32[2,2,2,64,128]{4,3,2,1,0:T(8,128)S(1)}, u32[]{:S(2)}, u32[]{:S(2)}) collective-permute-start(f32[2,2,2,64,128]{4,3,2,1,0:T(8,128)S(1)} %get-tuple-element.45), channel_id=1, source_target_pairs={{32,0},{64,32},{96,64},{128,96},{160,128},{192,160},{224,192},{0,2... | collective-permute-start | bytes 786440 | tf_op jit(solution)/jit(body)/shard_map/ppermute | solution.py:129
  150.1 7.0 %collective-permute-start.11 = (f32[2,2,2,64,128]{4,3,2,1,0:T(8,128)S(1)}, f32[2,2,2,64,128]{4,3,2,1,0:T(8,128)S(1)}, u32[]{:S(2)}, u32[]{:S(2)}) collective-permute-start(f32[2,2,2,64,128]{4,3,2,1,0:T(8,128)S(1)} %get-tuple-element.44), channel_id=1, source_target_pairs={{0,32},{32,64},{64,96},{96,128},{128,160},{160,192},{192,224},{224... | collective-permute-start | bytes 786440 | tf_op jit(solution)/jit(body)/shard_map/ppermute | solution.py:130
Sparse Core Ops, SparseCore 0:
  100.8 46.1 reduce-scatter.1

commit v6 on v5

--- a/solution.py
+++ b/solution.py
@@ -123,14 +123,12 @@
         cols_s = jnp.take(side_cols[s], sources, axis=2)
         return combine(cols_s, dense[s, :, :, :, lo:hi], gathered[:, :, :, :, lo:hi])
 
-    merged = jnp.concatenate([side_part(0), side_part(1), side_part(2)], axis=4)
-    mine = lax.psum_scatter(merged, "gy", scatter_dimension=0, tiled=False)
-    first, middle = 2 * width, 2 * width + blocks
-    from_up = lax.ppermute(mine[:, :, :, :first], "line", down)
-    from_down = lax.ppermute(mine[:, :, :, middle:], "line", up)
-    result = mine[:, :, :, first:middle]
-    result = result.at[:, :, :, width:].add(from_up)
-    result = result.at[:, :, :, : 2 * width].add(from_down)
+    from_up = lax.ppermute(side_part(0), "line", down)
+    from_down = lax.ppermute(side_part(2), "line", up)
+    total = side_part(1)
+    total = total.at[:, :, :, :, width:].add(from_up)
+    total = total.at[:, :, :, :, : 2 * width].add(from_down)
+    result = lax.psum_scatter(total, "gy", scatter_dimension=0, tiled=False)
     result = jnp.transpose(result, (0, 3, 1, 2, 4))
     return result.reshape(shots, recv, 2, NF)
 

time: 166 us -> 150 us (0.904)
  waiting for transfers between devices: 67.7 us -> 53.4 us
  local copies, waits for them, and re-layouts: 32.2 us -> 30.3 us
    reduce_scatter x1, waiting for transfers between devices: 46.3 us -> 29.3 us  [body(): result = lax.psum_scatter(total, 'gy', scatter_dimension=0, tiled=False)]
    ppermute x2, waiting for transfers between devices: 4.98 us -> 7.49 us  [the longest x1 7.48 us: body(): from_up = lax.ppermute(side_part(0), 'line', down)]
    concatenate x1 -> x0, local copies, waits for them, and re-layouts: 2.11 us -> none  [body(): merged = jnp.concatenate([side_part(0), side_part(1), side_part(2)], axis=4)]
    slice x2 -> x0, local copies, waits for them, and re-layouts: 2.09 us -> none  [the longest x1 1.07 us: body(): from_down = lax.ppermute(mine[:, :, :, middle:], 'line', up)]
  transfers between devices with their start and end apart: 14 -> 14, of which waited for: 7 -> 6; matrix products, arithmetic and copies ran while one was open for 12% -> 17% of each run, Pallas kernels for 0% -> 0%
where the time goes in v6:
time: 150 us; the launch traced here: 149 us
  waiting for transfers between devices  53.4 us (36%)
  local copies, waits for them, and re-layouts  30.3 us (20%)
  starting transfers between devices  22.7 us (15%)
  other arithmetic  19.7 us (13%)
  between operations  13.9 us (9%)
  matrix products  9.01 us (6%)
    reduce_scatter x1, waiting for transfers between devices, body(): result = lax.psum_scatter(total, 'gy', scatter_dimension=0, tiled=False)  29.3 us
    reduce_sum x3, other arithmetic, combine(): prod_re = -jnp.sum(w * (col_re * row_re - col_im * row_im), axis=(2, 3))  12.1 us
    dot_general x1, matrix products, spectrum(): out = jnp.dot(traces.reshape(shots * recv, samples), table, precision=HIGH)  9.01 us
    mul x12, local copies, waits for them, and re-layouts, combine(): prod_re = -jnp.sum(w * (col_re * row_re - col_im * row_im), axis=(2, 3))  7.58 us
    ppermute x1, waiting for transfers between devices, body(): from_up = lax.ppermute(side_part(0), 'line', down)  7.48 us
    unnamed x32, local copies, waits for them, and re-layouts  7.2 us
    ppermute x3, waiting for transfers between devices, body(): backward = lax.ppermute(backward, 'gz', left)  6.95 us
    all_to_all x1, waiting for transfers between devices, body(): lax.all_to_all(stacked, 'gy', split_axis=2, concat_axis=2, tiled=True)  5.25 us
  transfers between devices with their start and end apart: 14, of which 6 were waited for; matrix products, arithmetic and copies ran while one was open for 17% of the time, Pallas kernels for 0%

profile of v6, /device:TPU:32, one launch (start us, length us, event | category | flops | bytes accessed | tf_op | source)
XLA Modules:
  0.0 149.1 jit_solution(16246610907371965376)
XLA Ops:
  7.6 9.0 %fusion.4 = f32[384,256]{0,1:T(8,128)S(1)} fusion(f32[384,4096]{1,0:T(8,128)} %bitcast.104, f32[4096,128]{1,0:T(8,128)S(1)} %bitcast.103, f32[4096,128]{1,0:T(8,128)S(1)} %bitcast.102), kind=kOutput, calls=%fused_computation.22 | convolution fusion | flops 2416967680 | bytes 10878976 | tf_op jit(solution)/jit(body)/shard_map/dot_general | solution.py:36
  19.4 1.9 %collective-permute-start = (f32[792,128]{1,0:T(8,128)}, f32[792,128]{1,0:T(8,128)}, u32[]{:S(2)}, u32[]{:S(2)}) collective-permute-start(f32[792,128]{1,0:T(8,128)} %pad_maximum_fusion.3), channel_id=1, source_target_pairs={{0,1},{1,2},{2,3},{3,4},{4,5},{5,6},{6,7},{7,0},{8,9},{9,10},{10,1... | collective-permute-start | bytes 1216520 | tf_op jit(solution)/jit(body)/shard_map/ppermute | solution.py:104
  21.6 0.9 copy.104
  22.5 4.5 %all-to-all-start = ((f32[3,2,4,8,2,2,128]{6,5,4,3,1,0,2:T(2,128)}), f32[3,2,4,8,2,2,128]{6,5,4,3,1,0,2:T(2,128)S(1)}, u32[]{:S(2)}, u32[]{:S(2)}) async-start(f32[3,2,4,8,2,2,128]{6,5,4,3,1,0,2:T(2,128)} %copy.104), calls=%async_computation | async-start | bytes 786432 | tf_op jit(solution)/jit(body)/shard_map/all_to_all | solution.py:81
  29.4 5.3 %all-to-all-done = f32[3,2,4,8,2,2,128]{6,5,4,3,1,0,2:T(2,128)S(1)} async-done(((f32[3,2,4,8,2,2,128]{6,5,4,3,1,0,2:T(2,128)}), f32[3,2,4,8,2,2,128]{6,5,4,3,1,0,2:T(2,128)S(1)}, u32[]{:S(2)}, u32[]{:S(2)}) %all-to-all-start) | async-done | bytes 393248 | tf_op jit(solution)/jit(body)/shard_map/all_to_all | solution.py:81
  35.0 2.9 %collective-permute-start.10 = (f32[4,2,8,2,2,128]{5,0,4,3,2,1:T(4,128)S(1)}, f32[4,2,8,2,2,128]{5,0,4,3,2,1:T(4,128)S(1)}, u32[]{:S(2)}, u32[]{:S(2)}) collective-permute-start(f32[4,2,8,2,2,128]{5,0,4,3,2,1:T(4,128)S(1)} %get-tuple-element.44), channel_id=1, source_target_pairs={{32,0},{64,32},{96,64},{128,96},{160,128},{192,160},{224,192},{0,2... | collective-permute-start | bytes 393224 | tf_op jit(solution)/jit(body)/shard_map/ppermute | solution.py:86
  38.6 2.0 %collective-permute-start.2 = (f32[792,128]{1,0:T(8,128)}, f32[792,128]{1,0:T(8,128)S(1)}, u32[]{:S(2)}, u32[]{:S(2)}) collective-permute-start(f32[792,128]{1,0:T(8,128)} %collective-permute-done), channel_id=1, source_target_pairs={{0,1},{1,2},{2,3},{3,4},{4,5},{5,6},{6,7},{7,0},{8,9},{9,10},{10,1... | collective-permute-start | bytes 1216520 | tf_op jit(solution)/jit(body)/shard_map/ppermute | solution.py:104
  40.6 1.8 %bitcast_dynamic-update-slice_fusion.5 = f32[8,792,128]{2,1,0:T(8,128)} fusion(f32[8,792,128]{2,1,0:T(8,128)} %bitcast_dynamic-update-slice_fusion.6, f32[792,128]{1,0:T(8,128)} %collective-permute-done), kind=kLoop, calls=%fused_computation.50 | loop fusion | bytes 811008
  42.4 2.1 %collective-permute-start.3 = (f32[792,128]{1,0:T(8,128)}, f32[792,128]{1,0:T(8,128)S(1)}, u32[]{:S(2)}, u32[]{:S(2)}) collective-permute-start(f32[792,128]{1,0:T(8,128)} %collective-permute-done.1), channel_id=1, source_target_pairs={{1,0},{2,1},{3,2},{4,3},{5,4},{6,5},{7,6},{0,7},{9,8},{10,9},{11,1... | collective-permute-start | bytes 1216520 | tf_op jit(solution)/jit(body)/shard_map/ppermute | solution.py:107
  44.5 1.8 %bitcast_dynamic-update-slice_fusion.4 = f32[8,792,128]{2,1,0:T(8,128)} fusion(f32[8,792,128]{2,1,0:T(8,128)} %bitcast_dynamic-update-slice_fusion.5, f32[792,128]{1,0:T(8,128)} %collective-permute-done.1), kind=kLoop, calls=%fused_computation.49 | loop fusion | bytes 811008
  52.4 1.0 collective-permute-start.4
  53.6 2.1 %collective-permute-start.5 = (f32[792,128]{1,0:T(8,128)S(1)}, f32[792,128]{1,0:T(8,128)S(1)}, u32[]{:S(2)}, u32[]{:S(2)}) collective-permute-start(f32[792,128]{1,0:T(8,128)S(1)} %collective-permute-done.3), channel_id=1, source_target_pairs={{1,0},{2,1},{3,2},{4,3},{5,4},{6,5},{7,6},{0,7},{9,8},{10,9},{11,1... | collective-permute-start | bytes 1216520 | tf_op jit(solution)/jit(body)/shard_map/ppermute | solution.py:107
  57.3 6.7 %collective-permute-done.5 = f32[792,128]{1,0:T(8,128)S(1)} collective-permute-done((f32[792,128]{1,0:T(8,128)S(1)}, f32[792,128]{1,0:T(8,128)S(1)}, u32[]{:S(2)}, u32[]{:S(2)}) %collective-permute-start.5) | collective-permute-done | bytes 405536 | tf_op jit(solution)/jit(body)/shard_map/ppermute | solution.py:107
  64.0 1.6 %collective-permute-start.7 = (f32[400,128]{1,0:T(8,128)S(1)}, f32[400,128]{1,0:T(8,128)S(1)}, u32[]{:S(2)}, u32[]{:S(2)}) collective-permute-start(f32[400,128]{1,0:T(8,128)S(1)} %slice.183), channel_id=1, source_target_pairs={{1,0},{2,1},{3,2},{4,3},{5,4},{6,5},{7,6},{0,7},{9,8},{10,9},{11,1... | collective-permute-start | bytes 614408 | tf_op jit(solution)/jit(body)/shard_map/ppermute | solution.py:100
  65.6 1.6 %collective-permute-start.6 = (f32[392,128]{1,0:T(8,128)S(1)}, f32[392,128]{1,0:T(8,128)S(1)}, u32[]{:S(2)}, u32[]{:S(2)}) collective-permute-start(f32[392,128]{1,0:T(8,128)S(1)} %slice.182), channel_id=1, source_target_pairs={{0,1},{1,2},{2,3},{3,4},{4,5},{5,6},{6,7},{7,0},{8,9},{9,10},{10,1... | collective-permute-start | bytes 602120 | tf_op jit(solution)/jit(body)/shard_map/ppermute | solution.py:99
  68.7 4.3 %collective-permute-done.6 = f32[392,128]{1,0:T(8,128)S(1)} collective-permute-done((f32[392,128]{1,0:T(8,128)S(1)}, f32[392,128]{1,0:T(8,128)S(1)}, u32[]{:S(2)}, u32[]{:S(2)}) %collective-permute-start.6) | collective-permute-done | bytes 200736 | tf_op jit(solution)/jit(body)/shard_map/ppermute | solution.py:99
  73.8 0.9 slice.184
  74.7 2.1 %slice.188 = f32[8,768,128]{2,1,0:T(8,128)S(1)} slice(f32[8,792,128]{2,1,0:T(8,128)} %fusion.11), slice={[0:8], [0:768], [0:128]} | slice | bytes 6291456 | tf_op jit(solution)/jit(body)/shard_map/slice | solution.py:112
  76.9 2.1 %slice_bitcast_fusion.3 = (f32[8,2,2,64,128]{4,3,2,1,0:T(8,128)}, f32[8,2,2,64,128]{4,3,2,1,0:T(8,128)}, f32[8,2,2,64,128]{4,3,2,1,0:T(8,128)}, f32[8,2,2,64,128]{4,3,2,1,0:T(8,128)}) fusion(f32[8,2,2,2,96,128]{5,4,3,2,1,0:T(8,128)S(1)} %bitcast.100), kind=kLoop, calls=%fused_computation.27 | loop fusion | bytes 8388608 | tf_op jit(solution)/jit(body)/shard_map/mul | solution.py:46
  79.0 1.4 slice_bitcast_fusion.1
  80.4 1.6 %copy.99 = f32[8,24,128]{0,2,1:T(8,128)} copy(f32[8,24,128]{2,1,0:T(8,128)S(1)} %slice.184) | data formatting | bytes 196608 | tf_op jit(solution)/jit(body)/shard_map/slice | solution.py:114
  82.0 0.9 dynamic-slice_bitcast_fusion
  83.7 1.7 %select_reduce_fusion = f32[8,3,4,96,2]{3,4,2,1,0:T(2,128)S(1)} fusion(f32[8,3,4,16,2]{3,4,2,1,0:T(2,128)} %copy.101, pred[8,3,4,16,96]{4,3,2,1,0:T(8,128)(4,1)S(1)} %iota_compare_fusion), kind=kLoop, calls=%fused_computation.21 | loop fusion | flops 571392 | bytes 233472 | tf_op jit(solution)/jit(body)/shard_map/reduce_sum | solution.py:118
  85.5 4.5 %multiply_reduce_fusion.3 = (f32[4,2,2,64,128]{4,3,2,1,0:T(8,128)S(1)}, f32[4,2,2,64,128]{4,3,2,1,0:T(8,128)S(1)}) fusion(f32[8,2,2,64,128]{4,3,2,1,0:T(8,128)} %get-tuple-element.39, f32[4,2,8,2,128]{4,3,2,1,0:T(2,128)} %copy.113, f32[8,2,2,64,128]{4,3,2,1,0:T(8,128)} %get-tuple-element.38, f32[4,2,8,2,128]{4,3,2,1,0:T(2,128)} %copy.112, ...), kind=kLoop, calls=%fused_computation.7 | loop fusion | flops 20709376 | bytes 3293184 | tf_op jit(solution)/jit(body)/shard_map/reduce_sum | solution.py:46
  90.2 3.1 %multiply_reduce_fusion.5 = (f32[4,2,2,64,128]{4,3,2,1,0:T(8,128)S(1)}, f32[4,2,2,64,128]{4,3,2,1,0:T(8,128)S(1)}) fusion(f32[8,2,2,64,128]{4,3,2,1,0:T(8,128)S(1)} %copy-done.2, f32[4,2,8,2,128]{4,3,2,1,0:T(2,128)S(1)} %copy-done.7, f32[8,2,2,64,128]{4,3,2,1,0:T(8,128)S(1)} %copy-done.3, f32[4,2,8,2,128]{4,3,2,1,0:T(2,128)S(1)} %copy-done.6, ...), kind=kLoop, calls=%fused_computation.9 | loop fusion | flops 20709376 | bytes 3293184 | tf_op jit(solution)/jit(body)/shard_map/reduce_sum | solution.py:46
  93.6 2.9 %collective-permute-start.9 = (f32[4,2,2,2,64,128]{5,4,2,1,0,3:T(8,128)S(1)}, f32[4,2,2,2,64,128]{5,4,2,1,0,3:T(8,128)S(1)}, u32[]{:S(2)}, u32[]{:S(2)}) collective-permute-start(f32[4,2,2,2,64,128]{5,4,2,1,0,3:T(8,128)S(1)} %pad_maximum_fusion.1), channel_id=1, source_target_pairs={{32,0},{64,32},{96,64},{128,96},{160,128},{192,160},{224,192},{0,2... | collective-permute-start | bytes 3145736 | tf_op jit(solution)/jit(body)/shard_map/ppermute | solution.py:126
  96.5 4.5 %multiply_reduce_fusion.1 = (f32[4,2,2,96,128]{4,3,2,1,0:T(8,128)S(1)}, f32[4,2,2,96,128]{4,3,2,1,0:T(8,128)S(1)}) fusion(f32[8,2,2,96,128]{4,3,2,1,0:T(8,128)S(1)} %copy-done.1, f32[4,2,8,2,128]{4,3,2,1,0:T(2,128)S(1)} %copy-done.5, f32[8,2,2,96,128]{4,3,2,1,0:T(8,128)S(1)} %get-tuple-element.42, f32[4,2,8,2,128]{4,3,2,1,0:T(2,128)S(1)} %copy-done.4, ...), kind=kLoop, calls=%fused_computation.5 | loop fusion | flops 31064064 | bytes 4882432 | tf_op jit(solution)/jit(body)/shard_map/reduce_sum | solution.py:46
  101.3 7.5 %collective-permute-done.9 = f32[4,2,2,2,64,128]{5,4,2,1,0,3:T(8,128)S(1)} collective-permute-done((f32[4,2,2,2,64,128]{5,4,2,1,0,3:T(8,128)S(1)}, f32[4,2,2,2,64,128]{5,4,2,1,0,3:T(8,128)S(1)}, u32[]{:S(2)}, u32[]{:S(2)}) %collective-permute-start.9) | collective-permute-done | bytes 1048608 | tf_op jit(solution)/jit(body)/shard_map/ppermute | solution.py:126
  109.2 1.3 copy.114
  110.6 29.3 %reduce-scatter.2.cloned.1.call-done = f32[1,2,2,2,96,128]{5,4,3,2,1,0:T(8,128)} async-done(((f32[4,2,2,2,96,128]{5,4,3,2,1,0:T(8,128)}), f32[1,2,2,2,96,128]{5,4,3,2,1,0:T(8,128)}) %reduce-scatter.2.cloned.1.call-update) | async-done | bytes 393232 | tf_op jit(solution)/jit(body)/shard_map/reduce_scatter | solution.py:131
  139.9 1.3 copy.115
  141.2 1.1 copy.116
  (96 shorter events, 19.5 us)
Async XLA Ops:
  6.5 20.4 %copy-start = (s32[256,3,32,16]{0,3,2,1:T(8,128)S(1)}, s32[256,3,32,16]{0,3,2,1:T(8,128)}, u32[]{:S(2)}) copy-start(s32[256,3,32,16]{0,3,2,1:T(8,128)} %param.12) | copy-start | bytes 4718596
  7.6 9.5 %copy-start.8 = (s32[1,3,32,16]{2,3,1,0:T(8,128)S(1)}, s32[1,3,32,16]{2,3,1,0:T(8,128)}, u32[]{:S(2)}) copy-start(s32[1,3,32,16]{2,3,1,0:T(8,128)} %param.13) | copy-start | bytes 18436
  7.6 9.6 %copy-start.10 = (f32[8,2]{0,1:T(2,128)S(1)}, f32[8,2]{0,1:T(2,128)}, u32[]{:S(2)}) copy-start(f32[8,2]{0,1:T(2,128)} %param.14) | copy-start | bytes 196
  18.2 9.3 %copy-start.11 = (s32[8]{0:T(128)S(1)}, s32[8]{0:T(128)}, u32[]{:S(2)}) copy-start(s32[8]{0:T(128)} %constant.147.clone) | copy-start | bytes 100
  19.4 19.2 %collective-permute-start = (f32[792,128]{1,0:T(8,128)}, f32[792,128]{1,0:T(8,128)}, u32[]{:S(2)}, u32[]{:S(2)}) collective-permute-start(f32[792,128]{1,0:T(8,128)} %pad_maximum_fusion.3), channel_id=1, source_target_pairs={{0,1},{1,2},{2,3},{3,4},{4,5},{5,6},{6,7},{7,0},{8,9},{9,10},{10,1... | collective-permute-start | bytes 1216520 | tf_op jit(solution)/jit(body)/shard_map/ppermute | solution.py:104
  21.3 21.1 %collective-permute-start.1 = (f32[792,128]{1,0:T(8,128)}, f32[792,128]{1,0:T(8,128)}, u32[]{:S(2)}, u32[]{:S(2)}) collective-permute-start(f32[792,128]{1,0:T(8,128)} %pad_maximum_fusion.3), channel_id=1, source_target_pairs={{1,0},{2,1},{3,2},{4,3},{5,4},{6,5},{7,6},{0,7},{9,8},{10,9},{11,1... | collective-permute-start | bytes 1216520 | tf_op jit(solution)/jit(body)/shard_map/ppermute | solution.py:107
  22.5 12.2 %all-to-all-start = ((f32[3,2,4,8,2,2,128]{6,5,4,3,1,0,2:T(2,128)}), f32[3,2,4,8,2,2,128]{6,5,4,3,1,0,2:T(2,128)S(1)}, u32[]{:S(2)}, u32[]{:S(2)}) async-start(f32[3,2,4,8,2,2,128]{6,5,4,3,1,0,2:T(2,128)} %copy.104), calls=%async_computation | async-start | bytes 786432 | tf_op jit(solution)/jit(body)/shard_map/all_to_all | solution.py:81
  27.0 112.9 %reduce-scatter.2.cloned.1.call-start = ((), (), s32[]{:S(2)}) async-start(), calls=%async_computation.2 | async-start | bytes 1966080 | tf_op jit(solution)/jit(body)/shard_map/reduce_scatter | solution.py:131
  27.6 7.3 %copy-start.9 = (pred[8]{0:T(512)(128)(4,1)}, pred[8]{0:T(512)(128)(4,1)S(1)}, u32[]{:S(2)}) copy-start(pred[8]{0:T(512)(128)(4,1)S(1)} %get-tuple-element.36) | copy-start | bytes 28
  35.0 11.4 %collective-permute-start.8 = (f32[4,2,8,2,2,128]{5,0,4,3,2,1:T(4,128)S(1)}, f32[4,2,8,2,2,128]{5,0,4,3,2,1:T(4,128)S(1)}, u32[]{:S(2)}, u32[]{:S(2)}) collective-permute-start(f32[4,2,8,2,2,128]{5,0,4,3,2,1:T(4,128)S(1)} %get-tuple-element.45), channel_id=1, source_target_pairs={{0,32},{32,64},{64,96},{96,128},{128,160},{160,192},{192,224},{224... | collective-permute-start | bytes 393224 | tf_op jit(solution)/jit(body)/shard_map/ppermute | solution.py:84
  35.0 12.0 %collective-permute-start.10 = (f32[4,2,8,2,2,128]{5,0,4,3,2,1:T(4,128)S(1)}, f32[4,2,8,2,2,128]{5,0,4,3,2,1:T(4,128)S(1)}, u32[]{:S(2)}, u32[]{:S(2)}) collective-permute-start(f32[4,2,8,2,2,128]{5,0,4,3,2,1:T(4,128)S(1)} %get-tuple-element.44), channel_id=1, source_target_pairs={{32,0},{64,32},{96,64},{128,96},{160,128},{192,160},{224,192},{0,2... | collective-permute-start | bytes 393224 | tf_op jit(solution)/jit(body)/shard_map/ppermute | solution.py:86
  38.6 13.8 %collective-permute-start.2 = (f32[792,128]{1,0:T(8,128)}, f32[792,128]{1,0:T(8,128)S(1)}, u32[]{:S(2)}, u32[]{:S(2)}) collective-permute-start(f32[792,128]{1,0:T(8,128)} %collective-permute-done), channel_id=1, source_target_pairs={{0,1},{1,2},{2,3},{3,4},{4,5},{5,6},{6,7},{7,0},{8,9},{9,10},{10,1... | collective-permute-start | bytes 1216520 | tf_op jit(solution)/jit(body)/shard_map/ppermute | solution.py:104
  42.4 11.3 %collective-permute-start.3 = (f32[792,128]{1,0:T(8,128)}, f32[792,128]{1,0:T(8,128)S(1)}, u32[]{:S(2)}, u32[]{:S(2)}) collective-permute-start(f32[792,128]{1,0:T(8,128)} %collective-permute-done.1), channel_id=1, source_target_pairs={{1,0},{2,1},{3,2},{4,3},{5,4},{6,5},{7,6},{0,7},{9,8},{10,9},{11,1... | collective-permute-start | bytes 1216520 | tf_op jit(solution)/jit(body)/shard_map/ppermute | solution.py:107
  52.4 13.2 %collective-permute-start.4 = (f32[792,128]{1,0:T(8,128)S(1)}, f32[792,128]{1,0:T(8,128)S(1)}, u32[]{:S(2)}, u32[]{:S(2)}) collective-permute-start(f32[792,128]{1,0:T(8,128)S(1)} %collective-permute-done.2), channel_id=1, source_target_pairs={{0,1},{1,2},{2,3},{3,4},{4,5},{5,6},{6,7},{7,0},{8,9},{9,10},{10,1... | collective-permute-start | bytes 1216520 | tf_op jit(solution)/jit(body)/shard_map/ppermute | solution.py:104
  53.6 10.3 %collective-permute-start.5 = (f32[792,128]{1,0:T(8,128)S(1)}, f32[792,128]{1,0:T(8,128)S(1)}, u32[]{:S(2)}, u32[]{:S(2)}) collective-permute-start(f32[792,128]{1,0:T(8,128)S(1)} %collective-permute-done.3), channel_id=1, source_target_pairs={{1,0},{2,1},{3,2},{4,3},{5,4},{6,5},{7,6},{0,7},{9,8},{10,9},{11,1... | collective-permute-start | bytes 1216520 | tf_op jit(solution)/jit(body)/shard_map/ppermute | solution.py:107
  64.0 9.1 %collective-permute-start.7 = (f32[400,128]{1,0:T(8,128)S(1)}, f32[400,128]{1,0:T(8,128)S(1)}, u32[]{:S(2)}, u32[]{:S(2)}) collective-permute-start(f32[400,128]{1,0:T(8,128)S(1)} %slice.183), channel_id=1, source_target_pairs={{1,0},{2,1},{3,2},{4,3},{5,4},{6,5},{7,6},{0,7},{9,8},{10,9},{11,1... | collective-permute-start | bytes 614408 | tf_op jit(solution)/jit(body)/shard_map/ppermute | solution.py:100
  65.6 7.5 %collective-permute-start.6 = (f32[392,128]{1,0:T(8,128)S(1)}, f32[392,128]{1,0:T(8,128)S(1)}, u32[]{:S(2)}, u32[]{:S(2)}) collective-permute-start(f32[392,128]{1,0:T(8,128)S(1)} %slice.182), channel_id=1, source_target_pairs={{0,1},{1,2},{2,3},{3,4},{4,5},{5,6},{6,7},{7,0},{8,9},{9,10},{10,1... | collective-permute-start | bytes 602120 | tf_op jit(solution)/jit(body)/shard_map/ppermute | solution.py:99
  85.5 4.7 %copy-start.2 = (f32[8,2,2,64,128]{4,3,2,1,0:T(8,128)S(1)}, f32[8,2,2,64,128]{4,3,2,1,0:T(8,128)}, u32[]{:S(2)}) copy-start(f32[8,2,2,64,128]{4,3,2,1,0:T(8,128)} %get-tuple-element.40) | copy-start | bytes 3145732
  85.5 4.7 %copy-start.3 = (f32[8,2,2,64,128]{4,3,2,1,0:T(8,128)S(1)}, f32[8,2,2,64,128]{4,3,2,1,0:T(8,128)}, u32[]{:S(2)}) copy-start(f32[8,2,2,64,128]{4,3,2,1,0:T(8,128)} %get-tuple-element.41) | copy-start | bytes 3145732
  85.5 4.7 %copy-start.6 = (f32[4,2,8,2,128]{4,3,2,1,0:T(2,128)S(1)}, f32[4,2,8,2,128]{4,3,2,1,0:T(2,128)}, u32[]{:S(2)}) copy-start(f32[4,2,8,2,128]{4,3,2,1,0:T(2,128)} %copy.109) | copy-start | bytes 196612
  85.5 4.7 %copy-start.7 = (f32[4,2,8,2,128]{4,3,2,1,0:T(2,128)S(1)}, f32[4,2,8,2,128]{4,3,2,1,0:T(2,128)}, u32[]{:S(2)}) copy-start(f32[4,2,8,2,128]{4,3,2,1,0:T(2,128)} %copy.110) | copy-start | bytes 196612
  90.1 18.8 %collective-permute-start.11 = (f32[4,2,2,2,64,128]{5,4,2,1,0,3:T(8,128)S(1)}, f32[4,2,2,2,64,128]{5,4,2,1,0,3:T(8,128)S(1)}, u32[]{:S(2)}, u32[]{:S(2)}) collective-permute-start(f32[4,2,2,2,64,128]{5,4,2,1,0,3:T(8,128)S(1)} %pad_maximum_fusion.2), channel_id=1, source_target_pairs={{0,32},{32,64},{64,96},{96,128},{128,160},{160,192},{192,224},{224... | collective-permute-start | bytes 3145736 | tf_op jit(solution)/jit(body)/shard_map/ppermute | solution.py:127
  90.2 6.3 %copy-start.1 = (f32[8,2,2,96,128]{4,3,2,1,0:T(8,128)S(1)}, f32[8,2,2,96,128]{4,3,2,1,0:T(8,128)}, u32[]{:S(2)}) copy-start(f32[8,2,2,96,128]{4,3,2,1,0:T(8,128)} %get-tuple-element.43) | copy-start | bytes 4718596
  90.2 6.3 %copy-start.4 = (f32[4,2,8,2,128]{4,3,2,1,0:T(2,128)S(1)}, f32[4,2,8,2,128]{4,3,2,1,0:T(2,128)}, u32[]{:S(2)}) copy-start(f32[4,2,8,2,128]{4,3,2,1,0:T(2,128)} %copy.106) | copy-start | bytes 196612
  90.2 6.3 %copy-start.5 = (f32[4,2,8,2,128]{4,3,2,1,0:T(2,128)S(1)}, f32[4,2,8,2,128]{4,3,2,1,0:T(2,128)}, u32[]{:S(2)}) copy-start(f32[4,2,8,2,128]{4,3,2,1,0:T(2,128)} %copy.107) | copy-start | bytes 196612
  93.6 15.2 %collective-permute-start.9 = (f32[4,2,2,2,64,128]{5,4,2,1,0,3:T(8,128)S(1)}, f32[4,2,2,2,64,128]{5,4,2,1,0,3:T(8,128)S(1)}, u32[]{:S(2)}, u32[]{:S(2)}) collective-permute-start(f32[4,2,2,2,64,128]{5,4,2,1,0,3:T(8,128)S(1)} %pad_maximum_fusion.1), channel_id=1, source_target_pairs={{32,0},{64,32},{96,64},{128,96},{160,128},{192,160},{224,192},{0,2... | collective-permute-start | bytes 3145736 | tf_op jit(solution)/jit(body)/shard_map/ppermute | solution.py:126
Sparse Core Ops, SparseCore 0:
  110.7 29.1 reduce-scatter.1

commit v7 on v6

--- a/solution.py
+++ b/solution.py
@@ -119,9 +119,9 @@
     dense = jnp.transpose(dense, (1, 2, 0, 4, 3))
 
     def side_part(s):
+        cols_s = jnp.take(side_cols[s], sources, axis=2)
         lo, hi = spans[s]
-        cols_s = jnp.take(side_cols[s], sources, axis=2)
-        return combine(cols_s, dense[s, :, :, :, lo:hi], gathered[:, :, :, :, lo:hi])
+        return combine(cols_s, dense[s], gathered)[:, :, :, :, lo:hi]
 
     from_up = lax.ppermute(side_part(0), "line", down)
     from_down = lax.ppermute(side_part(2), "line", up)

time: 150 us -> 155 us (1.033)
  waiting for transfers between devices: 53.4 us -> 59.3 us
  other arithmetic: 19.7 us -> 23.4 us
  starting transfers between devices: 22.7 us -> 20.3 us
  local copies, waits for them, and re-layouts: 30.3 us -> 28 us
    reduce_sum x3 -> x1, other arithmetic: 12.1 us -> 16.6 us  [combine(): prod_re = -jnp.sum(w * (col_re * row_re - col_im * row_im), axis=(2, 3))]
    ppermute x1, waiting for transfers between devices: 7.48 us -> 11.4 us  [body(): from_up = lax.ppermute(side_part(0), 'line', down)]
    ppermute x1, waiting for transfers between devices: 0.01 us -> 3.14 us  [body(): from_down = lax.ppermute(side_part(2), 'line', up)]
    ppermute x1, starting transfers between devices: 2.93 us -> 0.02 us  [body(): from_up = lax.ppermute(side_part(0), 'line', down)]
    slice x1, local copies, waits for them, and re-layouts: 2.11 us -> 3.81 us  [body(): gathered = ring[:, :spec_rows].reshape((len(carried),) + lanes.shape)]
    mul x12 -> x11, local copies, waits for them, and re-layouts: 7.58 us -> 6.23 us  [combine(): prod_re = -jnp.sum(w * (col_re * row_re - col_im * row_im), axis=(2, 3))]
    unnamed x32 -> x30, local copies, waits for them, and re-layouts: 7.2 us -> 7.22 us
  transfers between devices with their start and end apart: 14 -> 14, of which waited for: 6 -> 7; matrix products, arithmetic and copies ran while one was open for 17% -> 12% of each run, Pallas kernels for 0% -> 0%
where the time goes in v7:
time: 155 us; the launch traced here: 154 us
  waiting for transfers between devices  59.3 us (38%)
  local copies, waits for them, and re-layouts  28 us (18%)
  other arithmetic  23.4 us (15%)
  starting transfers between devices  20.3 us (13%)
  between operations  13.9 us (9%)
  matrix products  9.01 us (6%)
    reduce_scatter x1, waiting for transfers between devices, body(): result = lax.psum_scatter(total, 'gy', scatter_dimension=0, tiled=False)  28.3 us
    reduce_sum x1, other arithmetic, combine(): prod_re = -jnp.sum(w * (col_re * row_re - col_im * row_im), axis=(2, 3))  16.6 us
    ppermute x1, waiting for transfers between devices, body(): from_up = lax.ppermute(side_part(0), 'line', down)  11.4 us
    dot_general x1, matrix products, spectrum(): out = jnp.dot(traces.reshape(shots * recv, samples), table, precision=HIGH)  9.01 us
    unnamed x30, local copies, waits for them, and re-layouts  7.22 us
    ppermute x3, waiting for transfers between devices, body(): backward = lax.ppermute(backward, 'gz', left)  6.94 us
    mul x11, local copies, waits for them, and re-layouts, combine(): prod_re = -jnp.sum(w * (col_re * row_re - col_im * row_im), axis=(2, 3))  6.23 us
    all_to_all x1, waiting for transfers between devices, body(): lax.all_to_all(stacked, 'gy', split_axis=2, concat_axis=2, tiled=True)  5.26 us
  transfers between devices with their start and end apart: 14, of which 7 were waited for; matrix products, arithmetic and copies ran while one was open for 12% of the time, Pallas kernels for 0%

profile of v7, /device:TPU:32, one launch (start us, length us, event | category | flops | bytes accessed | tf_op | source)
XLA Modules:
  0.0 154.0 jit_solution(9748158822604942722)
XLA Ops:
  7.6 9.0 %fusion.4 = f32[384,256]{0,1:T(8,128)S(1)} fusion(f32[384,4096]{1,0:T(8,128)} %bitcast.93, f32[4096,128]{1,0:T(8,128)S(1)} %bitcast.92, f32[4096,128]{1,0:T(8,128)S(1)} %bitcast.91), kind=kOutput, calls=%fused_computation.22 | convolution fusion | flops 2416967680 | bytes 10878976 | tf_op jit(solution)/jit(body)/shard_map/dot_general | solution.py:36
  18.6 0.8 pad_maximum_fusion.3
  19.4 1.9 %collective-permute-start = (f32[792,128]{1,0:T(8,128)}, f32[792,128]{1,0:T(8,128)}, u32[]{:S(2)}, u32[]{:S(2)}) collective-permute-start(f32[792,128]{1,0:T(8,128)} %pad_maximum_fusion.3), channel_id=1, source_target_pairs={{0,1},{1,2},{2,3},{3,4},{4,5},{5,6},{6,7},{7,0},{8,9},{9,10},{10,1... | collective-permute-start | bytes 1216520 | tf_op jit(solution)/jit(body)/shard_map/ppermute | solution.py:104
  21.6 0.9 copy.104
  22.5 4.5 %all-to-all-start = ((f32[3,2,4,8,2,2,128]{6,5,4,3,1,0,2:T(2,128)}), f32[3,2,4,8,2,2,128]{6,5,4,3,1,0,2:T(2,128)S(1)}, u32[]{:S(2)}, u32[]{:S(2)}) async-start(f32[3,2,4,8,2,2,128]{6,5,4,3,1,0,2:T(2,128)} %copy.104), calls=%async_computation | async-start | bytes 786432 | tf_op jit(solution)/jit(body)/shard_map/all_to_all | solution.py:81
  28.6 0.8 bitcast_dynamic-update-slice_fusion.6
  29.4 5.3 %all-to-all-done = f32[3,2,4,8,2,2,128]{6,5,4,3,1,0,2:T(2,128)S(1)} async-done(((f32[3,2,4,8,2,2,128]{6,5,4,3,1,0,2:T(2,128)}), f32[3,2,4,8,2,2,128]{6,5,4,3,1,0,2:T(2,128)S(1)}, u32[]{:S(2)}, u32[]{:S(2)}) %all-to-all-start) | async-done | bytes 393248 | tf_op jit(solution)/jit(body)/shard_map/all_to_all | solution.py:81
  35.0 2.9 %collective-permute-start.10 = (f32[4,2,8,2,2,128]{5,0,4,3,2,1:T(4,128)S(1)}, f32[4,2,8,2,2,128]{5,0,4,3,2,1:T(4,128)S(1)}, u32[]{:S(2)}, u32[]{:S(2)}) collective-permute-start(f32[4,2,8,2,2,128]{5,0,4,3,2,1:T(4,128)S(1)} %get-tuple-element.45), channel_id=1, source_target_pairs={{32,0},{64,32},{96,64},{128,96},{160,128},{192,160},{224,192},{0,2... | collective-permute-start | bytes 393224 | tf_op jit(solution)/jit(body)/shard_map/ppermute | solution.py:86
  38.6 2.0 %collective-permute-start.2 = (f32[792,128]{1,0:T(8,128)}, f32[792,128]{1,0:T(8,128)S(1)}, u32[]{:S(2)}, u32[]{:S(2)}) collective-permute-start(f32[792,128]{1,0:T(8,128)} %collective-permute-done), channel_id=1, source_target_pairs={{0,1},{1,2},{2,3},{3,4},{4,5},{5,6},{6,7},{7,0},{8,9},{9,10},{10,1... | collective-permute-start | bytes 1216520 | tf_op jit(solution)/jit(body)/shard_map/ppermute | solution.py:104
  40.6 1.8 %bitcast_dynamic-update-slice_fusion.5 = f32[8,792,128]{2,1,0:T(8,128)} fusion(f32[8,792,128]{2,1,0:T(8,128)} %bitcast_dynamic-update-slice_fusion.6, f32[792,128]{1,0:T(8,128)} %collective-permute-done), kind=kLoop, calls=%fused_computation.46 | loop fusion | bytes 811008
  42.4 2.1 %collective-permute-start.3 = (f32[792,128]{1,0:T(8,128)}, f32[792,128]{1,0:T(8,128)S(1)}, u32[]{:S(2)}, u32[]{:S(2)}) collective-permute-start(f32[792,128]{1,0:T(8,128)} %collective-permute-done.1), channel_id=1, source_target_pairs={{1,0},{2,1},{3,2},{4,3},{5,4},{6,5},{7,6},{0,7},{9,8},{10,9},{11,1... | collective-permute-start | bytes 1216520 | tf_op jit(solution)/jit(body)/shard_map/ppermute | solution.py:107
  44.5 1.8 %bitcast_dynamic-update-slice_fusion.4 = f32[8,792,128]{2,1,0:T(8,128)} fusion(f32[8,792,128]{2,1,0:T(8,128)} %bitcast_dynamic-update-slice_fusion.5, f32[792,128]{1,0:T(8,128)} %collective-permute-done.1), kind=kLoop, calls=%fused_computation.45 | loop fusion | bytes 811008
  52.4 1.0 collective-permute-start.4
  53.7 2.1 %collective-permute-start.5 = (f32[792,128]{1,0:T(8,128)S(1)}, f32[792,128]{1,0:T(8,128)S(1)}, u32[]{:S(2)}, u32[]{:S(2)}) collective-permute-start(f32[792,128]{1,0:T(8,128)S(1)} %collective-permute-done.3), channel_id=1, source_target_pairs={{1,0},{2,1},{3,2},{4,3},{5,4},{6,5},{7,6},{0,7},{9,8},{10,9},{11,1... | collective-permute-start | bytes 1216520 | tf_op jit(solution)/jit(body)/shard_map/ppermute | solution.py:107
  55.7 0.8 bitcast_dynamic-update-slice_fusion.3
  57.3 6.7 %collective-permute-done.5 = f32[792,128]{1,0:T(8,128)S(1)} collective-permute-done((f32[792,128]{1,0:T(8,128)S(1)}, f32[792,128]{1,0:T(8,128)S(1)}, u32[]{:S(2)}, u32[]{:S(2)}) %collective-permute-start.5) | collective-permute-done | bytes 405536 | tf_op jit(solution)/jit(body)/shard_map/ppermute | solution.py:107
  64.0 1.6 %collective-permute-start.7 = (f32[400,128]{1,0:T(8,128)S(1)}, f32[400,128]{1,0:T(8,128)S(1)}, u32[]{:S(2)}, u32[]{:S(2)}) collective-permute-start(f32[400,128]{1,0:T(8,128)S(1)} %slice.173), channel_id=1, source_target_pairs={{1,0},{2,1},{3,2},{4,3},{5,4},{6,5},{7,6},{0,7},{9,8},{10,9},{11,1... | collective-permute-start | bytes 614408 | tf_op jit(solution)/jit(body)/shard_map/ppermute | solution.py:100
  65.6 1.6 %collective-permute-start.6 = (f32[392,128]{1,0:T(8,128)S(1)}, f32[392,128]{1,0:T(8,128)S(1)}, u32[]{:S(2)}, u32[]{:S(2)}) collective-permute-start(f32[392,128]{1,0:T(8,128)S(1)} %slice.172), channel_id=1, source_target_pairs={{0,1},{1,2},{2,3},{3,4},{4,5},{5,6},{6,7},{7,0},{8,9},{9,10},{10,1... | collective-permute-start | bytes 602120 | tf_op jit(solution)/jit(body)/shard_map/ppermute | solution.py:99
  67.2 0.8 bitcast_dynamic-update-slice_fusion.1
  68.0 0.8 bitcast_dynamic-update-slice_fusion
  68.8 4.3 %collective-permute-done.6 = f32[392,128]{1,0:T(8,128)S(1)} collective-permute-done((f32[392,128]{1,0:T(8,128)S(1)}, f32[392,128]{1,0:T(8,128)S(1)}, u32[]{:S(2)}, u32[]{:S(2)}) %collective-permute-start.6) | collective-permute-done | bytes 200736 | tf_op jit(solution)/jit(body)/shard_map/ppermute | solution.py:99
  73.1 0.8 fusion.11
  73.9 0.9 slice.174
  74.8 3.8 %slice.178 = f32[8,768,128]{2,1,0:T(8,128)} slice(f32[8,792,128]{2,1,0:T(8,128)} %fusion.11), slice={[0:8], [0:768], [0:128]} | slice | bytes 6291456 | tf_op jit(solution)/jit(body)/shard_map/slice | solution.py:112
  80.1 2.2 %slice_bitcast_fusion.1 = (f32[8,2,2,96,128]{4,3,2,1,0:T(8,128)S(1)}, f32[8,2,2,96,128]{4,3,2,1,0:T(8,128)S(1)}) fusion(f32[8,2,2,2,96,128]{5,4,3,2,1,0:T(8,128)} %bitcast.90), kind=kLoop, calls=%fused_computation.20 | loop fusion | bytes 6291456 | tf_op jit(solution)/jit(body)/shard_map/mul | solution.py:46
  82.4 16.6 %multiply_reduce_fusion.1 = (f32[4,2,2,96,128]{4,3,2,1,0:T(8,128)S(1)}, f32[4,2,2,96,128]{4,3,2,1,0:T(8,128)S(1)}, f32[4,2,2,96,128]{4,3,2,1,0:T(8,128)S(1)}, f3...) fusion(f32[4,2,8,2,128]{4,3,2,1,0:T(2,128)S(1)} %copy-done.6, ...), kind=kLoop, calls=%fused_computation.5 | loop fusion | flops 93192192 | bytes 8331264 | tf_op jit(solution)/jit(body)/shard_map/reduce_sum | solution.py:46
  100.3 11.4 %collective-permute-done.9 = f32[4,2,2,2,64,128]{5,4,2,1,0,3:T(8,128)S(1)} collective-permute-done((f32[4,2,2,2,64,128]{5,4,2,1,0,3:T(8,128)S(1)}, f32[4,2,2,2,64,128]{5,4,2,1,0,3:T(8,128)S(1)}, u32[]{:S(2)}, u32[]{:S(2)}) %collective-permute-start.9) | collective-permute-done | bytes 1048608 | tf_op jit(solution)/jit(body)/shard_map/ppermute | solution.py:126
  111.8 3.1 %collective-permute-done.11 = f32[4,2,2,2,64,128]{5,4,2,1,0,3:T(8,128)S(1)} collective-permute-done((f32[4,2,2,2,64,128]{5,4,2,1,0,3:T(8,128)S(1)}, f32[4,2,2,2,64,128]{5,4,2,1,0,3:T(8,128)S(1)}, u32[]{:S(2)}, u32[]{:S(2)}) %collective-permute-start.11) | collective-permute-done | bytes 1048608 | tf_op jit(solution)/jit(body)/shard_map/ppermute | solution.py:127
  115.2 1.3 copy.114
  116.5 28.3 %reduce-scatter.2.cloned.1.call-done = f32[1,2,2,2,96,128]{5,4,3,2,1,0:T(8,128)} async-done(((f32[4,2,2,2,96,128]{5,4,3,2,1,0:T(8,128)}), f32[1,2,2,2,96,128]{5,4,3,2,1,0:T(8,128)}) %reduce-scatter.2.cloned.1.call-update) | async-done | bytes 393232 | tf_op jit(solution)/jit(body)/shard_map/reduce_scatter | solution.py:131
  144.8 1.3 copy.115
  146.1 1.1 copy.116
  (91 shorter events, 15.9 us)
Async XLA Ops:
  6.5 20.5 %copy-start = (s32[256,3,32,16]{0,3,2,1:T(8,128)S(1)}, s32[256,3,32,16]{0,3,2,1:T(8,128)}, u32[]{:S(2)}) copy-start(s32[256,3,32,16]{0,3,2,1:T(8,128)} %param.12) | copy-start | bytes 4718596
  7.6 9.5 %copy-start.7 = (s32[1,3,32,16]{2,3,1,0:T(8,128)S(1)}, s32[1,3,32,16]{2,3,1,0:T(8,128)}, u32[]{:S(2)}) copy-start(s32[1,3,32,16]{2,3,1,0:T(8,128)} %param.13) | copy-start | bytes 18436
  7.6 9.6 %copy-start.9 = (f32[8,2]{0,1:T(2,128)S(1)}, f32[8,2]{0,1:T(2,128)}, u32[]{:S(2)}) copy-start(f32[8,2]{0,1:T(2,128)} %param.14) | copy-start | bytes 196
  18.2 9.4 %copy-start.10 = (s32[8]{0:T(128)S(1)}, s32[8]{0:T(128)}, u32[]{:S(2)}) copy-start(s32[8]{0:T(128)} %constant.147.clone) | copy-start | bytes 100
  19.4 19.2 %collective-permute-start = (f32[792,128]{1,0:T(8,128)}, f32[792,128]{1,0:T(8,128)}, u32[]{:S(2)}, u32[]{:S(2)}) collective-permute-start(f32[792,128]{1,0:T(8,128)} %pad_maximum_fusion.3), channel_id=1, source_target_pairs={{0,1},{1,2},{2,3},{3,4},{4,5},{5,6},{6,7},{7,0},{8,9},{9,10},{10,1... | collective-permute-start | bytes 1216520 | tf_op jit(solution)/jit(body)/shard_map/ppermute | solution.py:104
  21.3 21.1 %collective-permute-start.1 = (f32[792,128]{1,0:T(8,128)}, f32[792,128]{1,0:T(8,128)}, u32[]{:S(2)}, u32[]{:S(2)}) collective-permute-start(f32[792,128]{1,0:T(8,128)} %pad_maximum_fusion.3), channel_id=1, source_target_pairs={{1,0},{2,1},{3,2},{4,3},{5,4},{6,5},{7,6},{0,7},{9,8},{10,9},{11,1... | collective-permute-start | bytes 1216520 | tf_op jit(solution)/jit(body)/shard_map/ppermute | solution.py:107
  22.5 12.2 %all-to-all-start = ((f32[3,2,4,8,2,2,128]{6,5,4,3,1,0,2:T(2,128)}), f32[3,2,4,8,2,2,128]{6,5,4,3,1,0,2:T(2,128)S(1)}, u32[]{:S(2)}, u32[]{:S(2)}) async-start(f32[3,2,4,8,2,2,128]{6,5,4,3,1,0,2:T(2,128)} %copy.104), calls=%async_computation | async-start | bytes 786432 | tf_op jit(solution)/jit(body)/shard_map/all_to_all | solution.py:81
  27.0 117.8 %reduce-scatter.2.cloned.1.call-start = ((), (), s32[]{:S(2)}) async-start(), calls=%async_computation.2 | async-start | bytes 1966080 | tf_op jit(solution)/jit(body)/shard_map/reduce_scatter | solution.py:131
  27.6 7.3 %copy-start.8 = (pred[8]{0:T(512)(128)(4,1)}, pred[8]{0:T(512)(128)(4,1)S(1)}, u32[]{:S(2)}) copy-start(pred[8]{0:T(512)(128)(4,1)S(1)} %get-tuple-element.40) | copy-start | bytes 28
  35.0 11.4 %collective-permute-start.8 = (f32[4,2,8,2,2,128]{5,0,4,3,2,1:T(4,128)S(1)}, f32[4,2,8,2,2,128]{5,0,4,3,2,1:T(4,128)S(1)}, u32[]{:S(2)}, u32[]{:S(2)}) collective-permute-start(f32[4,2,8,2,2,128]{5,0,4,3,2,1:T(4,128)S(1)} %get-tuple-element.46), channel_id=1, source_target_pairs={{0,32},{32,64},{64,96},{96,128},{128,160},{160,192},{192,224},{224... | collective-permute-start | bytes 393224 | tf_op jit(solution)/jit(body)/shard_map/ppermute | solution.py:84
  35.0 12.0 %collective-permute-start.10 = (f32[4,2,8,2,2,128]{5,0,4,3,2,1:T(4,128)S(1)}, f32[4,2,8,2,2,128]{5,0,4,3,2,1:T(4,128)S(1)}, u32[]{:S(2)}, u32[]{:S(2)}) collective-permute-start(f32[4,2,8,2,2,128]{5,0,4,3,2,1:T(4,128)S(1)} %get-tuple-element.45), channel_id=1, source_target_pairs={{32,0},{64,32},{96,64},{128,96},{160,128},{192,160},{224,192},{0,2... | collective-permute-start | bytes 393224 | tf_op jit(solution)/jit(body)/shard_map/ppermute | solution.py:86
  38.6 13.8 %collective-permute-start.2 = (f32[792,128]{1,0:T(8,128)}, f32[792,128]{1,0:T(8,128)S(1)}, u32[]{:S(2)}, u32[]{:S(2)}) collective-permute-start(f32[792,128]{1,0:T(8,128)} %collective-permute-done), channel_id=1, source_target_pairs={{0,1},{1,2},{2,3},{3,4},{4,5},{5,6},{6,7},{7,0},{8,9},{9,10},{10,1... | collective-permute-start | bytes 1216520 | tf_op jit(solution)/jit(body)/shard_map/ppermute | solution.py:104
  42.4 11.3 %collective-permute-start.3 = (f32[792,128]{1,0:T(8,128)}, f32[792,128]{1,0:T(8,128)S(1)}, u32[]{:S(2)}, u32[]{:S(2)}) collective-permute-start(f32[792,128]{1,0:T(8,128)} %collective-permute-done.1), channel_id=1, source_target_pairs={{1,0},{2,1},{3,2},{4,3},{5,4},{6,5},{7,6},{0,7},{9,8},{10,9},{11,1... | collective-permute-start | bytes 1216520 | tf_op jit(solution)/jit(body)/shard_map/ppermute | solution.py:107
  52.4 13.2 %collective-permute-start.4 = (f32[792,128]{1,0:T(8,128)S(1)}, f32[792,128]{1,0:T(8,128)S(1)}, u32[]{:S(2)}, u32[]{:S(2)}) collective-permute-start(f32[792,128]{1,0:T(8,128)S(1)} %collective-permute-done.2), channel_id=1, source_target_pairs={{0,1},{1,2},{2,3},{3,4},{4,5},{5,6},{6,7},{7,0},{8,9},{9,10},{10,1... | collective-permute-start | bytes 1216520 | tf_op jit(solution)/jit(body)/shard_map/ppermute | solution.py:104
  53.7 10.3 %collective-permute-start.5 = (f32[792,128]{1,0:T(8,128)S(1)}, f32[792,128]{1,0:T(8,128)S(1)}, u32[]{:S(2)}, u32[]{:S(2)}) collective-permute-start(f32[792,128]{1,0:T(8,128)S(1)} %collective-permute-done.3), channel_id=1, source_target_pairs={{1,0},{2,1},{3,2},{4,3},{5,4},{6,5},{7,6},{0,7},{9,8},{10,9},{11,1... | collective-permute-start | bytes 1216520 | tf_op jit(solution)/jit(body)/shard_map/ppermute | solution.py:107
  64.0 9.1 %collective-permute-start.7 = (f32[400,128]{1,0:T(8,128)S(1)}, f32[400,128]{1,0:T(8,128)S(1)}, u32[]{:S(2)}, u32[]{:S(2)}) collective-permute-start(f32[400,128]{1,0:T(8,128)S(1)} %slice.173), channel_id=1, source_target_pairs={{1,0},{2,1},{3,2},{4,3},{5,4},{6,5},{7,6},{0,7},{9,8},{10,9},{11,1... | collective-permute-start | bytes 614408 | tf_op jit(solution)/jit(body)/shard_map/ppermute | solution.py:100
  65.6 7.5 %collective-permute-start.6 = (f32[392,128]{1,0:T(8,128)S(1)}, f32[392,128]{1,0:T(8,128)S(1)}, u32[]{:S(2)}, u32[]{:S(2)}) collective-permute-start(f32[392,128]{1,0:T(8,128)S(1)} %slice.172), channel_id=1, source_target_pairs={{0,1},{1,2},{2,3},{3,4},{4,5},{5,6},{6,7},{7,0},{8,9},{9,10},{10,1... | collective-permute-start | bytes 602120 | tf_op jit(solution)/jit(body)/shard_map/ppermute | solution.py:99
  80.0 2.3 %copy-start.1 = (f32[4,2,8,2,128]{4,3,2,1,0:T(2,128)S(1)}, f32[4,2,8,2,128]{4,3,2,1,0:T(2,128)}, u32[]{:S(2)}) copy-start(f32[4,2,8,2,128]{4,3,2,1,0:T(2,128)} %copy.106) | copy-start | bytes 196612
  80.0 2.3 %copy-start.2 = (f32[4,2,8,2,128]{4,3,2,1,0:T(2,128)S(1)}, f32[4,2,8,2,128]{4,3,2,1,0:T(2,128)}, u32[]{:S(2)}) copy-start(f32[4,2,8,2,128]{4,3,2,1,0:T(2,128)} %copy.107) | copy-start | bytes 196612
  80.0 2.3 %copy-start.3 = (f32[4,2,8,2,128]{4,3,2,1,0:T(2,128)S(1)}, f32[4,2,8,2,128]{4,3,2,1,0:T(2,128)}, u32[]{:S(2)}) copy-start(f32[4,2,8,2,128]{4,3,2,1,0:T(2,128)} %copy.109) | copy-start | bytes 196612
  80.0 2.3 %copy-start.4 = (f32[4,2,8,2,128]{4,3,2,1,0:T(2,128)S(1)}, f32[4,2,8,2,128]{4,3,2,1,0:T(2,128)}, u32[]{:S(2)}) copy-start(f32[4,2,8,2,128]{4,3,2,1,0:T(2,128)} %copy.110) | copy-start | bytes 196612
  80.0 2.3 %copy-start.5 = (f32[4,2,8,2,128]{4,3,2,1,0:T(2,128)S(1)}, f32[4,2,8,2,128]{4,3,2,1,0:T(2,128)}, u32[]{:S(2)}) copy-start(f32[4,2,8,2,128]{4,3,2,1,0:T(2,128)} %copy.112) | copy-start | bytes 196612
  80.1 2.3 %copy-start.6 = (f32[4,2,8,2,128]{4,3,2,1,0:T(2,128)S(1)}, f32[4,2,8,2,128]{4,3,2,1,0:T(2,128)}, u32[]{:S(2)}) copy-start(f32[4,2,8,2,128]{4,3,2,1,0:T(2,128)} %copy.113) | copy-start | bytes 196612
  99.3 12.3 %collective-permute-start.9 = (f32[4,2,2,2,64,128]{5,4,2,1,0,3:T(8,128)S(1)}, f32[4,2,2,2,64,128]{5,4,2,1,0,3:T(8,128)S(1)}, u32[]{:S(2)}, u32[]{:S(2)}) collective-permute-start(f32[4,2,2,2,64,128]{5,4,2,1,0,3:T(8,128)S(1)} %pad_maximum_fusion.2), channel_id=1, source_target_pairs={{32,0},{64,32},{96,64},{128,96},{160,128},{192,160},{224,192},{0,2... | collective-permute-start | bytes 3145736 | tf_op jit(solution)/jit(body)/shard_map/ppermute | solution.py:126
  99.5 15.4 %collective-permute-start.11 = (f32[4,2,2,2,64,128]{5,4,2,1,0,3:T(8,128)S(1)}, f32[4,2,2,2,64,128]{5,4,2,1,0,3:T(8,128)S(1)}, u32[]{:S(2)}, u32[]{:S(2)}) collective-permute-start(f32[4,2,2,2,64,128]{5,4,2,1,0,3:T(8,128)S(1)} %pad_maximum_fusion.1), channel_id=1, source_target_pairs={{0,32},{32,64},{64,96},{96,128},{128,160},{160,192},{192,224},{224... | collective-permute-start | bytes 3145736 | tf_op jit(solution)/jit(body)/shard_map/ppermute | solution.py:127
Sparse Core Ops, SparseCore 0:
  116.6 28.0 reduce-scatter.1

commit v8 on v7

--- a/solution.py
+++ b/solution.py
@@ -118,16 +118,23 @@
     dense = jnp.sum(jnp.where(hit[..., None], weights[:, :, :, :, None, :], 0.0), axis=3)
     dense = jnp.transpose(dense, (1, 2, 0, 4, 3))
 
-    def side_part(s):
-        cols_s = jnp.take(side_cols[s], sources, axis=2)
+    def side_part(s, t0=0, t1=None):
         lo, hi = spans[s]
-        return combine(cols_s, dense[s], gathered)[:, :, :, :, lo:hi]
+        cols_s = jnp.take(side_cols[s][t0:t1], sources, axis=2)
+        return combine(cols_s, dense[s, t0:t1, :, :, lo:hi], gathered[:, :, :, :, lo:hi])
 
-    from_up = lax.ppermute(side_part(0), "line", down)
-    from_down = lax.ppermute(side_part(2), "line", up)
+    cut = rows // 2
+    shifted = []
+    for t0, t1 in ((0, cut), (cut, rows)):
+        shifted.append((
+            t0, t1,
+            lax.ppermute(side_part(0, t0, t1), "line", down),
+            lax.ppermute(side_part(2, t0, t1), "line", up),
+        ))
     total = side_part(1)
-    total = total.at[:, :, :, :, width:].add(from_up)
-    total = total.at[:, :, :, :, : 2 * width].add(from_down)
+    for t0, t1, from_up, from_down in shifted:
+        total = total.at[t0:t1, :, :, :, width:].add(from_up)
+        total = total.at[t0:t1, :, :, :, : 2 * width].add(from_down)
     result = lax.psum_scatter(total, "gy", scatter_dimension=0, tiled=False)
     result = jnp.transpose(result, (0, 3, 1, 2, 4))
     return result.reshape(shots, recv, 2, NF)

time: 155 us -> 163 us (1.052)
  waiting for transfers between devices: 59.3 us -> 47.7 us
  local copies, waits for them, and re-layouts: 28 us -> 37.7 us
  other arithmetic: 23.4 us -> 28.5 us
  starting transfers between devices: 20.3 us -> 25 us
    ppermute x2 -> x4, waiting for transfers between devices: 14.5 us -> 3.75 us  [the longest x2 3.74 us: body(): lax.ppermute(side_part(0, t0, t1), 'line', down)]
    ppermute x2 -> x4, starting transfers between devices: 0.52 us -> 5.91 us  [the longest x2 5.9 us: body(): lax.ppermute(side_part(0, t0, t1), 'line', down)]
    reduce_sum x1 -> x3, other arithmetic: 16.6 us -> 12.1 us  [combine(): prod_re = -jnp.sum(w * (col_re * row_re - col_im * row_im), axis=(2, 3))]
    scatter-add x1 -> x2, local copies, waits for them, and re-layouts: 1.29 us -> 5.17 us  [the longest x1 3.88 us: body(): total = total.at[t0:t1, :, :, :, width:].add(from_up)]
    another operation x0 -> x3, other arithmetic: none -> 3.61 us
    scatter-add x2 -> x3, other arithmetic: 0.42 us -> 3.52 us  [the longest x2 2.35 us: body(): total = total.at[t0:t1, :, :, :, :2 * width].add(from_down)]
    slice x0 -> x10, local copies, waits for them, and re-layouts: none -> 2.91 us  [the longest x4 2.67 us: combine(): col_re = cols[:, :, :, :, None, 0, None, :]]
    all_to_all x1, waiting for transfers between devices: 5.26 us -> 2.51 us  [body(): lax.all_to_all(stacked, 'gy', split_axis=2, concat_axis=2, tiled=True)]
  transfers between devices with their start and end apart: 14 -> 16, of which waited for: 7 -> 6; matrix products, arithmetic and copies ran while one was open for 12% -> 25% of each run, Pallas kernels for 0% -> 0%
where the time goes in v8:
time: 163 us; the launch traced here: 162 us
  waiting for transfers between devices  47.7 us (29%)
  local copies, waits for them, and re-layouts  37.7 us (23%)
  other arithmetic  28.5 us (17%)
  starting transfers between devices  25 us (15%)
  between operations  13.9 us (9%)
  matrix products  9.01 us (6%)
    reduce_scatter x1, waiting for transfers between devices, body(): result = lax.psum_scatter(total, 'gy', scatter_dimension=0, tiled=False)  29.4 us
    reduce_sum x3, other arithmetic, combine(): prod_re = -jnp.sum(w * (col_re * row_re - col_im * row_im), axis=(2, 3))  12.1 us
    dot_general x1, matrix products, spectrum(): out = jnp.dot(traces.reshape(shots * recv, samples), table, precision=HIGH)  9.01 us
    ppermute x3, waiting for transfers between devices, body(): backward = lax.ppermute(backward, 'gz', left)  7.64 us
    unnamed x36, local copies, waits for them, and re-layouts  7.21 us
    ppermute x2, starting transfers between devices, body(): lax.ppermute(side_part(0, t0, t1), 'line', down)  5.9 us
    mul x6, local copies, waits for them, and re-layouts, combine(): prod_re = -jnp.sum(w * (col_re * row_re - col_im * row_im), axis=(2, 3))  4.86 us
    ppermute x3, starting transfers between devices, body(): forward = lax.ppermute(forward, 'gz', right)  4.83 us
  transfers between devices with their start and end apart: 16, of which 6 were waited for; matrix products, arithmetic and copies ran while one was open for 25% of the time, Pallas kernels for 0%

profile of v8, /device:TPU:32, one launch (start us, length us, event | category | flops | bytes accessed | tf_op | source)
XLA Modules:
  0.0 161.8 jit_solution(15444181181487621235)
XLA Ops:
  7.6 9.0 %fusion.4 = f32[384,256]{0,1:T(8,128)S(1)} fusion(f32[384,4096]{1,0:T(8,128)} %bitcast.122, f32[4096,128]{1,0:T(8,128)S(1)} %bitcast.121, f32[4096,128]{1,0:T(8,128)S(1)} %bitcast.120), kind=kOutput, calls=%fused_computation.28 | convolution fusion | flops 2416967680 | bytes 10878976 | tf_op jit(solution)/jit(body)/shard_map/dot_general | solution.py:36
  19.4 1.9 %collective-permute-start = (f32[792,128]{1,0:T(8,128)}, f32[792,128]{1,0:T(8,128)}, u32[]{:S(2)}, u32[]{:S(2)}) collective-permute-start(f32[792,128]{1,0:T(8,128)} %pad_maximum_fusion.5), channel_id=1, source_target_pairs={{0,1},{1,2},{2,3},{3,4},{4,5},{5,6},{6,7},{7,0},{8,9},{9,10},{10,1... | collective-permute-start | bytes 1216520 | tf_op jit(solution)/jit(body)/shard_map/ppermute | solution.py:104
  22.5 4.5 %all-to-all-start = ((f32[3,2,4,8,2,2,128]{6,5,4,3,1,0,2:T(2,128)}), f32[3,2,4,8,2,2,128]{6,5,4,3,1,0,2:T(2,128)S(1)}, u32[]{:S(2)}, u32[]{:S(2)}) async-start(f32[3,2,4,8,2,2,128]{6,5,4,3,1,0,2:T(2,128)} %copy.150), calls=%async_computation | async-start | bytes 786432 | tf_op jit(solution)/jit(body)/shard_map/all_to_all | solution.py:81
  29.8 1.4 concatenate.23
  32.2 2.5 %all-to-all-done = f32[3,2,4,8,2,2,128]{6,5,4,3,1,0,2:T(2,128)S(1)} async-done(((f32[3,2,4,8,2,2,128]{6,5,4,3,1,0,2:T(2,128)}), f32[3,2,4,8,2,2,128]{6,5,4,3,1,0,2:T(2,128)S(1)}, u32[]{:S(2)}, u32[]{:S(2)}) %all-to-all-start) | async-done | bytes 393248 | tf_op jit(solution)/jit(body)/shard_map/all_to_all | solution.py:81
  35.0 2.9 %collective-permute-start.10 = (f32[4,2,8,2,2,128]{5,0,4,3,2,1:T(4,128)S(1)}, f32[4,2,8,2,2,128]{5,0,4,3,2,1:T(4,128)S(1)}, u32[]{:S(2)}, u32[]{:S(2)}) collective-permute-start(f32[4,2,8,2,2,128]{5,0,4,3,2,1:T(4,128)S(1)} %get-tuple-element.76), channel_id=1, source_target_pairs={{32,0},{64,32},{96,64},{128,96},{160,128},{192,160},{224,192},{0,2... | collective-permute-start | bytes 393224 | tf_op jit(solution)/jit(body)/shard_map/ppermute | solution.py:86
  40.0 1.9 %collective-permute-start.2 = (f32[792,128]{1,0:T(8,128)}, f32[792,128]{1,0:T(8,128)S(1)}, u32[]{:S(2)}, u32[]{:S(2)}) collective-permute-start(f32[792,128]{1,0:T(8,128)} %collective-permute-done), channel_id=1, source_target_pairs={{0,1},{1,2},{2,3},{3,4},{4,5},{5,6},{6,7},{7,0},{8,9},{9,10},{10,1... | collective-permute-start | bytes 1216520 | tf_op jit(solution)/jit(body)/shard_map/ppermute | solution.py:104
  41.9 1.8 %bitcast_dynamic-update-slice_fusion.5 = f32[8,792,128]{2,1,0:T(8,128)} fusion(f32[8,792,128]{2,1,0:T(8,128)} %bitcast_dynamic-update-slice_fusion.6, f32[792,128]{1,0:T(8,128)} %collective-permute-done), kind=kLoop, calls=%fused_computation.57 | loop fusion | bytes 811008
  43.7 2.1 %collective-permute-start.3 = (f32[792,128]{1,0:T(8,128)}, f32[792,128]{1,0:T(8,128)S(1)}, u32[]{:S(2)}, u32[]{:S(2)}) collective-permute-start(f32[792,128]{1,0:T(8,128)} %collective-permute-done.1), channel_id=1, source_target_pairs={{1,0},{2,1},{3,2},{4,3},{5,4},{6,5},{7,6},{0,7},{9,8},{10,9},{11,1... | collective-permute-start | bytes 1216520 | tf_op jit(solution)/jit(body)/shard_map/ppermute | solution.py:107
  45.9 1.8 %bitcast_dynamic-update-slice_fusion.4 = f32[8,792,128]{2,1,0:T(8,128)} fusion(f32[8,792,128]{2,1,0:T(8,128)} %bitcast_dynamic-update-slice_fusion.5, f32[792,128]{1,0:T(8,128)} %collective-permute-done.1), kind=kLoop, calls=%fused_computation.56 | loop fusion | bytes 811008
  55.0 1.7 %collective-permute-start.5 = (f32[792,128]{1,0:T(8,128)S(1)}, f32[792,128]{1,0:T(8,128)S(1)}, u32[]{:S(2)}, u32[]{:S(2)}) collective-permute-start(f32[792,128]{1,0:T(8,128)S(1)} %collective-permute-done.3), channel_id=1, source_target_pairs={{1,0},{2,1},{3,2},{4,3},{5,4},{6,5},{7,6},{0,7},{9,8},{10,9},{11,1... | collective-permute-start | bytes 1216520 | tf_op jit(solution)/jit(body)/shard_map/ppermute | solution.py:107
  58.3 7.0 %collective-permute-done.5 = f32[792,128]{1,0:T(8,128)S(1)} collective-permute-done((f32[792,128]{1,0:T(8,128)S(1)}, f32[792,128]{1,0:T(8,128)S(1)}, u32[]{:S(2)}, u32[]{:S(2)}) %collective-permute-start.5) | collective-permute-done | bytes 405536 | tf_op jit(solution)/jit(body)/shard_map/ppermute | solution.py:107
  65.3 1.3 collective-permute-start.7
  66.6 1.6 collective-permute-start.6
  69.7 4.3 %collective-permute-done.6 = f32[392,128]{1,0:T(8,128)S(1)} collective-permute-done((f32[392,128]{1,0:T(8,128)S(1)}, f32[392,128]{1,0:T(8,128)S(1)}, u32[]{:S(2)}, u32[]{:S(2)}) %collective-permute-start.6) | collective-permute-done | bytes 200736 | tf_op jit(solution)/jit(body)/shard_map/ppermute | solution.py:99
  75.8 2.1 %slice.343 = f32[8,768,128]{2,1,0:T(8,128)S(1)} slice(f32[8,792,128]{2,1,0:T(8,128)} %fusion.11), slice={[0:8], [0:768], [0:128]} | slice | bytes 6291456 | tf_op jit(solution)/jit(body)/shard_map/slice | solution.py:112
  77.9 2.1 %slice_bitcast_fusion.3 = (f32[8,2,2,64,128]{4,3,2,1,0:T(8,128)}, f32[8,2,2,64,128]{4,3,2,1,0:T(8,128)}, f32[8,2,2,64,128]{4,3,2,1,0:T(8,128)}, f32[8,2,2,64,128]{4,3,2,1,0:T(8,128)}) fusion(f32[8,2,2,2,96,128]{5,4,3,2,1,0:T(8,128)S(1)} %bitcast.118), kind=kLoop, calls=%fused_computation.30 | loop fusion | bytes 8388608 | tf_op jit(solution)/jit(body)/shard_map/mul | solution.py:46
  80.0 1.4 slice_bitcast_fusion.1
  81.3 1.6 %copy.145 = f32[8,24,128]{0,2,1:T(8,128)} copy(f32[8,24,128]{2,1,0:T(8,128)S(1)} %slice.339) | data formatting | bytes 196608 | tf_op jit(solution)/jit(body)/shard_map/slice | solution.py:114
  84.7 1.8 %select_reduce_fusion = f32[8,3,4,96,2]{3,4,2,1,0:T(2,128)S(1)} fusion(f32[8,3,4,16,2]{3,4,2,1,0:T(2,128)} %copy.147, pred[8,3,4,16,96]{4,3,2,1,0:T(8,128)(4,1)S(1)} %iota_compare_fusion), kind=kLoop, calls=%fused_computation.27 | loop fusion | flops 571392 | bytes 233472 | tf_op jit(solution)/jit(body)/shard_map/reduce_sum | solution.py:118
  86.6 4.4 %multiply_reduce_fusion.3 = (f32[2,2,2,64,128]{4,3,2,1,0:T(8,128)S(1)}, f32[2,2,2,64,128]{4,3,2,1,0:T(8,128)S(1)}, f32[2,2,2,64,128]{4,3,2,1,0:T(8,128)S(1)}, f32[2,2,2,64,128]{4,3,2,1,0:T(8,128)S(1)}) fusion(f32[8,2,2,64,128]{4,3,2,1,0:T(8,128)} %get-tuple-element.71, f32[8,2,2,64,128]{4,3,2,1,0:T(8,128)} %get-tuple-element.70, ...), kind=kLoop, calls=%fused_computation.13 | loop fusion | flops 20709376 | bytes 3293184 | tf_op jit(solution)/jit(body)/shard_map/reduce_sum | solution.py:46
  92.0 3.2 %multiply_reduce_fusion.5 = (f32[2,2,2,64,128]{4,3,2,1,0:T(8,128)S(1)}, f32[2,2,2,64,128]{4,3,2,1,0:T(8,128)S(1)}, f32[2,2,2,64,128]{4,3,2,1,0:T(8,128)S(1)}, f32[2,2,2,64,128]{4,3,2,1,0:T(8,128)S(1)}) fusion(f32[8,2,2,64,128]{4,3,2,1,0:T(8,128)S(1)} %copy-done.2, f32[8,2,2,64,128]{4,3,2,1,0:T(8,128)S(1)} %copy-done.3, ...), kind=kLoop, calls=%fused_computation.15 | loop fusion | flops 20709376 | bytes 3293184 | tf_op jit(solution)/jit(body)/shard_map/reduce_sum | solution.py:46
  96.1 2.9 %collective-permute-start.12 = (f32[2,2,2,2,64,128]{5,4,2,1,0,3:T(8,128)}, f32[2,2,2,2,64,128]{5,4,2,1,0,3:T(8,128)}, u32[]{:S(2)}, u32[]{:S(2)}) collective-permute-start(f32[2,2,2,2,64,128]{5,4,2,1,0,3:T(8,128)} %pad_maximum_fusion.3), channel_id=1, source_target_pairs={{32,0},{64,32},{96,64},{128,96},{160,128},{192,160},{224,192},{0,2... | collective-permute-start | bytes 1572872 | tf_op jit(solution)/jit(body)/shard_map/ppermute | solution.py:131
  100.0 3.0 %collective-permute-start.9 = (f32[2,2,2,2,64,128]{5,4,2,1,0,3:T(8,128)S(1)}, f32[2,2,2,2,64,128]{5,4,2,1,0,3:T(8,128)S(1)}, u32[]{:S(2)}, u32[]{:S(2)}) collective-permute-start(f32[2,2,2,2,64,128]{5,4,2,1,0,3:T(8,128)S(1)} %pad_maximum_fusion.1), channel_id=1, source_target_pairs={{32,0},{64,32},{96,64},{128,96},{160,128},{192,160},{224,192},{0,2... | collective-permute-start | bytes 1572872 | tf_op jit(solution)/jit(body)/shard_map/ppermute | solution.py:131
  103.0 4.5 %multiply_reduce_fusion.1 = (f32[4,2,2,96,128]{4,3,2,1,0:T(8,128)S(1)}, f32[4,2,2,96,128]{4,3,2,1,0:T(8,128)S(1)}) fusion(f32[8,2,2,96,128]{4,3,2,1,0:T(8,128)S(1)} %copy-done.1, f32[4,2,8,2,128]{4,3,2,1,0:T(2,128)S(1)} %copy-done.5, f32[8,2,2,96,128]{4,3,2,1,0:T(8,128)S(1)} %get-tuple-element.74, f32[4,2,8,2,128]{4,3,2,1,0:T(2,128)S(1)} %copy-done.4, ...), kind=kLoop, calls=%fused_computation.7 | loop fusion | flops 31064064 | bytes 4882432 | tf_op jit(solution)/jit(body)/shard_map/reduce_sum | solution.py:46
  107.8 3.7 %collective-permute-done.9 = f32[2,2,2,2,64,128]{5,4,2,1,0,3:T(8,128)S(1)} collective-permute-done((f32[2,2,2,2,64,128]{5,4,2,1,0,3:T(8,128)S(1)}, f32[2,2,2,2,64,128]{5,4,2,1,0,3:T(8,128)S(1)}, u32[]{:S(2)}, u32[]{:S(2)}) %collective-permute-start.9) | collective-permute-done | bytes 524320 | tf_op jit(solution)/jit(body)/shard_map/ppermute | solution.py:131
  111.6 2.9 %add_select_fusion = f32[2,2,2,2,64,128]{5,4,2,1,0,3:T(8,128)} fusion(f32[2,2,2,2,64,128]{5,4,2,1,0,3:T(8,128)S(1)} %collective-permute-done.9, s32[]{:T(128)} %bitcast.32, s32[]{:T(128)} %bitcast.33, f32[4,2,2,1,96,128]{5,4,2,1,0,3:T(8,128)S(1)} %negate_bitcast_fusion.1, f32[4,2,2,1,96,128]{5,4,2,1,0,3:T(8,128)S(1)} %negate_bitcast_fusion, pred[]{:T(512)} %and_reduce_fusion), kind=kLoop, calls=%fused_computation.33 | loop fusion | flops 393216 | bytes 2621449 | tf_op jit(solution)/jit(body)/shard_map/select.4
  114.5 3.9 %scatter-add.14 = f32[4,2,2,2,96,128]{5,4,2,1,0,3:T(8,128)S(1)} dynamic-update-slice(f32[4,2,2,2,96,128]{5,4,2,1,0,3:T(8,128)S(1)} %pad_maximum_fusion, f32[2,2,2,2,64,128]{5,4,2,1,0,3:T(8,128)} %add_select_fusion, s32[]{:T(128)} %bitcast.32, s32[]{:T(128)} %constant.205.clone.1, s32[]{:T(128)} %constant.205.clone.1, s32[]{:T(128)} %constant.205.clone.1, s32[]{:T(128)} %bitcast.33, ...) | dynamic-update-slice | bytes 1048580 | tf_op jit(solution)/jit(body)/shard_map/scatter-add | solution.py:136
  120.7 1.2 fusion.8
  121.9 1.3 copy.170
  123.2 29.4 %reduce-scatter.2.cloned.1.call-done = f32[1,2,2,2,96,128]{5,4,3,2,1,0:T(8,128)} async-done(((f32[4,2,2,2,96,128]{5,4,3,2,1,0:T(8,128)}), f32[1,2,2,2,96,128]{5,4,3,2,1,0:T(8,128)}) %reduce-scatter.2.cloned.1.call-update) | async-done | bytes 393232 | tf_op jit(solution)/jit(body)/shard_map/reduce_scatter | solution.py:138
  152.6 1.3 copy.171
  (124 shorter events, 31.4 us)
Async XLA Ops:
  6.5 21.2 %copy-start = (s32[256,3,32,16]{0,3,2,1:T(8,128)S(1)}, s32[256,3,32,16]{0,3,2,1:T(8,128)}, u32[]{:S(2)}) copy-start(s32[256,3,32,16]{0,3,2,1:T(8,128)} %param.16) | copy-start | bytes 4718596
  7.6 9.5 %copy-start.10 = (s32[1,3,32,16]{2,3,1,0:T(8,128)S(1)}, s32[1,3,32,16]{2,3,1,0:T(8,128)}, u32[]{:S(2)}) copy-start(s32[1,3,32,16]{2,3,1,0:T(8,128)} %param.17) | copy-start | bytes 18436
  7.6 9.6 %copy-start.11 = (f32[8,2]{0,1:T(2,128)S(1)}, f32[8,2]{0,1:T(2,128)}, u32[]{:S(2)}) copy-start(f32[8,2]{0,1:T(2,128)} %param.18) | copy-start | bytes 196
  18.6 9.8 %copy-start.12 = (s32[8]{0:T(128)S(1)}, s32[8]{0:T(128)}, u32[]{:S(2)}) copy-start(s32[8]{0:T(128)} %constant.225.clone) | copy-start | bytes 100
  19.4 11.8 %copy-start.13 = (s32[6]{0:T(128)S(1)}, s32[6]{0:T(128)}, u32[]{:S(2)}) copy-start(s32[6]{0:T(128)} %constant.222.clone.1) | copy-start | bytes 76
  19.4 20.6 %collective-permute-start = (f32[792,128]{1,0:T(8,128)}, f32[792,128]{1,0:T(8,128)}, u32[]{:S(2)}, u32[]{:S(2)}) collective-permute-start(f32[792,128]{1,0:T(8,128)} %pad_maximum_fusion.5), channel_id=1, source_target_pairs={{0,1},{1,2},{2,3},{3,4},{4,5},{5,6},{6,7},{7,0},{8,9},{9,10},{10,1... | collective-permute-start | bytes 1216520 | tf_op jit(solution)/jit(body)/shard_map/ppermute | solution.py:104
  21.3 22.4 %collective-permute-start.1 = (f32[792,128]{1,0:T(8,128)}, f32[792,128]{1,0:T(8,128)}, u32[]{:S(2)}, u32[]{:S(2)}) collective-permute-start(f32[792,128]{1,0:T(8,128)} %pad_maximum_fusion.5), channel_id=1, source_target_pairs={{1,0},{2,1},{3,2},{4,3},{5,4},{6,5},{7,6},{0,7},{9,8},{10,9},{11,1... | collective-permute-start | bytes 1216520 | tf_op jit(solution)/jit(body)/shard_map/ppermute | solution.py:107
  22.5 12.2 %all-to-all-start = ((f32[3,2,4,8,2,2,128]{6,5,4,3,1,0,2:T(2,128)}), f32[3,2,4,8,2,2,128]{6,5,4,3,1,0,2:T(2,128)S(1)}, u32[]{:S(2)}, u32[]{:S(2)}) async-start(f32[3,2,4,8,2,2,128]{6,5,4,3,1,0,2:T(2,128)} %copy.150), calls=%async_computation | async-start | bytes 786432 | tf_op jit(solution)/jit(body)/shard_map/all_to_all | solution.py:81
  27.0 125.6 %reduce-scatter.2.cloned.1.call-start = ((), (), s32[]{:S(2)}) async-start(), calls=%async_computation.2 | async-start | bytes 1966080 | tf_op jit(solution)/jit(body)/shard_map/reduce_scatter | solution.py:138
  35.0 12.7 %collective-permute-start.8 = (f32[4,2,8,2,2,128]{5,0,4,3,2,1:T(4,128)S(1)}, f32[4,2,8,2,2,128]{5,0,4,3,2,1:T(4,128)S(1)}, u32[]{:S(2)}, u32[]{:S(2)}) collective-permute-start(f32[4,2,8,2,2,128]{5,0,4,3,2,1:T(4,128)S(1)} %get-tuple-element.77), channel_id=1, source_target_pairs={{0,32},{32,64},{64,96},{96,128},{128,160},{160,192},{192,224},{224... | collective-permute-start | bytes 393224 | tf_op jit(solution)/jit(body)/shard_map/ppermute | solution.py:84
  35.0 13.4 %collective-permute-start.10 = (f32[4,2,8,2,2,128]{5,0,4,3,2,1:T(4,128)S(1)}, f32[4,2,8,2,2,128]{5,0,4,3,2,1:T(4,128)S(1)}, u32[]{:S(2)}, u32[]{:S(2)}) collective-permute-start(f32[4,2,8,2,2,128]{5,0,4,3,2,1:T(4,128)S(1)} %get-tuple-element.76), channel_id=1, source_target_pairs={{32,0},{64,32},{96,64},{128,96},{160,128},{192,160},{224,192},{0,2... | collective-permute-start | bytes 393224 | tf_op jit(solution)/jit(body)/shard_map/ppermute | solution.py:86
  40.0 13.4 %collective-permute-start.2 = (f32[792,128]{1,0:T(8,128)}, f32[792,128]{1,0:T(8,128)S(1)}, u32[]{:S(2)}, u32[]{:S(2)}) collective-permute-start(f32[792,128]{1,0:T(8,128)} %collective-permute-done), channel_id=1, source_target_pairs={{0,1},{1,2},{2,3},{3,4},{4,5},{5,6},{6,7},{7,0},{8,9},{9,10},{10,1... | collective-permute-start | bytes 1216520 | tf_op jit(solution)/jit(body)/shard_map/ppermute | solution.py:104
  43.7 11.3 %collective-permute-start.3 = (f32[792,128]{1,0:T(8,128)}, f32[792,128]{1,0:T(8,128)S(1)}, u32[]{:S(2)}, u32[]{:S(2)}) collective-permute-start(f32[792,128]{1,0:T(8,128)} %collective-permute-done.1), channel_id=1, source_target_pairs={{1,0},{2,1},{3,2},{4,3},{5,4},{6,5},{7,6},{0,7},{9,8},{10,9},{11,1... | collective-permute-start | bytes 1216520 | tf_op jit(solution)/jit(body)/shard_map/ppermute | solution.py:107
  53.4 13.2 %collective-permute-start.4 = (f32[792,128]{1,0:T(8,128)S(1)}, f32[792,128]{1,0:T(8,128)S(1)}, u32[]{:S(2)}, u32[]{:S(2)}) collective-permute-start(f32[792,128]{1,0:T(8,128)S(1)} %collective-permute-done.2), channel_id=1, source_target_pairs={{0,1},{1,2},{2,3},{3,4},{4,5},{5,6},{6,7},{7,0},{8,9},{9,10},{10,1... | collective-permute-start | bytes 1216520 | tf_op jit(solution)/jit(body)/shard_map/ppermute | solution.py:104
  55.0 10.3 %collective-permute-start.5 = (f32[792,128]{1,0:T(8,128)S(1)}, f32[792,128]{1,0:T(8,128)S(1)}, u32[]{:S(2)}, u32[]{:S(2)}) collective-permute-start(f32[792,128]{1,0:T(8,128)S(1)} %collective-permute-done.3), channel_id=1, source_target_pairs={{1,0},{2,1},{3,2},{4,3},{5,4},{6,5},{7,6},{0,7},{9,8},{10,9},{11,1... | collective-permute-start | bytes 1216520 | tf_op jit(solution)/jit(body)/shard_map/ppermute | solution.py:107
  65.3 8.8 %collective-permute-start.7 = (f32[400,128]{1,0:T(8,128)S(1)}, f32[400,128]{1,0:T(8,128)S(1)}, u32[]{:S(2)}, u32[]{:S(2)}) collective-permute-start(f32[400,128]{1,0:T(8,128)S(1)} %slice.338), channel_id=1, source_target_pairs={{1,0},{2,1},{3,2},{4,3},{5,4},{6,5},{7,6},{0,7},{9,8},{10,9},{11,1... | collective-permute-start | bytes 614408 | tf_op jit(solution)/jit(body)/shard_map/ppermute | solution.py:100
  66.6 7.5 %collective-permute-start.6 = (f32[392,128]{1,0:T(8,128)S(1)}, f32[392,128]{1,0:T(8,128)S(1)}, u32[]{:S(2)}, u32[]{:S(2)}) collective-permute-start(f32[392,128]{1,0:T(8,128)S(1)} %slice.337), channel_id=1, source_target_pairs={{0,1},{1,2},{2,3},{3,4},{4,5},{5,6},{6,7},{7,0},{8,9},{9,10},{10,1... | collective-permute-start | bytes 602120 | tf_op jit(solution)/jit(body)/shard_map/ppermute | solution.py:99
  84.7 7.3 %copy-start.2 = (f32[8,2,2,64,128]{4,3,2,1,0:T(8,128)S(1)}, f32[8,2,2,64,128]{4,3,2,1,0:T(8,128)}, u32[]{:S(2)}) copy-start(f32[8,2,2,64,128]{4,3,2,1,0:T(8,128)} %get-tuple-element.72) | copy-start | bytes 3145732
  84.7 7.3 %copy-start.3 = (f32[8,2,2,64,128]{4,3,2,1,0:T(8,128)S(1)}, f32[8,2,2,64,128]{4,3,2,1,0:T(8,128)}, u32[]{:S(2)}) copy-start(f32[8,2,2,64,128]{4,3,2,1,0:T(8,128)} %get-tuple-element.73) | copy-start | bytes 3145732
  84.7 7.3 %copy-start.6 = (f32[2,2,8,2,1,128]{5,4,3,1,0,2:T(1,128)S(1)}, f32[2,2,8,2,1,128]{5,4,3,1,0,2:T(1,128)}, u32[]{:S(2)}) copy-start(f32[2,2,8,2,1,128]{5,4,3,1,0,2:T(1,128)} %get-tuple-element.95) | copy-start | bytes 98308
  84.7 7.3 %copy-start.7 = (f32[2,2,8,2,1,128]{5,4,3,1,0,2:T(1,128)S(1)}, f32[2,2,8,2,1,128]{5,4,3,1,0,2:T(1,128)}, u32[]{:S(2)}) copy-start(f32[2,2,8,2,1,128]{5,4,3,1,0,2:T(1,128)} %get-tuple-element.96) | copy-start | bytes 98308
  84.7 7.3 %copy-start.8 = (f32[2,2,8,2,1,128]{5,4,3,1,0,2:T(1,128)S(1)}, f32[2,2,8,2,1,128]{5,4,3,1,0,2:T(1,128)}, u32[]{:S(2)}) copy-start(f32[2,2,8,2,1,128]{5,4,3,1,0,2:T(1,128)} %get-tuple-element.97) | copy-start | bytes 98308
  84.7 7.3 %copy-start.9 = (f32[2,2,8,2,1,128]{5,4,3,1,0,2:T(1,128)S(1)}, f32[2,2,8,2,1,128]{5,4,3,1,0,2:T(1,128)}, u32[]{:S(2)}) copy-start(f32[2,2,8,2,1,128]{5,4,3,1,0,2:T(1,128)} %get-tuple-element.98) | copy-start | bytes 98308
  91.9 28.8 %collective-permute-start.13 = (f32[2,2,2,2,64,128]{5,4,2,1,0,3:T(8,128)}, f32[2,2,2,2,64,128]{5,4,2,1,0,3:T(8,128)}, u32[]{:S(2)}, u32[]{:S(2)}) collective-permute-start(f32[2,2,2,2,64,128]{5,4,2,1,0,3:T(8,128)} %pad_maximum_fusion.4), channel_id=1, source_target_pairs={{0,32},{32,64},{64,96},{96,128},{128,160},{160,192},{192,224},{224... | collective-permute-start | bytes 1572872 | tf_op jit(solution)/jit(body)/shard_map/ppermute | solution.py:132
  95.2 7.8 %copy-start.1 = (f32[8,2,2,96,128]{4,3,2,1,0:T(8,128)S(1)}, f32[8,2,2,96,128]{4,3,2,1,0:T(8,128)}, u32[]{:S(2)}) copy-start(f32[8,2,2,96,128]{4,3,2,1,0:T(8,128)} %get-tuple-element.75) | copy-start | bytes 4718596
  95.2 7.8 %copy-start.4 = (f32[4,2,8,2,128]{4,3,2,1,0:T(2,128)S(1)}, f32[4,2,8,2,128]{4,3,2,1,0:T(2,128)}, u32[]{:S(2)}) copy-start(f32[4,2,8,2,128]{4,3,2,1,0:T(2,128)} %copy.152) | copy-start | bytes 196612
  95.2 7.8 %copy-start.5 = (f32[4,2,8,2,128]{4,3,2,1,0:T(2,128)S(1)}, f32[4,2,8,2,128]{4,3,2,1,0:T(2,128)}, u32[]{:S(2)}) copy-start(f32[4,2,8,2,128]{4,3,2,1,0:T(2,128)} %copy.153) | copy-start | bytes 196612
  96.1 23.4 %collective-permute-start.12 = (f32[2,2,2,2,64,128]{5,4,2,1,0,3:T(8,128)}, f32[2,2,2,2,64,128]{5,4,2,1,0,3:T(8,128)}, u32[]{:S(2)}, u32[]{:S(2)}) collective-permute-start(f32[2,2,2,2,64,128]{5,4,2,1,0,3:T(8,128)} %pad_maximum_fusion.3), channel_id=1, source_target_pairs={{32,0},{64,32},{96,64},{128,96},{160,128},{192,160},{224,192},{0,2... | collective-permute-start | bytes 1572872 | tf_op jit(solution)/jit(body)/shard_map/ppermute | solution.py:131
  99.9 18.4 %collective-permute-start.11 = (f32[2,2,2,2,64,128]{5,4,2,1,0,3:T(8,128)}, f32[2,2,2,2,64,128]{5,4,2,1,0,3:T(8,128)}, u32[]{:S(2)}, u32[]{:S(2)}) collective-permute-start(f32[2,2,2,2,64,128]{5,4,2,1,0,3:T(8,128)} %pad_maximum_fusion.2), channel_id=1, source_target_pairs={{0,32},{32,64},{64,96},{96,128},{128,160},{160,192},{192,224},{224... | collective-permute-start | bytes 1572872 | tf_op jit(solution)/jit(body)/shard_map/ppermute | solution.py:132
  100.0 11.5 %collective-permute-start.9 = (f32[2,2,2,2,64,128]{5,4,2,1,0,3:T(8,128)S(1)}, f32[2,2,2,2,64,128]{5,4,2,1,0,3:T(8,128)S(1)}, u32[]{:S(2)}, u32[]{:S(2)}) collective-permute-start(f32[2,2,2,2,64,128]{5,4,2,1,0,3:T(8,128)S(1)} %pad_maximum_fusion.1), channel_id=1, source_target_pairs={{32,0},{64,32},{96,64},{128,96},{160,128},{192,160},{224,192},{0,2... | collective-permute-start | bytes 1572872 | tf_op jit(solution)/jit(body)/shard_map/ppermute | solution.py:131
Sparse Core Ops, SparseCore 0:
  123.3 29.2 reduce-scatter.1
